TPU v7x, 32 devices: a whole 2x2x4 slice. The times are simulated.
32 devices in a mesh: vis: 8 (over y, x, core), tile: 4 (over z).
Axes of the slice: x: 2, y: 2, z: 4, core: 2. Of those that a mesh axis runs over, the one named last changes fastest.
Arguments:
- image: float32 [8192, 8192], P('vis', 'tile'), may hold values from 0 to 2
- extrapolated: float32 [8192, 8192], P('vis', 'tile'), may hold values from -6 to 6
- vis_dual: float32 [8192, 2, 128], P(('vis', 'tile')), may hold values from -6 to 6
- tree_dual: float32 [2, 8192, 4096], P(None, 'vis', 'tile'), may hold values from -6 to 6
- observed: float32 [8192, 2, 128], P(('vis', 'tile')), may hold values from -6 to 6
- kernel: float32 [128, 128], replicated, may hold values from -0.5 to 0.5
- block_index: int32 [8192], P(('vis', 'tile')), may hold values from 0 to 16383
- live_blocks: int32 [32], P(('vis', 'tile')), may hold values from 1 to 256, as said below
Outputs:
- image_next: float32 [8192, 8192], P('vis', 'tile')
- vis_next: float32 [8192, 2, 128], P(('vis', 'tile'))
- tree_next: float32 [2, 8192, 4096], P(None, 'vis', 'tile')
Inputs may be any that keep to these rules, and one draw needn't show every extreme that they name: Each device's live slots are its first live_blocks entries of 256; some device has all 256 live in every draw.
All inputs are finite; a program needn't handle non-finite values.
Results may differ from a plain program's by a relative error of at most 0.00005.
Values sent between devices are 32-bit elements; how exact they have to be, the bound alone decides.
No kernel may reach another device: no remote copies, remote signals or barrier semaphores. Data moves between devices by JAX's collectives and lax.ppermute only.
A program may use at most 192 MiB of HBM per device.

v0:
```python
import math

import jax
import jax.numpy as jnp
from jax import lax
from jax.sharding import PartitionSpec as P

LOW_TAPS = (
    -0.010597401784997278,
    0.032883011666982945,
    0.030841381835986965,
    -0.18703481171888114,
    -0.02798376941698385,
    0.6308807679295904,
    0.7148465705525415,
    0.23037781330885523,
)
HIGH_TAPS = tuple(
    ((1.0 if position % 2 == 0 else -1.0) * LOW_TAPS[7 - position] for position in range(8))
)
TWO_PI = 2.0 * math.pi


def shifted(block, axis, distance):
    devices = range(lax.axis_size(axis))
    route = [((i - distance) % len(devices), i) for i in devices]
    return lax.ppermute(block, axis, route)


def phase_table(left_ids, right_ids, period):
    turns = left_ids[:, None] * right_ids[None, :] % period
    angles = turns.astype(jnp.float32) * (TWO_PI / period)
    return (jnp.cos(angles), jnp.sin(angles))


def factor_pair(length):
    chosen_factor = 1
    for candidate in range(1, math.isqrt(length) + 1):
        if length % candidate == 0:
            chosen_factor = candidate
    return (chosen_factor, length // chosen_factor)


def complex_einsum(form, left_real, left_imag, table_cos, table_sin, real_only):
    precise = lax.Precision.HIGHEST
    real_part = jnp.einsum(form, left_real, table_cos, precision=precise)
    if left_imag is not None:
        real_part = real_part - jnp.einsum(form, left_imag, table_sin, precision=precise)
    if real_only:
        return (real_part, None)
    imag_part = jnp.einsum(form, left_real, table_sin, precision=precise)
    if left_imag is not None:
        imag_part = imag_part + jnp.einsum(form, left_imag, table_cos, precision=precise)
    return (imag_part * 0.0 + real_part, imag_part)


def transform_axis(real_in, imag_in, sign_value, along, real_only):
    length = real_in.shape[along]
    first_factor, second_factor = factor_pair(length)
    first_ids = jnp.arange(first_factor, dtype=jnp.int32)
    second_ids = jnp.arange(second_factor, dtype=jnp.int32)
    cos_first, sin_first = phase_table(first_ids, first_ids, first_factor)
    cos_twist, sin_twist = phase_table(first_ids, second_ids, length)
    cos_second, sin_second = phase_table(second_ids, second_ids, second_factor)
    sin_twist = sign_value * sin_twist
    if along == 0:
        other_len = real_in.shape[1]
        shape_in = (first_factor, second_factor, other_len)
        form_first = "abm,ca->cbm"
        form_second = "cbm,db->dcm"
        cos_twist = cos_twist[:, :, None]
        sin_twist = sin_twist[:, :, None]
        shape_out = (length, other_len)
    else:
        other_len = real_in.shape[0]
        shape_in = (other_len, first_factor, second_factor)
        form_first = "mab,ca->mcb"
        form_second = "mcb,db->mdc"
        cos_twist = cos_twist[None, :, :]
        sin_twist = sin_twist[None, :, :]
        shape_out = (other_len, length)
    shaped_real = real_in.reshape(shape_in)
    shaped_imag = None if imag_in is None else imag_in.reshape(shape_in)
    section_real, section_imag = complex_einsum(
        form_first, shaped_real, shaped_imag, cos_first, sign_value * sin_first, False
    )
    twisted_real = section_real * cos_twist - section_imag * sin_twist
    twisted_imag = section_real * sin_twist + section_imag * cos_twist
    out_real, out_imag = complex_einsum(
        form_second, twisted_real, twisted_imag, cos_second, sign_value * sin_second, real_only
    )
    if real_only:
        return (out_real.reshape(shape_out), None)
    return (out_real.reshape(shape_out), out_imag.reshape(shape_out))


def analyse_local(coarse):
    half_rows = coarse.shape[1] // 2
    next_rows = shifted(coarse[:, :6], "tile", -1)
    extended = jnp.concatenate([coarse, next_rows], axis=1)
    approx = jnp.zeros((coarse.shape[0], half_rows), jnp.float32)
    detail = jnp.zeros_like(approx)
    for position in range(8):
        strided = lax.slice_in_dim(extended, position, position + 2 * half_rows - 1, 2, 1)
        approx = approx + LOW_TAPS[position] * strided
        detail = detail + HIGH_TAPS[position] * strided
    return (approx, detail)


def upsample(ext_approx, ext_detail):
    out_rows = ext_detail.shape[1] - 3
    even_part = jnp.zeros((ext_detail.shape[0], out_rows), jnp.float32)
    odd_part = jnp.zeros_like(even_part)
    for lag_index in range(4):
        window_detail = ext_detail[:, 3 - lag_index : 3 - lag_index + out_rows]
        even_part = even_part + HIGH_TAPS[2 * lag_index] * window_detail
        odd_part = odd_part + HIGH_TAPS[2 * lag_index + 1] * window_detail
        if ext_approx is not None:
            window_approx = ext_approx[:, 3 - lag_index : 3 - lag_index + out_rows]
            even_part = even_part + LOW_TAPS[2 * lag_index] * window_approx
            odd_part = odd_part + LOW_TAPS[2 * lag_index + 1] * window_approx
    return jnp.stack([even_part, odd_part], axis=2).reshape(ext_detail.shape[0], 2 * out_rows)


def on_device(image, extrapolated, vis_dual, tree_dual, observed, kernel, block_index, live_blocks):
    slab_cols = image.shape[0]
    rows_here = image.shape[1]
    block_width = kernel.shape[0]
    total_rows = rows_here * lax.axis_size("tile")
    spectral_len = slab_cols * lax.axis_size("vis")
    norm_scale = 1.0 / math.sqrt(spectral_len * total_rows)
    row_real = lax.all_to_all(extrapolated, "tile", split_axis=0, concat_axis=1, tiled=True)
    part_real, part_imag = transform_axis(row_real, None, -1.0, 1, False)
    back_real, back_imag = (
        lax.all_to_all(part_real, "tile", split_axis=1, concat_axis=0, tiled=True),
        lax.all_to_all(part_imag, "tile", split_axis=1, concat_axis=0, tiled=True),
    )
    pencil_real, pencil_imag = (
        lax.all_to_all(back_real, "vis", split_axis=1, concat_axis=0, tiled=True),
        lax.all_to_all(back_imag, "vis", split_axis=1, concat_axis=0, tiled=True),
    )
    done_real, done_imag = transform_axis(pencil_real, pencil_imag, -1.0, 0, False)
    grid_real, grid_imag = (
        lax.all_to_all(done_real, "vis", split_axis=0, concat_axis=1, tiled=True),
        lax.all_to_all(done_imag, "vis", split_axis=0, concat_axis=1, tiled=True),
    )
    grid = jnp.stack([grid_real, grid_imag]) * norm_scale
    block_count = slab_cols * (rows_here // block_width)
    blocks = grid.reshape(2, block_count, block_width)
    chosen = jnp.take(blocks, block_index, axis=1)
    model = jnp.einsum("ij,scj->csi", kernel, chosen, precision=lax.Precision.HIGHEST)
    slot_count = vis_dual.shape[0]
    live_mask = (jnp.arange(slot_count, dtype=jnp.int32) < live_blocks[0]).astype(jnp.float32)[
        :, None, None
    ]
    misfit = (vis_dual / 0.5 + model - observed) * live_mask
    totals = lax.psum((jnp.sum(misfit * misfit), jnp.sum(live_mask)), ("vis", "tile"))
    radius = jnp.sqrt(2.0 * block_width * totals[1])
    size_now = jnp.sqrt(totals[0])
    vis_next = 0.5 * misfit * (1.0 - radius / jnp.maximum(size_now, radius))
    contrib = jnp.einsum("ij,csi->scj", kernel, vis_next, precision=lax.Precision.HIGHEST)
    selector = (block_index[:, None] == jnp.arange(block_count, dtype=jnp.int32)[None, :]).astype(
        jnp.float32
    )
    grid_adj = jnp.einsum("cu,scj->suj", selector, contrib, precision=lax.Precision.HIGHEST)
    grid_adj = grid_adj.reshape(2, slab_cols, rows_here)
    column_adj_real, column_adj_imag = (
        lax.all_to_all(grid_adj[0], "vis", split_axis=1, concat_axis=0, tiled=True),
        lax.all_to_all(grid_adj[1], "vis", split_axis=1, concat_axis=0, tiled=True),
    )
    inverse_real, inverse_imag = transform_axis(column_adj_real, column_adj_imag, 1.0, 0, False)
    half_real, half_imag = (
        lax.all_to_all(inverse_real, "vis", split_axis=0, concat_axis=1, tiled=True),
        lax.all_to_all(inverse_imag, "vis", split_axis=0, concat_axis=1, tiled=True),
    )
    row_adj_real, row_adj_imag = (
        lax.all_to_all(half_real, "tile", split_axis=0, concat_axis=1, tiled=True),
        lax.all_to_all(half_imag, "tile", split_axis=0, concat_axis=1, tiled=True),
    )
    pixel_real, unused_part = transform_axis(row_adj_real, row_adj_imag, 1.0, 1, True)
    data_term = (
        lax.all_to_all(pixel_real, "tile", split_axis=1, concat_axis=0, tiled=True) * norm_scale
    )
    approx_one, detail_one = analyse_local(extrapolated)
    approx_two, detail_two = analyse_local(approx_one)
    child = tree_dual[0] + 0.5 * detail_one
    parent = tree_dual[1] + 0.5 * jnp.repeat(detail_two, 2, axis=1)
    factor = 1.0 / jnp.maximum(jnp.sqrt(child * child + parent * parent), 1.0)
    child_next = child * factor
    parent_next = parent * factor
    parent_sum = parent_next[:, 0::2] + parent_next[:, 1::2]
    parent_tail = shifted(parent_sum[:, -3:], "tile", 1)
    level_one = upsample(None, jnp.concatenate([parent_tail, parent_sum], axis=1))
    both_tails = shifted(jnp.stack([level_one[:, -3:], child_next[:, -3:]]), "tile", 1)
    prior_term = upsample(
        jnp.concatenate([both_tails[0], level_one], axis=1),
        jnp.concatenate([both_tails[1], child_next], axis=1),
    )
    image_next = jnp.maximum(image - 0.5 * (data_term + prior_term), 0.0)
    return (image_next, vis_next, jnp.stack([child_next, parent_next]))


def solution(mesh):
    return jax.shard_map(
        on_device,
        mesh=mesh,
        in_specs=(
            P("vis", "tile"),
            P("vis", "tile"),
            P(("vis", "tile"), None, None),
            P(None, "vis", "tile"),
            P(("vis", "tile"), None, None),
            P(),
            P(("vis", "tile")),
            P(("vis", "tile")),
        ),
        out_specs=(P("vis", "tile"), P(("vis", "tile"), None, None), P(None, "vis", "tile")),
        check_vma=False,
    )
```

profile of v0, /device:TPU:0, one launch (start us, length us, event | category | flops | bytes accessed | tf_op | source)
XLA Modules:
  0.0 2884.7 jit_solution(4559415872826168675)
XLA Ops:
  7.3 184.0 %all-to-all-done = f32[4,256,2048]{2,1,0:T(8,128)} async-done(((f32[4,256,2048]{2,1,0:T(8,128)}), f32[4,256,2048]{2,1,0:T(8,128)}, u32[]{:S(2)}, u32[]{:S(2)}) %all-to-all-start) | async-done | bytes 8388640 | tf_op jit(solution)/shard_map/all_to_all | solution.py:132
  242.3 21.5 fusion.44
  263.8 26.9 add_bitcast_fusion.1
  323.6 22.6 bitcast_add_fusion.1
  357.7 129.7 %all-to-all-done.3 = f32[256,4,2048]{0,2,1:T(8,128)} async-done(((f32[256,4,2048]{0,2,1:T(8,128)}), f32[256,4,2048]{0,2,1:T(8,128)}, u32[]{:S(2)}, u32[]{:S(2)}) %all-to-all-start.3) | async-done | bytes 8388640 | tf_op jit(solution)/shard_map/all_to_all | solution.py:136
  515.2 160.5 %all-to-all-done.1 = f32[256,4,2048]{0,2,1:T(8,128)} async-done(((f32[256,4,2048]{0,2,1:T(8,128)}), f32[256,4,2048]{0,2,1:T(8,128)}, u32[]{:S(2)}, u32[]{:S(2)}) %all-to-all-start.1) | async-done | bytes 8388640 | tf_op jit(solution)/shard_map/all_to_all | solution.py:135
  703.2 71.9 %all-to-all-done.4 = f32[1024,8,256]{2,0,1:T(8,128)} async-done(((f32[1024,8,256]{2,0,1:T(8,128)}), f32[1024,8,256]{2,0,1:T(8,128)}, u32[]{:S(2)}, u32[]{:S(2)}) %all-to-all-start.4) | async-done | bytes 8388640 | tf_op jit(solution)/shard_map/all_to_all | solution.py:140
  815.7 58.6 %all-to-all-done.2 = f32[1024,8,256]{2,0,1:T(8,128)} async-done(((f32[1024,8,256]{2,0,1:T(8,128)}), f32[1024,8,256]{2,0,1:T(8,128)}, u32[]{:S(2)}, u32[]{:S(2)}) %all-to-all-start.2) | async-done | bytes 8388640 | tf_op jit(solution)/shard_map/all_to_all | solution.py:139
  892.0 20.4 multiply_subtract_fusion.1
  953.4 20.2 subtract_add_fusion.3
  1001.8 82.4 %all-to-all-done.5 = f32[8,1024,256]{2,1,0:T(8,128)} async-done(((f32[8,1024,256]{2,1,0:T(8,128)}), f32[8,1024,256]{2,1,0:T(8,128)}, u32[]{:S(2)}, u32[]{:S(2)}) %all-to-all-start.5) | async-done | bytes 8388640 | tf_op jit(solution)/shard_map/all_to_all | solution.py:144
  1111.6 72.1 %all-to-all-done.6 = f32[8,1024,256]{2,1,0:T(8,128)} async-done(((f32[8,1024,256]{2,1,0:T(8,128)}), f32[8,1024,256]{2,1,0:T(8,128)}, u32[]{:S(2)}, u32[]{:S(2)}) %all-to-all-start.6) | async-done | bytes 8388640 | tf_op jit(solution)/shard_map/all_to_all | solution.py:145
  1207.9 20.1 maximum_multiply_fusion
  1236.2 37.1 %all-reduce = (f32[]{:T(128)}, f32[]{:T(128)}) all-reduce(f32[]{:T(128)} %fusion.180, f32[]{:T(128)} %get-tuple-element.37), channel_id=1, replica_groups=mesh['vis'=8,'tile'=4] {'vis','tile'}, use_global_device_ids=true, to_apply=%region_1.2 | all-reduce | flops 2 | bytes 16 | tf_op jit(solution)/shard_map/psum | solution.py:157
  1352.6 65.9 %all-to-all-done.8 = f32[1024,8,256]{2,0,1:T(8,128)} async-done(((f32[1024,8,256]{2,0,1:T(8,128)}), f32[1024,8,256]{2,0,1:T(8,128)}, u32[]{:S(2)}, u32[]{:S(2)}) %all-to-all-start.8) | async-done | bytes 8388640 | tf_op jit(solution)/shard_map/all_to_all | solution.py:169
  1458.8 58.8 %all-to-all-done.7 = f32[1024,8,256]{2,0,1:T(8,128)} async-done(((f32[1024,8,256]{2,0,1:T(8,128)}), f32[1024,8,256]{2,0,1:T(8,128)}, u32[]{:S(2)}, u32[]{:S(2)}) %all-to-all-start.7) | async-done | bytes 8388640 | tf_op jit(solution)/shard_map/all_to_all | solution.py:168
  1535.2 22.0 multiply_subtract_fusion
  1557.2 20.4 fusion.12
  1621.3 19.4 subtract_add_fusion.1
  1652.4 46.7 %all-to-all-done.11 = f32[8,1024,256]{2,1,0:T(8,128)} async-done(((f32[8,1024,256]{2,1,0:T(8,128)}), f32[8,1024,256]{2,1,0:T(8,128)}, u32[]{:S(2)}, u32[]{:S(2)}) %all-to-all-start.11) | async-done | bytes 8388640 | tf_op jit(solution)/shard_map/all_to_all | solution.py:174
  1725.0 73.2 %all-to-all-done.9 = f32[8,1024,256]{2,1,0:T(8,128)} async-done(((f32[8,1024,256]{2,1,0:T(8,128)}), f32[8,1024,256]{2,1,0:T(8,128)}, u32[]{:S(2)}, u32[]{:S(2)}) %all-to-all-start.9) | async-done | bytes 8388640 | tf_op jit(solution)/shard_map/all_to_all | solution.py:173
  1824.9 159.9 %all-to-all-done.12 = f32[4,256,2048]{2,1,0:T(8,128)} async-done(((f32[4,256,2048]{2,1,0:T(8,128)}), f32[4,256,2048]{2,1,0:T(8,128)}, u32[]{:S(2)}, u32[]{:S(2)}) %all-to-all-start.12) | async-done | bytes 8388640 | tf_op jit(solution)/shard_map/all_to_all | solution.py:178
  2036.4 137.0 %all-to-all-done.10 = f32[4,256,2048]{2,1,0:T(8,128)} async-done(((f32[4,256,2048]{2,1,0:T(8,128)}), f32[4,256,2048]{2,1,0:T(8,128)}, u32[]{:S(2)}, u32[]{:S(2)}) %all-to-all-start.10) | async-done | bytes 8388640 | tf_op jit(solution)/shard_map/all_to_all | solution.py:177
  2208.3 19.8 subtract_bitcast_fusion
  2325.2 84.6 %collective-permute-done = f32[1024,6]{0,1:T(8,128)S(1)} collective-permute-done((f32[1024,6]{0,1:T(8,128)S(1)}, f32[1024,6]{0,1:T(8,128)S(1)}, u32[]{:S(2)}, u32[]{:S(2)}) %collective-permute-start) | collective-permute-done | bytes 24608 | tf_op jit(solution)/shard_map/ppermute | solution.py:27
  2418.2 18.8 slice.122
  2455.8 18.8 slice.124
  2474.6 18.8 slice.125
  2512.1 18.8 slice.127
  2675.5 21.2 fusion.55
  2725.3 36.7 %collective-permute-start.2 = (f32[1024,3]{0,1:T(4,128)S(1)}, f32[1024,3]{0,1:T(4,128)S(1)}, u32[]{:S(2)}, u32[]{:S(2)}) collective-permute-start(f32[1024,3]{0,1:T(4,128)S(1)} %slice.160), channel_id=1, source_target_pairs={{3,0},{0,1},{1,2},{2,3},{7,4},{4,5},{5,6},{6,7},{11,8},{8,9},{9,10... | collective-permute-start | bytes 36872 | tf_op jit(solution)/shard_map/ppermute | solution.py:27
  2797.6 21.3 add_bitcast_fusion.4
  (172 shorter events, 1091.1 us)
Async XLA Ops:
  0.6 1234.5 %copy-start = (f32[128,128]{1,0:T(8,128)S(1)}, f32[128,128]{1,0:T(8,128)}, u32[]{:S(2)}) copy-start(f32[128,128]{1,0:T(8,128)} %param.13) | copy-start | bytes 196612
  0.6 190.6 %all-to-all-start = ((f32[4,256,2048]{2,1,0:T(8,128)}), f32[4,256,2048]{2,1,0:T(8,128)}, u32[]{:S(2)}, u32[]{:S(2)}) async-start(f32[4,256,2048]{2,1,0:T(8,128)} %bitcast.200), calls=%async_computation | async-start | bytes 16777216 | tf_op jit(solution)/shard_map/all_to_all | solution.py:132
  7.3 772.9 %copy-start.13 = (f32[64,128]{1,0:T(8,128)}, f32[64,128]{1,0:T(8,128)S(1)}, u32[]{:S(2)}) copy-start(f32[64,128]{1,0:T(8,128)S(1)} %get-tuple-element.42) | copy-start | bytes 98308
  242.3 21.5 copy-start.9
  299.0 188.4 %all-to-all-start.3 = ((f32[256,4,2048]{0,2,1:T(8,128)}), f32[256,4,2048]{0,2,1:T(8,128)}, u32[]{:S(2)}, u32[]{:S(2)}) async-start(f32[256,4,2048]{0,2,1:T(8,128)} %bitcast.205), calls=%async_computation.3 | async-start | bytes 16777216 | tf_op jit(solution)/shard_map/all_to_all | solution.py:136
  305.0 18.5 copy-start.4
  487.4 188.3 %all-to-all-start.1 = ((f32[256,4,2048]{0,2,1:T(8,128)}), f32[256,4,2048]{0,2,1:T(8,128)}, u32[]{:S(2)}, u32[]{:S(2)}) async-start(f32[256,4,2048]{0,2,1:T(8,128)} %bitcast.203), calls=%async_computation.1 | async-start | bytes 16777216 | tf_op jit(solution)/shard_map/all_to_all | solution.py:135
  675.7 99.4 %all-to-all-start.4 = ((f32[1024,8,256]{2,0,1:T(8,128)}), f32[1024,8,256]{2,0,1:T(8,128)}, u32[]{:S(2)}, u32[]{:S(2)}) async-start(f32[1024,8,256]{2,0,1:T(8,128)} %copy.171), calls=%async_computation.4 | async-start | bytes 16777216 | tf_op jit(solution)/shard_map/all_to_all | solution.py:140
  775.1 99.2 %all-to-all-start.2 = ((f32[1024,8,256]{2,0,1:T(8,128)}), f32[1024,8,256]{2,0,1:T(8,128)}, u32[]{:S(2)}, u32[]{:S(2)}) async-start(f32[1024,8,256]{2,0,1:T(8,128)} %copy.167), calls=%async_computation.2 | async-start | bytes 16777216 | tf_op jit(solution)/shard_map/all_to_all | solution.py:139
  953.3 20.3 copy-start.2
  985.1 99.0 %all-to-all-start.5 = ((f32[8,1024,256]{2,1,0:T(8,128)}), f32[8,1024,256]{2,1,0:T(8,128)}, u32[]{:S(2)}, u32[]{:S(2)}) async-start(f32[8,1024,256]{2,1,0:T(8,128)} %bitcast.207), calls=%async_computation.5 | async-start | bytes 16777216 | tf_op jit(solution)/shard_map/all_to_all | solution.py:144
  1084.2 99.5 %all-to-all-start.6 = ((f32[8,1024,256]{2,1,0:T(8,128)}), f32[8,1024,256]{2,1,0:T(8,128)}, u32[]{:S(2)}, u32[]{:S(2)}) async-start(f32[8,1024,256]{2,1,0:T(8,128)} %bitcast.202), calls=%async_computation.6 | async-start | bytes 16777216 | tf_op jit(solution)/shard_map/all_to_all | solution.py:145
  1207.9 27.2 copy-start.15
  1207.9 27.2 copy-start.16
  1319.1 99.4 %all-to-all-start.8 = ((f32[1024,8,256]{2,0,1:T(8,128)}), f32[1024,8,256]{2,0,1:T(8,128)}, u32[]{:S(2)}, u32[]{:S(2)}) async-start(f32[1024,8,256]{2,0,1:T(8,128)} %copy.193), calls=%async_computation.8 | async-start | bytes 16777216 | tf_op jit(solution)/shard_map/all_to_all | solution.py:169
  1418.5 99.0 %all-to-all-start.7 = ((f32[1024,8,256]{2,0,1:T(8,128)}), f32[1024,8,256]{2,0,1:T(8,128)}, u32[]{:S(2)}, u32[]{:S(2)}) async-start(f32[1024,8,256]{2,0,1:T(8,128)} %copy.190), calls=%async_computation.7 | async-start | bytes 16777216 | tf_op jit(solution)/shard_map/all_to_all | solution.py:168
  1557.2 20.4 copy-start.8
  1600.0 99.2 %all-to-all-start.11 = ((f32[8,1024,256]{2,1,0:T(8,128)}), f32[8,1024,256]{2,1,0:T(8,128)}, u32[]{:S(2)}, u32[]{:S(2)}) async-start(f32[8,1024,256]{2,1,0:T(8,128)} %bitcast.206), calls=%async_computation.11 | async-start | bytes 16777216 | tf_op jit(solution)/shard_map/all_to_all | solution.py:174
  1605.1 16.2 copy-start.6
  1699.1 99.0 %all-to-all-start.9 = ((f32[8,1024,256]{2,1,0:T(8,128)}), f32[8,1024,256]{2,1,0:T(8,128)}, u32[]{:S(2)}, u32[]{:S(2)}) async-start(f32[8,1024,256]{2,1,0:T(8,128)} %bitcast.204), calls=%async_computation.9 | async-start | bytes 16777216 | tf_op jit(solution)/shard_map/all_to_all | solution.py:173
  1798.2 186.6 %all-to-all-start.12 = ((f32[4,256,2048]{2,1,0:T(8,128)}), f32[4,256,2048]{2,1,0:T(8,128)}, u32[]{:S(2)}, u32[]{:S(2)}) async-start(f32[4,256,2048]{2,1,0:T(8,128)} %all_to_all.202), calls=%async_computation.12 | async-start | bytes 16777216 | tf_op jit(solution)/shard_map/all_to_all | solution.py:178
  1984.7 188.6 %all-to-all-start.10 = ((f32[4,256,2048]{2,1,0:T(8,128)}), f32[4,256,2048]{2,1,0:T(8,128)}, u32[]{:S(2)}, u32[]{:S(2)}) async-start(f32[4,256,2048]{2,1,0:T(8,128)} %all_to_all.196), calls=%async_computation.10 | async-start | bytes 16777216 | tf_op jit(solution)/shard_map/all_to_all | solution.py:177
  2013.3 12.8 copy-start.7
  2196.2 12.1 copy-start.14
  2268.7 585.8 %all-to-all-start.13 = ((f32[256,4,2048]{0,2,1:T(8,128)}), f32[256,4,2048]{0,2,1:T(8,128)}, u32[]{:S(2)}, u32[]{:S(2)}) async-start(f32[256,4,2048]{0,2,1:T(8,128)} %bitcast.201), calls=%async_computation.13 | async-start | bytes 16777216 | tf_op jit(solution)/shard_map/all_to_all | solution.py:182
  2284.6 125.2 %collective-permute-start = (f32[1024,6]{0,1:T(8,128)S(1)}, f32[1024,6]{0,1:T(8,128)S(1)}, u32[]{:S(2)}, u32[]{:S(2)}) collective-permute-start(f32[1024,6]{0,1:T(8,128)S(1)} %slice.158), channel_id=1, source_target_pairs={{1,0},{2,1},{3,2},{0,3},{5,4},{6,5},{7,6},{4,7},{9,8},{10,9},{11,1... | collective-permute-start | bytes 73736 | tf_op jit(solution)/shard_map/ppermute | solution.py:27
  2543.6 13.0 copy-start.10
  2543.6 50.5 %collective-permute-start.1 = (f32[1024,6]{0,1:T(8,128)S(1)}, f32[1024,6]{0,1:T(8,128)S(1)}, u32[]{:S(2)}, u32[]{:S(2)}) collective-permute-start(f32[1024,6]{0,1:T(8,128)S(1)} %slice.159), channel_id=1, source_target_pairs={{1,0},{2,1},{3,2},{0,3},{5,4},{6,5},{7,6},{4,7},{9,8},{10,9},{11,1... | collective-permute-start | bytes 73736 | tf_op jit(solution)/shard_map/ppermute | solution.py:27
  2725.3 38.2 %collective-permute-start.2 = (f32[1024,3]{0,1:T(4,128)S(1)}, f32[1024,3]{0,1:T(4,128)S(1)}, u32[]{:S(2)}, u32[]{:S(2)}) collective-permute-start(f32[1024,3]{0,1:T(4,128)S(1)} %slice.160), channel_id=1, source_target_pairs={{3,0},{0,1},{1,2},{2,3},{7,4},{4,5},{5,6},{6,7},{11,8},{8,9},{9,10... | collective-permute-start | bytes 36872 | tf_op jit(solution)/shard_map/ppermute | solution.py:27
  2777.8 19.8 collective-permute-start.3
  2844.4 9.2 copy-start.12
  2870.6 13.6 copy-start.1
  (4 other events, 23.9 us)
where the time goes:
time: 2900 us; the launch traced here: 2880 us
  waiting for transfers between devices  1400 us (48%)
  local copies, waits for them, and re-layouts  689 us (24%)
  matrix products  494 us (17%)
  other arithmetic  141 us (5%)
  starting transfers between devices  124 us (4%)
  blocking collectives  37.1 us (1%)
    slice x16, local copies, waits for them, and re-layouts, analyse_local(): lax.slice_in_dim(extended, position, position + 2 * half_rows - 1, 2, 1)  227 us
    all_to_all x1, waiting for transfers between devices, on_device(): lax.all_to_all(extrapolated, 'tile', split_axis=0, concat_axis=1, tiled=T...  184 us
    all_to_all x1, waiting for transfers between devices, on_device(): lax.all_to_all(part_real, 'tile', split_axis=1, concat_axis=0, tiled=True)  160 us
    all_to_all x1, waiting for transfers between devices, on_device(): lax.all_to_all(half_imag, 'tile', split_axis=0, concat_axis=1, tiled=True)  160 us
    dot_general x8, matrix products, complex_einsum(): real_part = jnp.einsum(form, left_real, table_cos, precision=precise)  149 us
    all_to_all x1, waiting for transfers between devices, on_device(): lax.all_to_all(half_real, 'tile', split_axis=0, concat_axis=1, tiled=True)  137 us
    all_to_all x1, waiting for transfers between devices, on_device(): lax.all_to_all(part_imag, 'tile', split_axis=1, concat_axis=0, tiled=True)  130 us
    dot_general x7, matrix products, complex_einsum(): imag_part = jnp.einsum(form, left_real, table_sin, precision=precise)  122 us
  transfers between devices with their start and end apart: 18, of which 16 were waited for; matrix products, arithmetic and copies ran while one was open for 27% of the time, Pallas kernels for 0%

commit v1 on v0

--- a/solution.py
+++ b/solution.py
@@ -98,10 +98,13 @@
     half_rows = coarse.shape[1] // 2
     next_rows = shifted(coarse[:, :6], "tile", -1)
     extended = jnp.concatenate([coarse, next_rows], axis=1)
+    phases = [
+        lax.slice_in_dim(extended, parity, extended.shape[1], 2, 1) for parity in range(2)
+    ]
     approx = jnp.zeros((coarse.shape[0], half_rows), jnp.float32)
     detail = jnp.zeros_like(approx)
     for position in range(8):
-        strided = lax.slice_in_dim(extended, position, position + 2 * half_rows - 1, 2, 1)
+        strided = lax.slice_in_dim(phases[position % 2], position // 2, position // 2 + half_rows, 1, 1)
         approx = approx + LOW_TAPS[position] * strided
         detail = detail + HIGH_TAPS[position] * strided
     return (approx, detail)
@@ -122,34 +125,86 @@
     return jnp.stack([even_part, odd_part], axis=2).reshape(ext_detail.shape[0], 2 * out_rows)
 
 
+def split_three(values):
+    first = lax.reduce_precision(values, exponent_bits=8, mantissa_bits=7)
+    rest = values - first
+    second = lax.reduce_precision(rest, exponent_bits=8, mantissa_bits=7)
+    third = rest - second
+    pieces = [first, second, third]
+    return jnp.concatenate([piece.astype(jnp.bfloat16) for piece in pieces], axis=-1)
+
+
+def pick_rows(index, table):
+    width = table.shape[1]
+    selector = (index[:, None] == jnp.arange(table.shape[0], dtype=jnp.int32)[None, :]).astype(
+        jnp.bfloat16
+    )
+    summed = jnp.dot(selector, split_three(table), preferred_element_type=jnp.float32)
+    return summed[:, :width] + summed[:, width : 2 * width] + summed[:, 2 * width :]
+
+
+def rows_to_grid(local_rows, values, row_count):
+    groups, members, width = values.shape
+    pieces = split_three(values)
+    selector = (
+        jnp.arange(row_count, dtype=jnp.int32)[None, :, None] == local_rows[:, None, :]
+    ).astype(jnp.bfloat16)
+    summed = jnp.einsum("gkb,gbc->gkc", selector, pieces, preferred_element_type=jnp.float32)
+    summed = summed[..., :width] + summed[..., width : 2 * width] + summed[..., 2 * width :]
+    return summed.reshape(groups * row_count, width)
+
+
 def on_device(image, extrapolated, vis_dual, tree_dual, observed, kernel, block_index, live_blocks):
-    slab_cols = image.shape[0]
-    rows_here = image.shape[1]
+    precise = lax.Precision.HIGHEST
+    slab_rows, slab_cols = image.shape
+    n_vis = lax.axis_size("vis")
+    n_tile = lax.axis_size("tile")
+    vis_id = lax.axis_index("vis")
+    tile_id = lax.axis_index("tile")
+    len_rows = slab_rows * n_vis
+    len_cols = slab_cols * n_tile
     block_width = kernel.shape[0]
-    total_rows = rows_here * lax.axis_size("tile")
-    spectral_len = slab_cols * lax.axis_size("vis")
-    norm_scale = 1.0 / math.sqrt(spectral_len * total_rows)
-    row_real = lax.all_to_all(extrapolated, "tile", split_axis=0, concat_axis=1, tiled=True)
-    part_real, part_imag = transform_axis(row_real, None, -1.0, 1, False)
-    back_real, back_imag = (
-        lax.all_to_all(part_real, "tile", split_axis=1, concat_axis=0, tiled=True),
-        lax.all_to_all(part_imag, "tile", split_axis=1, concat_axis=0, tiled=True),
-    )
-    pencil_real, pencil_imag = (
-        lax.all_to_all(back_real, "vis", split_axis=1, concat_axis=0, tiled=True),
-        lax.all_to_all(back_imag, "vis", split_axis=1, concat_axis=0, tiled=True),
-    )
-    done_real, done_imag = transform_axis(pencil_real, pencil_imag, -1.0, 0, False)
-    grid_real, grid_imag = (
-        lax.all_to_all(done_real, "vis", split_axis=0, concat_axis=1, tiled=True),
-        lax.all_to_all(done_imag, "vis", split_axis=0, concat_axis=1, tiled=True),
-    )
-    grid = jnp.stack([grid_real, grid_imag]) * norm_scale
-    block_count = slab_cols * (rows_here // block_width)
-    blocks = grid.reshape(2, block_count, block_width)
-    chosen = jnp.take(blocks, block_index, axis=1)
-    model = jnp.einsum("ij,scj->csi", kernel, chosen, precision=lax.Precision.HIGHEST)
+    chunk = slab_cols // n_vis
     slot_count = vis_dual.shape[0]
+    norm_scale = 1.0 / math.sqrt(len_rows * len_cols)
+    columns = lax.all_to_all(extrapolated, "vis", split_axis=1, concat_axis=0, tiled=True)
+    spec_real, spec_imag = transform_axis(columns, None, -1.0, 0, False)
+    all_index = lax.all_gather(block_index, ("vis", "tile"), tiled=True)
+    total_blocks = all_index.shape[0]
+    owner = jnp.arange(total_blocks, dtype=jnp.int32) // slot_count
+    per_row = slab_cols // block_width
+    local_row = all_index // per_row
+    row_of = (owner // n_tile) * slab_rows + local_row
+    band_of = (owner % n_tile) * per_row + all_index % per_row
+    col_ids = tile_id * slab_cols + vis_id * chunk + jnp.arange(chunk, dtype=jnp.int32)
+    band_count = len_cols // block_width
+    band_turns = (
+        (jnp.arange(band_count, dtype=jnp.int32) * block_width)[:, None] * col_ids[None, :]
+    ) % len_cols
+    band_angles = band_turns.astype(jnp.float32) * (TWO_PI / len_cols)
+    band_both = pick_rows(band_of, jnp.concatenate([jnp.cos(band_angles), jnp.sin(band_angles)], 1))
+    band_cos = band_both[:, :chunk]
+    band_sin = band_both[:, chunk:]
+    cell_turns = (col_ids[:, None] * jnp.arange(block_width, dtype=jnp.int32)[None, :]) % len_cols
+    cell_angles = cell_turns.astype(jnp.float32) * (TWO_PI / len_cols)
+    cell_cos = jnp.cos(cell_angles)
+    cell_sin = jnp.sin(cell_angles)
+    picked_real = jnp.take(spec_real, row_of, axis=0)
+    picked_imag = jnp.take(spec_imag, row_of, axis=0)
+    twisted_real = picked_real * band_cos + picked_imag * band_sin
+    twisted_imag = picked_imag * band_cos - picked_real * band_sin
+    part_real = jnp.dot(twisted_real, cell_cos, precision=precise) + jnp.dot(
+        twisted_imag, cell_sin, precision=precise
+    )
+    part_imag = jnp.dot(twisted_imag, cell_cos, precision=precise) - jnp.dot(
+        twisted_real, cell_sin, precision=precise
+    )
+    partial = jnp.stack([part_real, part_imag], axis=1)
+    partial = lax.all_to_all(partial, "vis", split_axis=0, concat_axis=0, tiled=True)
+    partial = partial.reshape((n_vis, total_blocks // n_vis) + partial.shape[1:]).sum(axis=0)
+    partial = lax.all_to_all(partial, "tile", split_axis=0, concat_axis=0, tiled=True)
+    chosen = partial.reshape((n_tile, slot_count) + partial.shape[1:]).sum(axis=0) * norm_scale
+    model = jnp.einsum("ij,csj->csi", kernel, chosen, precision=precise)
     live_mask = (jnp.arange(slot_count, dtype=jnp.int32) < live_blocks[0]).astype(jnp.float32)[
         :, None, None
     ]
@@ -158,28 +213,23 @@
     radius = jnp.sqrt(2.0 * block_width * totals[1])
     size_now = jnp.sqrt(totals[0])
     vis_next = 0.5 * misfit * (1.0 - radius / jnp.maximum(size_now, radius))
-    contrib = jnp.einsum("ij,csi->scj", kernel, vis_next, precision=lax.Precision.HIGHEST)
-    selector = (block_index[:, None] == jnp.arange(block_count, dtype=jnp.int32)[None, :]).astype(
-        jnp.float32
-    )
-    grid_adj = jnp.einsum("cu,scj->suj", selector, contrib, precision=lax.Precision.HIGHEST)
-    grid_adj = grid_adj.reshape(2, slab_cols, rows_here)
-    column_adj_real, column_adj_imag = (
-        lax.all_to_all(grid_adj[0], "vis", split_axis=1, concat_axis=0, tiled=True),
-        lax.all_to_all(grid_adj[1], "vis", split_axis=1, concat_axis=0, tiled=True),
-    )
-    inverse_real, inverse_imag = transform_axis(column_adj_real, column_adj_imag, 1.0, 0, False)
-    half_real, half_imag = (
-        lax.all_to_all(inverse_real, "vis", split_axis=0, concat_axis=1, tiled=True),
-        lax.all_to_all(inverse_imag, "vis", split_axis=0, concat_axis=1, tiled=True),
-    )
-    row_adj_real, row_adj_imag = (
-        lax.all_to_all(half_real, "tile", split_axis=0, concat_axis=1, tiled=True),
-        lax.all_to_all(half_imag, "tile", split_axis=0, concat_axis=1, tiled=True),
-    )
-    pixel_real, unused_part = transform_axis(row_adj_real, row_adj_imag, 1.0, 1, True)
+    contrib = jnp.einsum("ij,csi->csj", kernel, vis_next, precision=precise)
+    every = lax.all_gather(contrib, "tile", tiled=True)
+    every = lax.all_gather(every, "vis", tiled=True)
+    back_real = jnp.dot(every[:, 0, :], cell_cos.T, precision=precise) - jnp.dot(
+        every[:, 1, :], cell_sin.T, precision=precise
+    )
+    back_imag = jnp.dot(every[:, 0, :], cell_sin.T, precision=precise) + jnp.dot(
+        every[:, 1, :], cell_cos.T, precision=precise
+    )
+    turned_real = back_real * band_cos - back_imag * band_sin
+    turned_imag = back_real * band_sin + back_imag * band_cos
+    turned = jnp.concatenate([turned_real, turned_imag], axis=1)
+    turned = turned.reshape(n_vis, total_blocks // n_vis, 2 * chunk)
+    gridded = rows_to_grid(local_row.reshape(n_vis, total_blocks // n_vis), turned, slab_rows)
+    pixel_real, unused_part = transform_axis(gridded[:, :chunk], gridded[:, chunk:], 1.0, 0, True)
     data_term = (
-        lax.all_to_all(pixel_real, "tile", split_axis=1, concat_axis=0, tiled=True) * norm_scale
+        lax.all_to_all(pixel_real, "vis", split_axis=0, concat_axis=1, tiled=True) * norm_scale
     )
     approx_one, detail_one = analyse_local(extrapolated)
     approx_two, detail_two = analyse_local(approx_one)

time: 2900 us -> 1250 us (0.43)
  waiting for transfers between devices: 1400 us -> 53.5 us
  local copies, waits for them, and re-layouts: 689 us -> 373 us
  blocking collectives: 37.1 us -> 206 us
  matrix products: 494 us -> 355 us
  starting transfers between devices: 124 us -> 19 us
  other arithmetic: 141 us -> 212 us
    all_to_all x14 -> x3, waiting for transfers between devices: 1300 us -> 24.1 us  [the longest x1 24.1 us: on_device(): lax.all_to_all(partial, 'tile', split_axis=0, concat_axis=0, tiled=True)]
    slice x19 -> x5, local copies, waits for them, and re-layouts: 252 us -> 64.3 us  [the longest x4 57.8 us: analyse_local(): lax.slice_in_dim(extended, parity, extended.shape[1], 2, 1)]
    all_to_all x17 -> x1, local copies, waits for them, and re-layouts: 169 us -> 9.13 us  [on_device(): lax.all_to_all(extrapolated, 'vis', split_axis=1, concat_axis=0, tiled=True)]
    dot_general x3 -> x12, matrix products: 9.92 us -> 167 us  [the longest x1 31.5 us: rows_to_grid(): jnp.einsum('gkb,gbc->gkc', selector, pieces, preferred_element_type=jnp.f...]
    all_to_all x0 -> x1, blocking collectives: none -> 97.4 us  [on_device(): lax.all_to_all(partial, 'vis', split_axis=0, concat_axis=0, tiled=True)]
    ppermute x4, waiting for transfers between devices: 95 us -> 0.01 us  [shifted(): return lax.ppermute(block, axis, route)]
    dot_general x8 -> x4, matrix products: 149 us -> 68.3 us  [complex_einsum(): real_part = jnp.einsum(form, left_real, table_cos, precision=precise)]
    gather x1 -> x4, local copies, waits for them, and re-layouts: 6.76 us -> 87.2 us  [the longest x2 43.6 us: on_device(): picked_imag = jnp.take(spec_imag, row_of, axis=0)]
  transfers between devices with their start and end apart: 18 -> 9, of which waited for: 16 -> 2; matrix products, arithmetic and copies ran while one was open for 27% -> 24% of each run, Pallas kernels for 0% -> 0%
where the time goes in v1:
time: 1250 us; the launch traced here: 1240 us
  local copies, waits for them, and re-layouts  373 us (30%)
  matrix products  355 us (28%)
  other arithmetic  212 us (17%)
  blocking collectives  206 us (16%)
  waiting for transfers between devices  53.5 us (4%)
  starting transfers between devices  19 us (2%)
  between operations  17 us (1%)
    all_to_all x1, blocking collectives, on_device(): lax.all_to_all(partial, 'vis', split_axis=0, concat_axis=0, tiled=True)  97.4 us
    all_gather x1, blocking collectives, on_device(): all_index = lax.all_gather(block_index, ('vis', 'tile'), tiled=True)  70.9 us
    dot_general x4, matrix products, complex_einsum(): real_part = jnp.einsum(form, left_real, table_cos, precision=precise)  68.3 us
    slice x4, local copies, waits for them, and re-layouts, analyse_local(): lax.slice_in_dim(extended, parity, extended.shape[1], 2, 1)  57.8 us
    unnamed x59, local copies, waits for them, and re-layouts  51.8 us
    dot_general x3, matrix products, complex_einsum(): imag_part = jnp.einsum(form, left_real, table_sin, precision=precise)  46 us
    gather x2, local copies, waits for them, and re-layouts, on_device(): picked_imag = jnp.take(spec_imag, row_of, axis=0)  43.6 us
    gather x2, local copies, waits for them, and re-layouts, on_device(): picked_real = jnp.take(spec_real, row_of, axis=0)  43.6 us
  transfers between devices with their start and end apart: 9, of which 2 were waited for; matrix products, arithmetic and copies ran while one was open for 24% of the time, Pallas kernels for 0%

profile of v1, /device:TPU:0, one launch (start us, length us, event | category | flops | bytes accessed | tf_op | source)
XLA Modules:
  0.0 1235.9 jit_solution(12371021110578368048)
XLA Ops:
  21.8 70.9 %all-gather = s32[32,1,256]{2,1,0:T(1,128)S(1)} all-gather(s32[1,1,256]{2,1,0:T(1,128)S(1)} %bitcast.146), channel_id=1, replica_groups=mesh['vis'=8,'tile'=4] {'vis','tile'}, dimensions={0}, use_global_device_ids=true | all-gather | bytes 33792 | tf_op jit(solution)/shard_map/all_gather | solution.py:172
  94.1 19.4 %fusion.63 = f32[8192,1536]{0,1:T(8,128)} fusion(s32[8192]{0:T(1024)S(1)} %fusion.124, bf16[64,512]{1,0:T(8,128)(2,1)S(1)} %get-tuple-element.55, bf16[64,512]{1,0:T(8,128)(2,1)S(1)} %get-tuple-element.54, bf16[64,512]{1,0:T(8,128)(2,1)S(1)} %get-tuple-element.53), kind=kOutput, calls=%fused_computation.120 | convolution fusion | flops 1611726848 | bytes 50561024 | tf_op jit(solution)/shard_map/dot_general | solution.py:142
  113.5 22.7 %slice_add_fusion.2 = f32[8192,512]{0,1:T(8,128)} fusion(f32[8192,1536]{0,1:T(8,128)} %fusion.63), kind=kLoop, calls=%fused_computation.16 | loop fusion | flops 8388608 | bytes 67108864 | tf_op jit(solution)/shard_map/add | solution.py:143
  145.4 17.5 %fusion.33 = f32[64,128,256]{2,0,1:T(8,128)} fusion(f32[64,128,256]{2,1,0:T(8,128)} %bitcast.127), kind=kOutput, calls=%fused_computation.66 | convolution fusion | flops 1610670080 | bytes 16777216 | tf_op jit(solution)/shard_map/abm,ca->cbm/dot_general | solution.py:46
  162.9 18.6 %multiply_subtract_fusion.3 = (f32[64,128,256]{2,0,1:T(8,128)S(1)}, f32[64,128,256]{2,0,1:T(8,128)}) fusion(f32[64,128,256]{2,0,1:T(8,128)} %fusion.33, f32[64,128]{0,1:T(8,128)S(1)} %get-tuple-element.64, f32[64,128]{0,1:T(8,128)S(1)} %get-tuple-element.65, f32[64,128,256]{2,1,0:T(8,128)} %bitcast.128), kind=kOutput, calls=%fused_computation.48 | convolution fusion | flops 1627451392 | bytes 33619968 | tf_op jit(solution)/shard_map/abm,ca->cbm/dot_general | solution.py:51
  181.5 17.5 %fusion.27 = f32[128,64,256]{2,0,1:T(8,128)} fusion(f32[64,128,256]{2,0,1:T(8,128)} %get-tuple-element.41), kind=kOutput, calls=%fused_computation.60 | convolution fusion | flops 3221454848 | bytes 16777216 | tf_op jit(solution)/shard_map/cbm,db->dcm/dot_general | solution.py:53
  212.5 14.3 %fusion.45 = f32[128,64,256]{2,0,1:T(8,128)S(1)} fusion(f32[128,64,256]{2,0,1:T(8,128)} %fusion.27, f32[64,128,256]{2,0,1:T(8,128)S(1)} %get-tuple-element.40), kind=kOutput, calls=%fused_computation.94 | convolution fusion | flops 3223568384 | bytes 25165824 | tf_op jit(solution)/shard_map/cbm,db->dcm/dot_general | solution.py:51
  235.1 17.4 %subtract_add_fusion.1 = f32[128,64,256]{2,0,1:T(8,128)} fusion(f32[128,64,256]{2,0,1:T(8,128)} %fusion.25, f32[128,64,256]{2,0,1:T(8,128)S(1)} %fusion.45, f32[64,128,256]{2,0,1:T(8,128)S(1)} %get-tuple-element.40), kind=kOutput, calls=%fused_computation.46 | convolution fusion | flops 3227746304 | bytes 33554432 | tf_op jit(solution)/shard_map/cbm,db->dcm/dot_general | solution.py:46
  264.0 34.7 %gather_fusion = f32[8192,256]{1,0:T(8,128)} fusion(f32[8192,256]{1,0:T(8,128)} %bitcast.121, s32[8192]{0:T(1024)S(1)} %broadcast_clamp_fusion), kind=kCustom, calls=%fused_computation.clone | custom fusion | bytes 16809984 | tf_op jit(solution)/shard_map/jit(_take)/gather | solution.py:192
  307.6 34.7 %gather_fusion.1 = f32[8192,256]{1,0:T(8,128)} fusion(f32[8192,256]{1,0:T(8,128)} %bitcast.120, s32[8192]{0:T(1024)S(1)} %broadcast_clamp_fusion), kind=kCustom, calls=%fused_computation.1.clone | custom fusion | bytes 16809984 | tf_op jit(solution)/shard_map/jit(_take)/gather | solution.py:193
  351.3 19.2 %multiply_add_fusion.2 = (f32[8192,256]{0,1:T(8,128)}, f32[8192,256]{0,1:T(8,128)}) fusion(f32[8192,256]{0,1:T(8,128)} %copy.250, f32[8192,256]{0,1:T(8,128)} %copy.248, f32[8192,512]{0,1:T(8,128)} %slice_add_fusion.2, pred[8192]{0:T(1024)(128)(4,1)S(1)} %get-tuple-element.30), kind=kLoop, calls=%fused_computation.45 | loop fusion | flops 16777216 | bytes 50339840 | tf_op jit(solution)/shard_map/add | solution.py:194
  370.5 17.2 %fusion.104 = f32[8192,128]{1,0:T(8,128)S(1)} fusion(f32[8192,256]{0,1:T(8,128)} %get-tuple-element.36, s32[256]{0:T(256)S(1)} %copy-done.16), kind=kOutput, calls=%fused_computation.183 | convolution fusion | flops 3221684224 | bytes 12583936 | tf_op jit(solution)/shard_map/dot_general | solution.py:196
  387.8 14.6 %fusion.102 = f32[8192,128]{1,0:T(8,128)S(1)} fusion(f32[8192,256]{0,1:T(8,128)S(1)} %copy-done.2, s32[256]{0:T(256)S(1)} %copy-done.16), kind=kOutput, calls=%fused_computation.182 | convolution fusion | flops 3221684224 | bytes 12583936 | tf_op jit(solution)/shard_map/dot_general | solution.py:199
  402.4 14.8 %fusion.9 = f32[8192,1,128]{2,0,1:T(8,128)S(1)} fusion(f32[8192,128]{1,0:T(8,128)S(1)} %fusion.104, f32[8192,256]{0,1:T(8,128)S(1)} %copy-done.2, s32[256]{0:T(256)S(1)} %copy-done.16), kind=kOutput, calls=%fused_computation.25 | convolution fusion | flops 3222732800 | bytes 16778240 | tf_op jit(solution)/shard_map/dot_general | solution.py:196
  417.2 14.6 %fusion.8 = f32[8192,1,128]{2,0,1:T(8,128)S(1)} fusion(f32[8192,128]{1,0:T(8,128)S(1)} %fusion.102, f32[8192,256]{0,1:T(8,128)S(1)} %bitcast.123, s32[256]{0:T(256)S(1)} %copy-done.16), kind=kOutput, calls=%fused_computation.23 | convolution fusion | flops 3222732800 | bytes 16778240 | tf_op jit(solution)/shard_map/dot_general | solution.py:199
  432.3 31.2 %copy.251 = f32[8192,2,128]{2,1,0:T(2,128)S(1)} copy(f32[8192,2,128]{2,0,1:T(8,128)S(1)} %pad_maximum_fusion.2) | data formatting | bytes 16777216 | tf_op jit(solution)/shard_map/stack | solution.py:202
  463.5 97.4 %all_to_all.39 = f32[8192,2,128]{2,1,0:T(2,128)} all-to-all(f32[8192,2,128]{2,1,0:T(2,128)S(1)} %copy.251), channel_id=1, replica_groups=mesh['vis'=8,'tile'=4] {'vis'}, dimensions={0} | all-to-all | bytes 16777216 | tf_op jit(solution)/shard_map/all_to_all | solution.py:203
  573.2 24.1 %all-to-all-done.2 = f32[1024,2,128]{2,1,0:T(2,128)S(1)} async-done(((f32[1024,2,128]{2,1,0:T(2,128)}), f32[1024,2,128]{2,1,0:T(2,128)S(1)}, u32[]{:S(2)}, u32[]{:S(2)}) %all-to-all-start.2) | async-done | bytes 1048608 | tf_op jit(solution)/shard_map/all_to_all | solution.py:205
  598.9 37.5 %all-reduce = (f32[]{:T(128)}, f32[]{:T(128)}) all-reduce(f32[]{:T(128)} %fusion.168, f32[]{:T(128)} %get-tuple-element.60), channel_id=1, replica_groups=mesh['vis'=8,'tile'=4] {'vis','tile'}, use_global_device_ids=true, to_apply=%region_3.5 | all-reduce | flops 2 | bytes 16 | tf_op jit(solution)/shard_map/psum | solution.py:212
  639.7 29.3 %all-gather.4.cloned.1.call-done = f32[1024,2,128]{2,0,1:T(8,128)} async-done(((f32[256,2,128]{2,0,1:T(8,128)}), f32[1024,2,128]{2,0,1:T(8,128)}) %all-gather.4.cloned.1.call-update) | async-done | bytes 1048592 | tf_op jit(solution)/shard_map/all_gather | solution.py:217
  684.5 18.9 %slice.172 = f32[1024,1027]{0,1:T(8,128)} slice(f32[1024,2054]{0,1:T(8,128)} %pad_maximum_fusion.1), slice={[0:1024:1], [0:2054:2]} | slice | bytes 8413184 | tf_op jit(solution)/shard_map/slice | solution.py:102
  703.4 18.8 %slice.174 = f32[1024,1027]{0,1:T(8,128)} slice(f32[1024,2054]{0,1:T(8,128)} %pad_maximum_fusion.1), slice={[0:1024:1], [1:2054:2]} | slice | bytes 8413184 | tf_op jit(solution)/shard_map/slice | solution.py:102
  722.2 13.6 %multiply_add_fusion.5 = f32[1024,1024]{0,1:T(8,128)S(1)} fusion(f32[1024,1027]{0,1:T(8,128)} %slice.174, f32[1024,1027]{0,1:T(8,128)} %slice.172), kind=kLoop, calls=%fused_computation.91 | loop fusion | flops 15728640 | bytes 37748736 | tf_op jit(solution)/shard_map/add | solution.py:108
  806.6 22.0 %multiply_subtract_fusion.1 = (f32[8192,256]{0,1:T(8,128)}, f32[8192,256]{0,1:T(8,128)}) fusion(f32[8192,256]{0,1:T(8,128)} %convolution_subtract_fusion, f32[8192,512]{0,1:T(8,128)} %slice_add_fusion.2, f32[8192,256]{0,1:T(8,128)} %fusion.43, s32[256]{0:T(256)S(1)} %copy-done.16, f32[8192,2,128]{2,0,1:T(8,128)} %all-gather.6.cloned.1.call-done), kind=kOutput, calls=%fused_computation.43 | convolution fusion | flops 3236364288 | bytes 54526976 | tf_op jit(solution)/shard_map/dot_general | solution.py:222
  840.3 17.5 %copy.276 = f32[8192,512]{1,0:T(8,128)} copy(f32[8192,512]{0,1:T(8,128)} %pad_maximum_fusion) | data formatting | bytes 33554432 | tf_op jit(solution)/shard_map/reshape | solution.py:228
  868.2 31.5 %fusion = f32[8,1024,1536]{2,1,0:T(8,128)} fusion(bf16[8,1024,512]{2,1,0:T(8,128)(2,1)S(1)} %get-tuple-element.45, bf16[8,1024,512]{2,1,0:T(8,128)(2,1)} %get-tuple-element.46, bf16[8,1024,512]{2,1,0:T(8,128)(2,1)S(1)} %get-tuple-element.44, s32[8,1024]{1,0:T(8,128)S(1)} %eq.45), kind=kOutput, calls=%fused_computation.3 | convolution fusion | flops 25853689856 | bytes 75530240 | tf_op jit(solution)/shard_map/gkb,gbc->gkc/dot_general | solution.py:152
  899.7 23.9 %slice_add_fusion = f32[8,1024,512]{2,1,0:T(8,128)} fusion(f32[8,1024,1536]{2,1,0:T(8,128)} %fusion), kind=kLoop, calls=%fused_computation.14 | loop fusion | flops 8388608 | bytes 67108864 | tf_op jit(solution)/shard_map/add | solution.py:153
  969.9 21.5 %multiply_subtract_fusion = (f32[64,128,256]{2,0,1:T(8,128)}, f32[64,128,256]{2,0,1:T(8,128)}) fusion(f32[64,128,256]{2,0,1:T(8,128)} %fusion.17, f32[64,128]{0,1:T(8,128)S(1)} %copy-done.12, f32[64,128]{0,1:T(8,128)S(1)} %copy-done.9, f32[64,128,256]{2,0,1:T(8,128)} %fusion.23, f32[64,128,256]{2,0,1:T(8,128)} %fusion.19, f32[64,128,256]{2,1,0:T(8,128)S(1)} %bitcast.134), kind=kOutput, calls=%fused_computation.40 | convolution fusion | flops 1631641600 | bytes 50397184 | tf_op jit(solution)/shard_map/abm,ca->cbm/dot_general | solution.py:46
  991.5 16.3 %fusion.13 = f32[128,64,256]{2,0,1:T(8,128)S(1)} fusion(f32[64,128,256]{2,0,1:T(8,128)} %get-tuple-element.35), kind=kOutput, calls=%fused_computation.34 | convolution fusion | flops 3221454848 | bytes 16777216 | tf_op jit(solution)/shard_map/cbm,db->dcm/dot_general | solution.py:48
  1047.6 20.8 %fusion.42 = (f32[1024,1024]{0,1:T(8,128)}, f32[1024,1024]{0,1:T(8,128)}) fusion(f32[1024,1024]{0,1:T(8,128)} %mul.725, f32[1,1024,1024]{1,2,0:T(8,128)} %copy.279, f32[1024,1027]{0,1:T(8,128)} %slice.174, f32[1024,1027]{0,1:T(8,128)} %slice.172, f32[1,1024,1024]{1,2,0:T(8,128)} %copy.278), kind=kLoop, calls=%fused_computation.90 | loop fusion | flops 25165824 | bytes 54525952 | tf_op jit(solution)/shard_map/mul | solution.py:239
  1142.0 20.7 %add_bitcast_fusion.1 = (f32[1024,1024,1]{0,1,2:T(8,128)S(1)}, f32[1024,1024,1]{0,1,2:T(8,128)S(1)}) fusion(f32[1024,1024]{0,1:T(8,128)} %reshape.132, f32[1024,1024]{0,1:T(8,128)} %get-tuple-element.32, f32[1024,3]{0,1:T(4,128)S(1)} %get-tuple-element.57, f32[1024,3]{0,1:T(4,128)S(1)} %get-tuple-element.56), kind=kLoop, calls=%fused_computation.87 | loop fusion | flops 41943040 | bytes 16801792 | tf_op jit(solution)/shard_map/stack | solution.py:125
  1205.9 13.6 %fusion.12 = f32[1024,2048]{0,1:T(8,128)} fusion(f32[1024,2048]{0,1:T(8,128)} %copy.272, f32[1024,2048]{0,1:T(8,128)} %reshape.133, f32[1024,8,256]{0,2,1:T(8,128)} %copy.265), kind=kLoop, calls=%fused_computation.33 | loop fusion | flops 8388608 | bytes 33554432 | tf_op jit(solution)/shard_map/max | solution.py:249
  (144 shorter events, 411.9 us)
Async XLA Ops:
  7.2 590.7 %copy-start = (f32[128,128]{1,0:T(8,128)S(1)}, f32[128,128]{1,0:T(8,128)}, u32[]{:S(2)}) copy-start(f32[128,128]{1,0:T(8,128)} %param.15) | copy-start | bytes 196612
  16.5 5.3 copy-start.17
  16.5 119.8 %all-to-all-start = ((f32[1024,8,256]{0,2,1:T(8,128)}), f32[1024,8,256]{0,2,1:T(8,128)}, u32[]{:S(2)}, u32[]{:S(2)}) async-start(f32[1024,8,256]{0,2,1:T(8,128)} %bitcast.124), calls=%async_computation | async-start | bytes 16777216 | tf_op jit(solution)/shard_map/all_to_all | solution.py:170
  93.0 69.9 %copy-start.8 = (f32[64,128]{0,1:T(8,128)}, f32[64,128]{0,1:T(8,128)S(1)}, u32[]{:S(2)}) copy-start(f32[64,128]{0,1:T(8,128)S(1)} %get-tuple-element.65) | copy-start | bytes 98308
  181.5 17.5 %slice-start.4 = ((s8[8388608]{0:T(1024)(128)(4,1)}), s8[4194304]{0:T(1024)(128)(4,1)S(1)}, s32[]{:S(2)}) async-start(s8[8388608]{0:T(1024)(128)(4,1)} %bitcast.129), calls=%async_computation.10 | async-start | bytes 8388608
  181.5 17.5 %slice-start.5 = ((s8[8388608]{0:T(1024)(128)(4,1)}), s8[4194304]{0:T(1024)(128)(4,1)S(1)}, s32[]{:S(2)}) async-start(s8[8388608]{0:T(1024)(128)(4,1)} %bitcast.129), calls=%async_computation.11 | async-start | bytes 8388608
  351.3 19.2 %copy-start.16 = (s32[256]{0:T(256)S(1)}, s32[256]{0:T(256)}, u32[]{:S(2)}) copy-start(s32[256]{0:T(256)} %copy-done.15) | copy-start | bytes 3076
  370.5 17.2 %copy-start.2 = (f32[8192,256]{0,1:T(8,128)S(1)}, f32[8192,256]{0,1:T(8,128)}, u32[]{:S(2)}) copy-start(f32[8192,256]{0,1:T(8,128)} %get-tuple-element.37) | copy-start | bytes 25165828
  387.8 29.4 %slice-start = ((s8[8388608]{0:T(1024)(128)(4,1)}), s8[4194304]{0:T(1024)(128)(4,1)S(1)}, s32[]{:S(2)}) async-start(s8[8388608]{0:T(1024)(128)(4,1)} %bitcast.122), calls=%async_computation.6 | async-start | bytes 8388608
  402.3 14.8 %slice-start.1 = ((s8[8388608]{0:T(1024)(128)(4,1)}), s8[4194304]{0:T(1024)(128)(4,1)S(1)}, s32[]{:S(2)}) async-start(s8[8388608]{0:T(1024)(128)(4,1)} %bitcast.122), calls=%async_computation.7 | async-start | bytes 8388608
  560.9 37.0 %copy-start.13 = (f32[256,2,128]{2,1,0:T(2,128)S(1)}, f32[256,2,128]{2,1,0:T(2,128)}, u32[]{:S(2)}) copy-start(f32[256,2,128]{2,1,0:T(2,128)} %param.14) | copy-start | bytes 786436
  560.9 37.0 %copy-start.14 = (f32[256,2,128]{2,1,0:T(2,128)S(1)}, f32[256,2,128]{2,1,0:T(2,128)}, u32[]{:S(2)}) copy-start(f32[256,2,128]{2,1,0:T(2,128)} %param.12) | copy-start | bytes 786436
  568.4 28.9 %all-to-all-start.2 = ((f32[1024,2,128]{2,1,0:T(2,128)}), f32[1024,2,128]{2,1,0:T(2,128)S(1)}, u32[]{:S(2)}, u32[]{:S(2)}) async-start(f32[1024,2,128]{2,1,0:T(2,128)} %reduce_sum.36), calls=%async_computation.2 | async-start | bytes 2097152 | tf_op jit(solution)/shard_map/all_to_all | solution.py:205
  571.9 97.1 %all-gather.4.cloned.1.call-start = ((), (), s32[]{:S(2)}) async-start(), calls=%async_computation.4 | async-start | bytes 1310720 | tf_op jit(solution)/shard_map/all_gather | solution.py:217
  639.6 136.3 %all-gather.6.cloned.1.call-start = ((), (), s32[]{:S(2)}) async-start(), calls=%async_computation.5 | async-start | bytes 9437184 | tf_op jit(solution)/shard_map/all_gather | solution.py:218
  669.0 11.3 slice-start.2
  670.0 10.4 slice-start.3
  670.0 10.4 collective-permute-start
  722.2 18.0 %copy-start.11 = (s32[8192]{0:T(1024)S(1)}, s32[8192]{0:T(1024)}, u32[]{:S(2)}) copy-start(s32[8192]{0:T(1024)} %copy-done.10) | copy-start | bytes 98308
  735.9 2.0 copy-start.5
  737.9 13.2 %collective-permute-start.1 = (f32[1024,6]{0,1:T(8,128)S(1)}, f32[1024,6]{0,1:T(8,128)S(1)}, u32[]{:S(2)}, u32[]{:S(2)}) collective-permute-start(f32[1024,6]{0,1:T(8,128)S(1)} %slice.235), channel_id=1, source_target_pairs={{1,0},{2,1},{3,2},{0,3},{5,4},{6,5},{7,6},{4,7},{9,8},{10,9},{11,1... | collective-permute-start | bytes 73736 | tf_op jit(solution)/shard_map/ppermute | solution.py:27
  776.0 10.0 copy-start.3
  956.8 13.2 %copy-start.9 = (f32[64,128]{0,1:T(8,128)S(1)}, f32[64,128]{0,1:T(8,128)}, u32[]{:S(2)}) copy-start(f32[64,128]{0,1:T(8,128)} %copy-done.8) | copy-start | bytes 98308
  956.8 13.2 %copy-start.12 = (f32[64,128]{0,1:T(8,128)S(1)}, f32[64,128]{0,1:T(8,128)}, u32[]{:S(2)}) copy-start(f32[64,128]{0,1:T(8,128)} %fusion.138) | copy-start | bytes 98308
  991.5 16.3 %slice-start.6 = ((s8[8388608]{0:T(1024)(128)(4,1)}), s8[4194304]{0:T(1024)(128)(4,1)S(1)}, s32[]{:S(2)}) async-start(s8[8388608]{0:T(1024)(128)(4,1)} %bitcast.140), calls=%async_computation.12 | async-start | bytes 8388608
  991.5 16.3 %slice-start.7 = ((s8[8388608]{0:T(1024)(128)(4,1)}), s8[4194304]{0:T(1024)(128)(4,1)S(1)}, s32[]{:S(2)}) async-start(s8[8388608]{0:T(1024)(128)(4,1)} %bitcast.140), calls=%async_computation.13 | async-start | bytes 8388608
  1027.9 5.1 copy-start.4
  1028.0 161.3 %all-to-all-start.3 = ((f32[8,1024,256]{2,1,0:T(8,128)}), f32[8,1024,256]{2,1,0:T(8,128)}, u32[]{:S(2)}, u32[]{:S(2)}) async-start(f32[8,1024,256]{2,1,0:T(8,128)} %bitcast.139), calls=%async_computation.3 | async-start | bytes 16777216 | tf_op jit(solution)/shard_map/all_to_all | solution.py:232
  1099.4 10.0 collective-permute-start.2
  1123.5 18.5 %collective-permute-start.3 = (f32[2,1024,3]{1,2,0:T(4,128)S(1)}, f32[2,1024,3]{1,2,0:T(4,128)S(1)}, u32[]{:S(2)}, u32[]{:S(2)}) collective-permute-start(f32[2,1024,3]{1,2,0:T(4,128)S(1)} %pad_maximum_fusion.11), channel_id=1, source_target_pairs={{3,0},{0,1},{1,2},{2,3},{7,4},{4,5},{5,6},{6,7},{11,8},{8,9},{9,10... | collective-permute-start | bytes 73736 | tf_op jit(solution)/shard_map/ppermute | solution.py:27
  1177.4 11.0 copy-start.7
  1205.9 22.8 %copy-start.1 = (f32[128,128]{1,0:T(8,128)S(1)}, f32[128,128]{1,0:T(8,128)}, u32[]{:S(2)}) copy-start(f32[128,128]{1,0:T(8,128)} %param.15) | copy-start | bytes 196612
  (3 other events, 2.0 us)
Sparse Core Ops, SparseCore 0:
  639.8 29.2 all-gather.3
  670.9 53.6 all-gather.5

commit v2 on v1

--- a/solution.py
+++ b/solution.py
@@ -169,7 +169,8 @@
     norm_scale = 1.0 / math.sqrt(len_rows * len_cols)
     columns = lax.all_to_all(extrapolated, "vis", split_axis=1, concat_axis=0, tiled=True)
     spec_real, spec_imag = transform_axis(columns, None, -1.0, 0, False)
-    all_index = lax.all_gather(block_index, ("vis", "tile"), tiled=True)
+    all_index = lax.all_gather(block_index.astype(jnp.float32), ("vis", "tile"), tiled=True)
+    all_index = all_index.astype(jnp.int32)
     total_blocks = all_index.shape[0]
     owner = jnp.arange(total_blocks, dtype=jnp.int32) // slot_count
     per_row = slab_cols // block_width
@@ -200,10 +201,8 @@
         twisted_real, cell_sin, precision=precise
     )
     partial = jnp.stack([part_real, part_imag], axis=1)
-    partial = lax.all_to_all(partial, "vis", split_axis=0, concat_axis=0, tiled=True)
-    partial = partial.reshape((n_vis, total_blocks // n_vis) + partial.shape[1:]).sum(axis=0)
-    partial = lax.all_to_all(partial, "tile", split_axis=0, concat_axis=0, tiled=True)
-    chosen = partial.reshape((n_tile, slot_count) + partial.shape[1:]).sum(axis=0) * norm_scale
+    partial = lax.psum_scatter(partial, "vis", scatter_dimension=0, tiled=True)
+    chosen = lax.psum_scatter(partial, "tile", scatter_dimension=0, tiled=True) * norm_scale
     model = jnp.einsum("ij,csj->csi", kernel, chosen, precision=precise)
     live_mask = (jnp.arange(slot_count, dtype=jnp.int32) < live_blocks[0]).astype(jnp.float32)[
         :, None, None

time: 1250 us -> 1190 us (0.952)
  blocking collectives: 206 us -> 110 us
  waiting for transfers between devices: 53.5 us -> 124 us
  local copies, waits for them, and re-layouts: 373 us -> 342 us
    all_to_all x1 -> x0, blocking collectives: 97.4 us -> none  [on_device(): lax.all_to_all(partial, 'vis', split_axis=0, concat_axis=0, tiled=True)]
    reduce_scatter x0 -> x2, waiting for transfers between devices: none -> 95.8 us  [the longest x1 67.6 us: on_device(): partial = lax.psum_scatter(partial, 'vis', scatter_dimension=0, tiled=True)]
    another operation x1 -> x0, local copies, waits for them, and re-layouts: 31.2 us -> none  [on_device(): partial = jnp.stack([part_real, part_imag], axis=1)]
    all_to_all x1 -> x0, waiting for transfers between devices: 24.1 us -> none  [on_device(): lax.all_to_all(partial, 'tile', split_axis=0, concat_axis=0, tiled=True)]
  transfers between devices with their start and end apart: 9 -> 10, of which waited for: 2 -> 3; matrix products, arithmetic and copies ran while one was open for 24% -> 26% of each run, Pallas kernels for 0% -> 0%
where the time goes in v2:
time: 1190 us; the launch traced here: 1170 us
  matrix products  356 us (30%)
  local copies, waits for them, and re-layouts  342 us (29%)
  other arithmetic  208 us (17%)
  waiting for transfers between devices  124 us (10%)
  blocking collectives  110 us (9%)
  between operations  16.5 us (1%)
  starting transfers between devices  15.6 us (1%)
    all_gather x1, blocking collectives, on_device(): lax.all_gather(block_index.astype(jnp.float32), ('vis', 'tile'), tiled=True)  70.9 us
    dot_general x4, matrix products, complex_einsum(): real_part = jnp.einsum(form, left_real, table_cos, precision=precise)  68.6 us
    reduce_scatter x1, waiting for transfers between devices, on_device(): partial = lax.psum_scatter(partial, 'vis', scatter_dimension=0, tiled=True)  67.6 us
    slice x4, local copies, waits for them, and re-layouts, analyse_local(): lax.slice_in_dim(extended, parity, extended.shape[1], 2, 1)  58.1 us
    unnamed x59, local copies, waits for them, and re-layouts  52 us
    dot_general x3, matrix products, complex_einsum(): imag_part = jnp.einsum(form, left_real, table_sin, precision=precise)  46 us
    gather x2, local copies, waits for them, and re-layouts, on_device(): picked_real = jnp.take(spec_real, row_of, axis=0)  43.7 us
    gather x2, local copies, waits for them, and re-layouts, on_device(): picked_imag = jnp.take(spec_imag, row_of, axis=0)  43.7 us
  transfers between devices with their start and end apart: 10, of which 3 were waited for; matrix products, arithmetic and copies ran while one was open for 26% of the time, Pallas kernels for 0%

profile of v2, /device:TPU:0, one launch (start us, length us, event | category | flops | bytes accessed | tf_op | source)
XLA Modules:
  0.0 1172.3 jit_solution(11013575199814025659)
XLA Ops:
  21.9 70.9 %all-gather = f32[32,1,256]{2,1,0:T(1,128)S(1)} all-gather(f32[1,1,256]{2,1,0:T(1,128)S(1)} %bitcast.142), channel_id=1, replica_groups=mesh['vis'=8,'tile'=4] {'vis','tile'}, dimensions={0}, use_global_device_ids=true | all-gather | bytes 33792 | tf_op jit(solution)/shard_map/all_gather | solution.py:172
  94.3 19.4 %fusion.63 = f32[8192,1536]{0,1:T(8,128)} fusion(s32[8192]{0:T(1024)S(1)} %fusion.125, bf16[64,512]{1,0:T(8,128)(2,1)S(1)} %get-tuple-element.46, bf16[64,512]{1,0:T(8,128)(2,1)S(1)} %get-tuple-element.45, bf16[64,512]{1,0:T(8,128)(2,1)S(1)} %get-tuple-element.44), kind=kOutput, calls=%fused_computation.120 | convolution fusion | flops 1611726848 | bytes 50561024 | tf_op jit(solution)/shard_map/dot_general | solution.py:142
  113.6 22.7 %slice_add_fusion.2 = f32[8192,512]{0,1:T(8,128)} fusion(f32[8192,1536]{0,1:T(8,128)} %fusion.63), kind=kLoop, calls=%fused_computation.16 | loop fusion | flops 8388608 | bytes 67108864 | tf_op jit(solution)/shard_map/add | solution.py:143
  145.5 17.6 %fusion.33 = f32[64,128,256]{2,0,1:T(8,128)} fusion(f32[64,128,256]{2,1,0:T(8,128)} %bitcast.125), kind=kOutput, calls=%fused_computation.66 | convolution fusion | flops 1610670080 | bytes 16777216 | tf_op jit(solution)/shard_map/abm,ca->cbm/dot_general | solution.py:46
  163.0 18.5 %multiply_subtract_fusion.3 = (f32[64,128,256]{2,0,1:T(8,128)S(1)}, f32[64,128,256]{2,0,1:T(8,128)}) fusion(f32[64,128,256]{2,0,1:T(8,128)} %fusion.33, f32[64,128]{0,1:T(8,128)S(1)} %get-tuple-element.55, f32[64,128]{0,1:T(8,128)S(1)} %get-tuple-element.56, f32[64,128,256]{2,1,0:T(8,128)} %bitcast.126), kind=kOutput, calls=%fused_computation.48 | convolution fusion | flops 1627451392 | bytes 33619968 | tf_op jit(solution)/shard_map/abm,ca->cbm/dot_general | solution.py:51
  181.6 17.5 %fusion.27 = f32[128,64,256]{2,0,1:T(8,128)} fusion(f32[64,128,256]{2,0,1:T(8,128)} %get-tuple-element.32), kind=kOutput, calls=%fused_computation.60 | convolution fusion | flops 3221454848 | bytes 16777216 | tf_op jit(solution)/shard_map/cbm,db->dcm/dot_general | solution.py:53
  199.1 13.5 %fusion.25 = f32[128,64,256]{2,0,1:T(8,128)} fusion(f32[64,128,256]{2,0,1:T(8,128)S(1)} %bitcast.128), kind=kOutput, calls=%fused_computation.58 | convolution fusion | flops 3221471232 | bytes 16777216 | tf_op jit(solution)/shard_map/cbm,db->dcm/dot_general | solution.py:48
  212.7 14.3 %fusion.45 = f32[128,64,256]{2,0,1:T(8,128)S(1)} fusion(f32[128,64,256]{2,0,1:T(8,128)} %fusion.27, f32[64,128,256]{2,0,1:T(8,128)S(1)} %get-tuple-element.31), kind=kOutput, calls=%fused_computation.94 | convolution fusion | flops 3223568384 | bytes 25165824 | tf_op jit(solution)/shard_map/cbm,db->dcm/dot_general | solution.py:51
  235.2 17.4 %subtract_add_fusion.1 = f32[128,64,256]{2,0,1:T(8,128)} fusion(f32[128,64,256]{2,0,1:T(8,128)} %fusion.25, f32[128,64,256]{2,0,1:T(8,128)S(1)} %fusion.45, f32[64,128,256]{2,0,1:T(8,128)S(1)} %get-tuple-element.31), kind=kOutput, calls=%fused_computation.46 | convolution fusion | flops 3227746304 | bytes 33554432 | tf_op jit(solution)/shard_map/cbm,db->dcm/dot_general | solution.py:46
  264.2 34.8 %gather_fusion = f32[8192,256]{1,0:T(8,128)} fusion(f32[8192,256]{1,0:T(8,128)} %bitcast.119, s32[8192]{0:T(1024)S(1)} %broadcast_clamp_fusion), kind=kCustom, calls=%fused_computation.clone | custom fusion | bytes 16809984 | tf_op jit(solution)/shard_map/jit(_take)/gather | solution.py:193
  307.9 34.8 %gather_fusion.1 = f32[8192,256]{1,0:T(8,128)} fusion(f32[8192,256]{1,0:T(8,128)} %bitcast.118, s32[8192]{0:T(1024)S(1)} %broadcast_clamp_fusion), kind=kCustom, calls=%fused_computation.1.clone | custom fusion | bytes 16809984 | tf_op jit(solution)/shard_map/jit(_take)/gather | solution.py:194
  351.5 19.2 %multiply_add_fusion.2 = (f32[8192,256]{0,1:T(8,128)}, f32[8192,256]{0,1:T(8,128)}) fusion(f32[8192,256]{0,1:T(8,128)} %copy.135, f32[8192,256]{0,1:T(8,128)} %copy.133, f32[8192,512]{0,1:T(8,128)} %slice_add_fusion.2, pred[8192]{0:T(1024)(128)(4,1)S(1)} %get-tuple-element.21), kind=kLoop, calls=%fused_computation.45 | loop fusion | flops 16777216 | bytes 50339840 | tf_op jit(solution)/shard_map/add | solution.py:195
  370.8 17.2 %fusion.105 = f32[8192,128]{1,0:T(8,128)S(1)} fusion(f32[8192,256]{0,1:T(8,128)} %get-tuple-element.27, s32[256]{0:T(256)S(1)} %copy-done.16), kind=kOutput, calls=%fused_computation.183 | convolution fusion | flops 3221684224 | bytes 12583936 | tf_op jit(solution)/shard_map/dot_general | solution.py:197
  388.0 14.6 %fusion.103 = f32[8192,128]{1,0:T(8,128)S(1)} fusion(f32[8192,256]{0,1:T(8,128)S(1)} %copy-done.2, s32[256]{0:T(256)S(1)} %copy-done.16), kind=kOutput, calls=%fused_computation.182 | convolution fusion | flops 3221684224 | bytes 12583936 | tf_op jit(solution)/shard_map/dot_general | solution.py:200
  402.6 14.8 %fusion.9 = f32[8192,1,128]{2,0,1:T(8,128)S(1)} fusion(f32[8192,128]{1,0:T(8,128)S(1)} %fusion.105, f32[8192,256]{0,1:T(8,128)S(1)} %copy-done.2, s32[256]{0:T(256)S(1)} %copy-done.16), kind=kOutput, calls=%fused_computation.25 | convolution fusion | flops 3222732800 | bytes 16778240 | tf_op jit(solution)/shard_map/dot_general | solution.py:197
  417.4 14.6 %fusion.8 = f32[8192,1,128]{2,0,1:T(8,128)S(1)} fusion(f32[8192,128]{1,0:T(8,128)S(1)} %fusion.103, f32[8192,256]{0,1:T(8,128)S(1)} %bitcast.121, s32[256]{0:T(256)S(1)} %copy-done.16), kind=kOutput, calls=%fused_computation.23 | convolution fusion | flops 3222732800 | bytes 16778240 | tf_op jit(solution)/shard_map/dot_general | solution.py:200
  436.0 67.6 %reduce-scatter.3.cloned.1.call-done = f32[1024,2,128]{2,0,1:T(8,128)} async-done(((f32[8192,2,128]{2,0,1:T(8,128)}), f32[1024,2,128]{2,0,1:T(8,128)}) %reduce-scatter.3.cloned.1.call-update) | async-done | bytes 1048592 | tf_op jit(solution)/shard_map/reduce_scatter | solution.py:204
  504.9 28.3 %reduce-scatter.5.cloned.1.call-done = f32[256,2,128]{2,0,1:T(8,128)} async-done(((f32[1024,2,128]{2,0,1:T(8,128)}), f32[256,2,128]{2,0,1:T(8,128)}) %reduce-scatter.5.cloned.1.call-update) | async-done | bytes 262160 | tf_op jit(solution)/shard_map/reduce_scatter | solution.py:205
  535.1 38.9 %all-reduce = (f32[]{:T(128)}, f32[]{:T(128)}) all-reduce(f32[]{:T(128)} %fusion.169, f32[]{:T(128)} %get-tuple-element.51), channel_id=1, replica_groups=mesh['vis'=8,'tile'=4] {'vis','tile'}, use_global_device_ids=true, to_apply=%region_3.5 | all-reduce | flops 2 | bytes 16 | tf_op jit(solution)/shard_map/psum | solution.py:211
  577.4 28.1 %all-gather.4.cloned.1.call-done = f32[1024,2,128]{2,0,1:T(8,128)} async-done(((f32[256,2,128]{2,0,1:T(8,128)}), f32[1024,2,128]{2,0,1:T(8,128)}) %all-gather.4.cloned.1.call-update) | async-done | bytes 1048592 | tf_op jit(solution)/shard_map/all_gather | solution.py:216
  620.9 19.1 %slice.172 = f32[1024,1027]{0,1:T(8,128)} slice(f32[1024,2054]{0,1:T(8,128)} %pad_maximum_fusion.1), slice={[0:1024:1], [0:2054:2]} | slice | bytes 8413184 | tf_op jit(solution)/shard_map/slice | solution.py:102
  640.0 18.9 %slice.174 = f32[1024,1027]{0,1:T(8,128)} slice(f32[1024,2054]{0,1:T(8,128)} %pad_maximum_fusion.1), slice={[0:1024:1], [1:2054:2]} | slice | bytes 8413184 | tf_op jit(solution)/shard_map/slice | solution.py:102
  658.9 13.7 %multiply_add_fusion.5 = f32[1024,1024]{0,1:T(8,128)S(1)} fusion(f32[1024,1027]{0,1:T(8,128)} %slice.174, f32[1024,1027]{0,1:T(8,128)} %slice.172), kind=kLoop, calls=%fused_computation.91 | loop fusion | flops 15728640 | bytes 37748736 | tf_op jit(solution)/shard_map/add | solution.py:108
  743.7 22.0 %multiply_subtract_fusion.1 = (f32[8192,256]{0,1:T(8,128)}, f32[8192,256]{0,1:T(8,128)}) fusion(f32[8192,256]{0,1:T(8,128)} %convolution_subtract_fusion, f32[8192,512]{0,1:T(8,128)} %slice_add_fusion.2, f32[8192,256]{0,1:T(8,128)} %fusion.43, s32[256]{0:T(256)S(1)} %copy-done.16, f32[8192,2,128]{2,0,1:T(8,128)} %all-gather.6.cloned.1.call-done), kind=kOutput, calls=%fused_computation.43 | convolution fusion | flops 3236364288 | bytes 54526976 | tf_op jit(solution)/shard_map/dot_general | solution.py:221
  777.4 17.4 %copy.157 = f32[8192,512]{1,0:T(8,128)} copy(f32[8192,512]{0,1:T(8,128)} %pad_maximum_fusion) | data formatting | bytes 33554432 | tf_op jit(solution)/shard_map/reshape | solution.py:227
  805.2 31.5 %fusion = f32[8,1024,1536]{2,1,0:T(8,128)} fusion(bf16[8,1024,512]{2,1,0:T(8,128)(2,1)S(1)} %get-tuple-element.36, bf16[8,1024,512]{2,1,0:T(8,128)(2,1)} %get-tuple-element.37, bf16[8,1024,512]{2,1,0:T(8,128)(2,1)S(1)} %get-tuple-element.35, s32[8,1024]{1,0:T(8,128)S(1)} %eq.45), kind=kOutput, calls=%fused_computation.3 | convolution fusion | flops 25853689856 | bytes 75530240 | tf_op jit(solution)/shard_map/gkb,gbc->gkc/dot_general | solution.py:152
  836.7 23.9 %slice_add_fusion = f32[8,1024,512]{2,1,0:T(8,128)} fusion(f32[8,1024,1536]{2,1,0:T(8,128)} %fusion), kind=kLoop, calls=%fused_computation.14 | loop fusion | flops 8388608 | bytes 67108864 | tf_op jit(solution)/shard_map/add | solution.py:153
  906.8 21.8 %multiply_subtract_fusion = (f32[64,128,256]{2,0,1:T(8,128)}, f32[64,128,256]{2,0,1:T(8,128)}) fusion(f32[64,128,256]{2,0,1:T(8,128)} %fusion.17, f32[64,128]{0,1:T(8,128)S(1)} %copy-done.12, f32[64,128]{0,1:T(8,128)S(1)} %copy-done.9, f32[64,128,256]{2,0,1:T(8,128)} %fusion.23, f32[64,128,256]{2,0,1:T(8,128)} %fusion.19, f32[64,128,256]{2,1,0:T(8,128)S(1)} %bitcast.132), kind=kOutput, calls=%fused_computation.40 | convolution fusion | flops 1631641600 | bytes 50397184 | tf_op jit(solution)/shard_map/abm,ca->cbm/dot_general | solution.py:46
  928.6 16.1 %fusion.13 = f32[128,64,256]{2,0,1:T(8,128)S(1)} fusion(f32[64,128,256]{2,0,1:T(8,128)} %get-tuple-element.26), kind=kOutput, calls=%fused_computation.34 | convolution fusion | flops 3221454848 | bytes 16777216 | tf_op jit(solution)/shard_map/cbm,db->dcm/dot_general | solution.py:48
  984.5 20.8 %fusion.42 = (f32[1024,1024]{0,1:T(8,128)}, f32[1024,1024]{0,1:T(8,128)}) fusion(f32[1024,1024]{0,1:T(8,128)} %mul.725, f32[1,1024,1024]{1,2,0:T(8,128)} %copy.159, f32[1024,1027]{0,1:T(8,128)} %slice.174, f32[1024,1027]{0,1:T(8,128)} %slice.172, f32[1,1024,1024]{1,2,0:T(8,128)} %copy.158), kind=kLoop, calls=%fused_computation.90 | loop fusion | flops 25165824 | bytes 54525952 | tf_op jit(solution)/shard_map/mul | solution.py:238
  1079.1 20.7 %add_bitcast_fusion.1 = (f32[1024,1024,1]{0,1,2:T(8,128)S(1)}, f32[1024,1024,1]{0,1,2:T(8,128)S(1)}) fusion(f32[1024,1024]{0,1:T(8,128)} %reshape.124, f32[1024,1024]{0,1:T(8,128)} %get-tuple-element.23, f32[1024,3]{0,1:T(4,128)S(1)} %get-tuple-element.48, f32[1024,3]{0,1:T(4,128)S(1)} %get-tuple-element.47), kind=kLoop, calls=%fused_computation.87 | loop fusion | flops 41943040 | bytes 16801792 | tf_op jit(solution)/shard_map/stack | solution.py:125
  1142.9 13.6 %fusion.12 = f32[1024,2048]{0,1:T(8,128)} fusion(f32[1024,2048]{0,1:T(8,128)} %copy.153, f32[1024,2048]{0,1:T(8,128)} %reshape.125, f32[1024,8,256]{0,2,1:T(8,128)} %copy.146), kind=kLoop, calls=%fused_computation.33 | loop fusion | flops 8388608 | bytes 33554432 | tf_op jit(solution)/shard_map/max | solution.py:248
  (146 shorter events, 391.8 us)
Async XLA Ops:
  7.2 526.0 %copy-start = (f32[128,128]{1,0:T(8,128)S(1)}, f32[128,128]{1,0:T(8,128)}, u32[]{:S(2)}) copy-start(f32[128,128]{1,0:T(8,128)} %param.15) | copy-start | bytes 196612
  16.5 5.4 copy-start.17
  16.5 119.9 %all-to-all-start = ((f32[1024,8,256]{0,2,1:T(8,128)}), f32[1024,8,256]{0,2,1:T(8,128)}, u32[]{:S(2)}, u32[]{:S(2)}) async-start(f32[1024,8,256]{0,2,1:T(8,128)} %bitcast.122), calls=%async_computation | async-start | bytes 16777216 | tf_op jit(solution)/shard_map/all_to_all | solution.py:170
  21.8 481.8 %reduce-scatter.3.cloned.1.call-start = ((), (), s32[]{:S(2)}) async-start(), calls=%async_computation.4 | async-start | bytes 9437184 | tf_op jit(solution)/shard_map/reduce_scatter | solution.py:204
  93.1 69.9 %copy-start.8 = (f32[64,128]{0,1:T(8,128)}, f32[64,128]{0,1:T(8,128)S(1)}, u32[]{:S(2)}) copy-start(f32[64,128]{0,1:T(8,128)S(1)} %get-tuple-element.56) | copy-start | bytes 98308
  181.6 17.5 %slice-start.4 = ((s8[8388608]{0:T(1024)(128)(4,1)}), s8[4194304]{0:T(1024)(128)(4,1)S(1)}, s32[]{:S(2)}) async-start(s8[8388608]{0:T(1024)(128)(4,1)} %bitcast.127), calls=%async_computation.12 | async-start | bytes 8388608
  181.6 17.6 %slice-start.5 = ((s8[8388608]{0:T(1024)(128)(4,1)}), s8[4194304]{0:T(1024)(128)(4,1)S(1)}, s32[]{:S(2)}) async-start(s8[8388608]{0:T(1024)(128)(4,1)} %bitcast.127), calls=%async_computation.13 | async-start | bytes 8388608
  351.5 19.2 %copy-start.16 = (s32[256]{0:T(256)S(1)}, s32[256]{0:T(256)}, u32[]{:S(2)}) copy-start(s32[256]{0:T(256)} %copy-done.15) | copy-start | bytes 3076
  370.8 17.2 %copy-start.2 = (f32[8192,256]{0,1:T(8,128)S(1)}, f32[8192,256]{0,1:T(8,128)}, u32[]{:S(2)}) copy-start(f32[8192,256]{0,1:T(8,128)} %get-tuple-element.28) | copy-start | bytes 25165828
  388.0 29.4 %slice-start = ((s8[8388608]{0:T(1024)(128)(4,1)}), s8[4194304]{0:T(1024)(128)(4,1)S(1)}, s32[]{:S(2)}) async-start(s8[8388608]{0:T(1024)(128)(4,1)} %bitcast.120), calls=%async_computation.8 | async-start | bytes 8388608
  402.6 14.8 %slice-start.1 = ((s8[8388608]{0:T(1024)(128)(4,1)}), s8[4194304]{0:T(1024)(128)(4,1)S(1)}, s32[]{:S(2)}) async-start(s8[8388608]{0:T(1024)(128)(4,1)} %bitcast.120), calls=%async_computation.9 | async-start | bytes 8388608
  436.0 97.2 %copy-start.13 = (f32[256,2,128]{2,1,0:T(2,128)S(1)}, f32[256,2,128]{2,1,0:T(2,128)}, u32[]{:S(2)}) copy-start(f32[256,2,128]{2,1,0:T(2,128)} %param.14) | copy-start | bytes 786436
  436.0 97.2 %copy-start.14 = (f32[256,2,128]{2,1,0:T(2,128)S(1)}, f32[256,2,128]{2,1,0:T(2,128)}, u32[]{:S(2)}) copy-start(f32[256,2,128]{2,1,0:T(2,128)} %param.12) | copy-start | bytes 786436
  436.0 97.2 %reduce-scatter.5.cloned.1.call-start = ((), (), s32[]{:S(2)}) async-start(), calls=%async_computation.5 | async-start | bytes 1310720 | tf_op jit(solution)/shard_map/reduce_scatter | solution.py:205
  503.6 101.8 %all-gather.4.cloned.1.call-start = ((), (), s32[]{:S(2)}) async-start(), calls=%async_computation.6 | async-start | bytes 1310720 | tf_op jit(solution)/shard_map/all_gather | solution.py:216
  577.3 135.5 %all-gather.6.cloned.1.call-start = ((), (), s32[]{:S(2)}) async-start(), calls=%async_computation.7 | async-start | bytes 9437184 | tf_op jit(solution)/shard_map/all_gather | solution.py:217
  605.5 11.2 slice-start.2
  606.4 10.3 slice-start.3
  606.4 10.3 collective-permute-start
  658.9 18.2 %copy-start.11 = (s32[8192]{0:T(1024)S(1)}, s32[8192]{0:T(1024)}, u32[]{:S(2)}) copy-start(s32[8192]{0:T(1024)} %copy-done.10) | copy-start | bytes 98308
  674.6 13.3 %collective-permute-start.1 = (f32[1024,6]{0,1:T(8,128)S(1)}, f32[1024,6]{0,1:T(8,128)S(1)}, u32[]{:S(2)}, u32[]{:S(2)}) collective-permute-start(f32[1024,6]{0,1:T(8,128)S(1)} %slice.235), channel_id=1, source_target_pairs={{1,0},{2,1},{3,2},{0,3},{5,4},{6,5},{7,6},{4,7},{9,8},{10,9},{11,1... | collective-permute-start | bytes 73736 | tf_op jit(solution)/shard_map/ppermute | solution.py:27
  712.8 10.0 copy-start.3
  893.6 13.2 %copy-start.9 = (f32[64,128]{0,1:T(8,128)S(1)}, f32[64,128]{0,1:T(8,128)}, u32[]{:S(2)}) copy-start(f32[64,128]{0,1:T(8,128)} %copy-done.8) | copy-start | bytes 98308
  893.6 13.2 %copy-start.12 = (f32[64,128]{0,1:T(8,128)S(1)}, f32[64,128]{0,1:T(8,128)}, u32[]{:S(2)}) copy-start(f32[64,128]{0,1:T(8,128)} %fusion.139) | copy-start | bytes 98308
  928.6 16.1 %slice-start.6 = ((s8[8388608]{0:T(1024)(128)(4,1)}), s8[4194304]{0:T(1024)(128)(4,1)S(1)}, s32[]{:S(2)}) async-start(s8[8388608]{0:T(1024)(128)(4,1)} %bitcast.138), calls=%async_computation.14 | async-start | bytes 8388608
  928.6 16.1 %slice-start.7 = ((s8[8388608]{0:T(1024)(128)(4,1)}), s8[4194304]{0:T(1024)(128)(4,1)S(1)}, s32[]{:S(2)}) async-start(s8[8388608]{0:T(1024)(128)(4,1)} %bitcast.138), calls=%async_computation.15 | async-start | bytes 8388608
  964.8 5.1 copy-start.4
  964.8 161.4 %all-to-all-start.1 = ((f32[8,1024,256]{2,1,0:T(8,128)}), f32[8,1024,256]{2,1,0:T(8,128)}, u32[]{:S(2)}, u32[]{:S(2)}) async-start(f32[8,1024,256]{2,1,0:T(8,128)} %bitcast.137), calls=%async_computation.3 | async-start | bytes 16777216 | tf_op jit(solution)/shard_map/all_to_all | solution.py:231
  1036.4 10.2 collective-permute-start.2
  1060.6 18.4 %collective-permute-start.3 = (f32[2,1024,3]{1,2,0:T(4,128)S(1)}, f32[2,1024,3]{1,2,0:T(4,128)S(1)}, u32[]{:S(2)}, u32[]{:S(2)}) collective-permute-start(f32[2,1024,3]{1,2,0:T(4,128)S(1)} %pad_maximum_fusion.11), channel_id=1, source_target_pairs={{3,0},{0,1},{1,2},{2,3},{7,4},{4,5},{5,6},{6,7},{11,8},{8,9},{9,10... | collective-permute-start | bytes 73736 | tf_op jit(solution)/shard_map/ppermute | solution.py:27
  1114.4 11.0 copy-start.7
  1142.9 22.7 %copy-start.1 = (f32[128,128]{1,0:T(8,128)S(1)}, f32[128,128]{1,0:T(8,128)}, u32[]{:S(2)}) copy-start(f32[128,128]{1,0:T(8,128)} %param.15) | copy-start | bytes 196612
  (4 other events, 4.1 us)
Sparse Core Ops, SparseCore 0:
  436.1 67.4 reduce-scatter.2
  505.9 27.2 reduce-scatter.4
  577.5 27.9 all-gather.3
  607.2 53.6 all-gather.5

commit v3 on v2

--- a/solution.py
+++ b/solution.py
@@ -203,6 +203,24 @@
     partial = jnp.stack([part_real, part_imag], axis=1)
     partial = lax.psum_scatter(partial, "vis", scatter_dimension=0, tiled=True)
     chosen = lax.psum_scatter(partial, "tile", scatter_dimension=0, tiled=True) * norm_scale
+    approx_one, detail_one = analyse_local(extrapolated)
+    approx_two, detail_two = analyse_local(approx_one)
+    child = tree_dual[0] + 0.5 * detail_one
+    parent = tree_dual[1] + 0.5 * jnp.repeat(detail_two, 2, axis=1)
+    factor = 1.0 / jnp.maximum(jnp.sqrt(child * child + parent * parent), 1.0)
+    child_next = child * factor
+    parent_next = parent * factor
+    parent_sum = parent_next[:, 0::2] + parent_next[:, 1::2]
+    parent_tail = shifted(parent_sum[:, -3:], "tile", 1)
+    level_one = upsample(None, jnp.concatenate([parent_tail, parent_sum], axis=1))
+    both_tails = shifted(jnp.stack([level_one[:, -3:], child_next[:, -3:]]), "tile", 1)
+    prior_term = upsample(
+        jnp.concatenate([both_tails[0], level_one], axis=1),
+        jnp.concatenate([both_tails[1], child_next], axis=1),
+    )
+    chosen, child_next, parent_next, prior_term = lax.optimization_barrier(
+        (chosen, child_next, parent_next, prior_term)
+    )
     model = jnp.einsum("ij,csj->csi", kernel, chosen, precision=precise)
     live_mask = (jnp.arange(slot_count, dtype=jnp.int32) < live_blocks[0]).astype(jnp.float32)[
         :, None, None
@@ -229,21 +247,6 @@
     pixel_real, unused_part = transform_axis(gridded[:, :chunk], gridded[:, chunk:], 1.0, 0, True)
     data_term = (
         lax.all_to_all(pixel_real, "vis", split_axis=0, concat_axis=1, tiled=True) * norm_scale
-    )
-    approx_one, detail_one = analyse_local(extrapolated)
-    approx_two, detail_two = analyse_local(approx_one)
-    child = tree_dual[0] + 0.5 * detail_one
-    parent = tree_dual[1] + 0.5 * jnp.repeat(detail_two, 2, axis=1)
-    factor = 1.0 / jnp.maximum(jnp.sqrt(child * child + parent * parent), 1.0)
-    child_next = child * factor
-    parent_next = parent * factor
-    parent_sum = parent_next[:, 0::2] + parent_next[:, 1::2]
-    parent_tail = shifted(parent_sum[:, -3:], "tile", 1)
-    level_one = upsample(None, jnp.concatenate([parent_tail, parent_sum], axis=1))
-    both_tails = shifted(jnp.stack([level_one[:, -3:], child_next[:, -3:]]), "tile", 1)
-    prior_term = upsample(
-        jnp.concatenate([both_tails[0], level_one], axis=1),
-        jnp.concatenate([both_tails[1], child_next], axis=1),
     )
     image_next = jnp.maximum(image - 0.5 * (data_term + prior_term), 0.0)
     return (image_next, vis_next, jnp.stack([child_next, parent_next]))

time: 1190 us -> 1220 us (1.025)
  waiting for transfers between devices: 124 us -> 160 us
    reduce_scatter x1, waiting for transfers between devices: 67.6 us -> 0.01 us  [on_device(): partial = lax.psum_scatter(partial, 'vis', scatter_dimension=0, tiled=True)]
    all_to_all x1, waiting for transfers between devices: 0.01 us -> 66.7 us  [on_device(): lax.all_to_all(pixel_real, 'vis', split_axis=0, concat_axis=1, tiled=True)]
    all_gather x1, waiting for transfers between devices: 0.01 us -> 55.1 us  [on_device(): every = lax.all_gather(every, 'vis', tiled=True)]
    reduce_scatter x1, waiting for transfers between devices: 28.3 us -> 0.01 us  [on_device(): lax.psum_scatter(partial, 'tile', scatter_dimension=0, tiled=True)]
    mul x1, other arithmetic: 20.8 us -> 7.31 us  [on_device(): child_next = child * factor]
    unnamed x59 -> x53, local copies, waits for them, and re-layouts: 52 us -> 50.2 us
  transfers between devices with their start and end apart: 10 -> 10, of which waited for: 3 -> 5; matrix products, arithmetic and copies ran while one was open for 26% -> 25% of each run, Pallas kernels for 0% -> 0%
where the time goes in v3:
time: 1220 us; the launch traced here: 1200 us
  matrix products  355 us (29%)
  local copies, waits for them, and re-layouts  338 us (28%)
  other arithmetic  212 us (17%)
  waiting for transfers between devices  160 us (13%)
  blocking collectives  108 us (9%)
  between operations  16.6 us (1%)
  starting transfers between devices  12.9 us (1%)
    all_gather x1, blocking collectives, on_device(): lax.all_gather(block_index.astype(jnp.float32), ('vis', 'tile'), tiled=True)  70.9 us
    dot_general x4, matrix products, complex_einsum(): real_part = jnp.einsum(form, left_real, table_cos, precision=precise)  68.3 us
    all_to_all x1, waiting for transfers between devices, on_device(): lax.all_to_all(pixel_real, 'vis', split_axis=0, concat_axis=1, tiled=True)  66.7 us
    slice x4, local copies, waits for them, and re-layouts, analyse_local(): lax.slice_in_dim(extended, parity, extended.shape[1], 2, 1)  57 us
    all_gather x1, waiting for transfers between devices, on_device(): every = lax.all_gather(every, 'vis', tiled=True)  55.1 us
    unnamed x53, local copies, waits for them, and re-layouts  50.2 us
    dot_general x3, matrix products, complex_einsum(): imag_part = jnp.einsum(form, left_real, table_sin, precision=precise)  46 us
    gather x2, local copies, waits for them, and re-layouts, on_device(): picked_real = jnp.take(spec_real, row_of, axis=0)  43.8 us
  transfers between devices with their start and end apart: 10, of which 5 were waited for; matrix products, arithmetic and copies ran while one was open for 25% of the time, Pallas kernels for 0%

profile of v3, /device:TPU:0, one launch (start us, length us, event | category | flops | bytes accessed | tf_op | source)
XLA Modules:
  0.0 1201.7 jit_solution(18234446821504876460)
XLA Ops:
  21.9 70.9 %all-gather = f32[32,1,256]{2,1,0:T(1,128)S(1)} all-gather(f32[1,1,256]{2,1,0:T(1,128)S(1)} %bitcast.141), channel_id=1, replica_groups=mesh['vis'=8,'tile'=4] {'vis','tile'}, dimensions={0}, use_global_device_ids=true | all-gather | bytes 33792 | tf_op jit(solution)/shard_map/all_gather | solution.py:172
  94.3 19.4 %fusion.63 = f32[8192,1536]{0,1:T(8,128)} fusion(s32[8192]{0:T(1024)S(1)} %fusion.123, bf16[64,512]{1,0:T(8,128)(2,1)S(1)} %get-tuple-element.54, bf16[64,512]{1,0:T(8,128)(2,1)S(1)} %get-tuple-element.53, bf16[64,512]{1,0:T(8,128)(2,1)S(1)} %get-tuple-element.52), kind=kOutput, calls=%fused_computation.120 | convolution fusion | flops 1611726848 | bytes 50561024 | tf_op jit(solution)/shard_map/dot_general | solution.py:142
  113.6 22.7 %slice_add_fusion.2 = f32[8192,512]{0,1:T(8,128)} fusion(f32[8192,1536]{0,1:T(8,128)} %fusion.63), kind=kLoop, calls=%fused_computation.16 | loop fusion | flops 8388608 | bytes 67108864 | tf_op jit(solution)/shard_map/add | solution.py:143
  145.5 17.5 %fusion.33 = f32[64,128,256]{2,0,1:T(8,128)} fusion(f32[64,128,256]{2,1,0:T(8,128)} %bitcast.124), kind=kOutput, calls=%fused_computation.66 | convolution fusion | flops 1610670080 | bytes 16777216 | tf_op jit(solution)/shard_map/abm,ca->cbm/dot_general | solution.py:46
  163.0 18.6 %multiply_subtract_fusion.3 = (f32[64,128,256]{2,0,1:T(8,128)S(1)}, f32[64,128,256]{2,0,1:T(8,128)}) fusion(f32[64,128,256]{2,0,1:T(8,128)} %fusion.33, f32[64,128]{0,1:T(8,128)S(1)} %get-tuple-element.61, f32[64,128]{0,1:T(8,128)S(1)} %get-tuple-element.62, f32[64,128,256]{2,1,0:T(8,128)} %bitcast.125), kind=kOutput, calls=%fused_computation.48 | convolution fusion | flops 1627451392 | bytes 33619968 | tf_op jit(solution)/shard_map/abm,ca->cbm/dot_general | solution.py:51
  181.6 17.5 %fusion.27 = f32[128,64,256]{2,0,1:T(8,128)} fusion(f32[64,128,256]{2,0,1:T(8,128)} %get-tuple-element.40), kind=kOutput, calls=%fused_computation.60 | convolution fusion | flops 3221454848 | bytes 16777216 | tf_op jit(solution)/shard_map/cbm,db->dcm/dot_general | solution.py:53
  199.1 13.5 %fusion.25 = f32[128,64,256]{2,0,1:T(8,128)} fusion(f32[64,128,256]{2,0,1:T(8,128)S(1)} %bitcast.127), kind=kOutput, calls=%fused_computation.58 | convolution fusion | flops 3221471232 | bytes 16777216 | tf_op jit(solution)/shard_map/cbm,db->dcm/dot_general | solution.py:48
  212.6 14.3 %fusion.45 = f32[128,64,256]{2,0,1:T(8,128)S(1)} fusion(f32[128,64,256]{2,0,1:T(8,128)} %fusion.27, f32[64,128,256]{2,0,1:T(8,128)S(1)} %get-tuple-element.39), kind=kOutput, calls=%fused_computation.94 | convolution fusion | flops 3223568384 | bytes 25165824 | tf_op jit(solution)/shard_map/cbm,db->dcm/dot_general | solution.py:51
  235.2 17.4 %subtract_add_fusion.1 = f32[128,64,256]{2,0,1:T(8,128)} fusion(f32[128,64,256]{2,0,1:T(8,128)} %fusion.25, f32[128,64,256]{2,0,1:T(8,128)S(1)} %fusion.45, f32[64,128,256]{2,0,1:T(8,128)S(1)} %get-tuple-element.39), kind=kOutput, calls=%fused_computation.46 | convolution fusion | flops 3227746304 | bytes 33554432 | tf_op jit(solution)/shard_map/cbm,db->dcm/dot_general | solution.py:46
  264.1 34.9 %gather_fusion = f32[8192,256]{1,0:T(8,128)} fusion(f32[8192,256]{1,0:T(8,128)} %bitcast.120, s32[8192]{0:T(1024)S(1)} %broadcast_clamp_fusion), kind=kCustom, calls=%fused_computation.clone | custom fusion | bytes 16809984 | tf_op jit(solution)/shard_map/jit(_take)/gather | solution.py:193
  307.9 34.9 %gather_fusion.1 = f32[8192,256]{1,0:T(8,128)} fusion(f32[8192,256]{1,0:T(8,128)} %bitcast.119, s32[8192]{0:T(1024)S(1)} %broadcast_clamp_fusion), kind=kCustom, calls=%fused_computation.1.clone | custom fusion | bytes 16809984 | tf_op jit(solution)/shard_map/jit(_take)/gather | solution.py:194
  351.7 19.3 %multiply_add_fusion.2 = (f32[8192,256]{0,1:T(8,128)}, f32[8192,256]{0,1:T(8,128)}) fusion(f32[8192,256]{0,1:T(8,128)} %copy.136, f32[8192,256]{0,1:T(8,128)} %copy.134, f32[8192,512]{0,1:T(8,128)} %slice_add_fusion.2, pred[8192]{0:T(1024)(128)(4,1)S(1)} %get-tuple-element.31), kind=kLoop, calls=%fused_computation.45 | loop fusion | flops 16777216 | bytes 50339840 | tf_op jit(solution)/shard_map/add | solution.py:195
  371.0 17.2 %fusion.103 = f32[8192,128]{1,0:T(8,128)S(1)} fusion(f32[8192,256]{0,1:T(8,128)} %get-tuple-element.35, s32[256]{0:T(256)S(1)} %copy-done.15), kind=kOutput, calls=%fused_computation.182 | convolution fusion | flops 3221684224 | bytes 12583936 | tf_op jit(solution)/shard_map/dot_general | solution.py:197
  388.2 14.6 %fusion.101 = f32[8192,128]{1,0:T(8,128)S(1)} fusion(f32[8192,256]{0,1:T(8,128)S(1)} %copy-done.2, s32[256]{0:T(256)S(1)} %copy-done.15), kind=kOutput, calls=%fused_computation.181 | convolution fusion | flops 3221684224 | bytes 12583936 | tf_op jit(solution)/shard_map/dot_general | solution.py:200
  402.8 14.8 %fusion.9 = f32[8192,1,128]{2,0,1:T(8,128)S(1)} fusion(f32[8192,128]{1,0:T(8,128)S(1)} %fusion.103, f32[8192,256]{0,1:T(8,128)S(1)} %copy-done.2, s32[256]{0:T(256)S(1)} %copy-done.15), kind=kOutput, calls=%fused_computation.25 | convolution fusion | flops 3222732800 | bytes 16778240 | tf_op jit(solution)/shard_map/dot_general | solution.py:197
  417.6 14.6 %fusion.8 = f32[8192,1,128]{2,0,1:T(8,128)S(1)} fusion(f32[8192,128]{1,0:T(8,128)S(1)} %fusion.101, f32[8192,256]{0,1:T(8,128)S(1)} %bitcast.122, s32[256]{0:T(256)S(1)} %copy-done.15), kind=kOutput, calls=%fused_computation.23 | convolution fusion | flops 3222732800 | bytes 16778240 | tf_op jit(solution)/shard_map/dot_general | solution.py:200
  450.8 19.0 %slice.165 = f32[1024,1027]{0,1:T(8,128)} slice(f32[1024,2054]{0,1:T(8,128)} %pad_maximum_fusion.1), slice={[0:1024:1], [0:2054:2]} | slice | bytes 8413184 | tf_op jit(solution)/shard_map/slice | solution.py:102
  469.8 19.0 %slice.167 = f32[1024,1027]{0,1:T(8,128)} slice(f32[1024,2054]{0,1:T(8,128)} %pad_maximum_fusion.1), slice={[0:1024:1], [1:2054:2]} | slice | bytes 8413184 | tf_op jit(solution)/shard_map/slice | solution.py:102
  488.8 13.6 %multiply_add_fusion.5 = f32[1024,1024]{0,1:T(8,128)S(1)} fusion(f32[1024,1027]{0,1:T(8,128)} %slice.167, f32[1024,1027]{0,1:T(8,128)} %slice.165), kind=kLoop, calls=%fused_computation.91 | loop fusion | flops 15728640 | bytes 37748736 | tf_op jit(solution)/shard_map/add | solution.py:108
  563.1 20.8 %fusion.41 = (f32[1024,1024]{0,1:T(8,128)}, f32[1024,1024]{0,1:T(8,128)}) fusion(f32[1024,1024]{0,1:T(8,128)} %mul.705, f32[1,1024,1024]{1,2,0:T(8,128)} %copy.160, f32[1024,1027]{0,1:T(8,128)} %slice.167, f32[1024,1027]{0,1:T(8,128)} %slice.165, f32[1,1024,1024]{1,2,0:T(8,128)} %copy.159), kind=kLoop, calls=%fused_computation.89 | loop fusion | flops 25165824 | bytes 54525952 | tf_op jit(solution)/shard_map/mul | solution.py:212
  632.2 20.3 %add_bitcast_fusion.1 = (f32[1024,1024,1]{0,1,2:T(8,128)S(1)}, f32[1024,1024,1]{0,1,2:T(8,128)S(1)}) fusion(f32[1024,1024]{0,1:T(8,128)} %reshape.120, f32[1024,1024]{0,1:T(8,128)} %fusion.42, f32[1024,3]{0,1:T(4,128)S(1)} %get-tuple-element.56, f32[1024,3]{0,1:T(4,128)S(1)} %get-tuple-element.55), kind=kLoop, calls=%fused_computation.87 | loop fusion | flops 41943040 | bytes 16801792 | tf_op jit(solution)/shard_map/stack | solution.py:125
  680.0 37.2 %all-reduce = (f32[]{:T(128)}, f32[]{:T(128)}) all-reduce(f32[]{:T(128)} %fusion.167, f32[]{:T(128)} %get-tuple-element.59), channel_id=1, replica_groups=mesh['vis'=8,'tile'=4] {'vis','tile'}, use_global_device_ids=true, to_apply=%region_3.5 | all-reduce | flops 2 | bytes 16 | tf_op jit(solution)/shard_map/psum | solution.py:229
  720.6 28.7 %all-gather.4.cloned.1.call-done = f32[1024,2,128]{2,0,1:T(8,128)} async-done(((f32[256,2,128]{2,0,1:T(8,128)}), f32[1024,2,128]{2,0,1:T(8,128)}) %all-gather.4.cloned.1.call-update) | async-done | bytes 1048592 | tf_op jit(solution)/shard_map/all_gather | solution.py:234
  749.6 55.1 %all-gather.6.cloned.1.call-done = f32[8192,2,128]{2,0,1:T(8,128)} async-done(((f32[1024,2,128]{2,0,1:T(8,128)}), f32[8192,2,128]{2,0,1:T(8,128)}) %all-gather.6.cloned.1.call-update) | async-done | bytes 8388624 | tf_op jit(solution)/shard_map/all_gather | solution.py:235
  835.4 22.0 %multiply_subtract_fusion.1 = (f32[8192,256]{0,1:T(8,128)}, f32[8192,256]{0,1:T(8,128)}) fusion(f32[8192,256]{0,1:T(8,128)} %convolution_subtract_fusion, f32[8192,512]{0,1:T(8,128)} %slice_add_fusion.2, f32[8192,256]{0,1:T(8,128)} %fusion.43, s32[256]{0:T(256)S(1)} %copy-done.15, f32[8192,2,128]{2,0,1:T(8,128)} %all-gather.6.cloned.1.call-done), kind=kOutput, calls=%fused_computation.43 | convolution fusion | flops 3236364288 | bytes 54526976 | tf_op jit(solution)/shard_map/dot_general | solution.py:239
  869.1 17.5 %copy.158 = f32[8192,512]{1,0:T(8,128)} copy(f32[8192,512]{0,1:T(8,128)} %pad_maximum_fusion) | data formatting | bytes 33554432 | tf_op jit(solution)/shard_map/reshape | solution.py:245
  897.0 31.7 %fusion = f32[8,1024,1536]{2,1,0:T(8,128)} fusion(bf16[8,1024,512]{2,1,0:T(8,128)(2,1)S(1)} %get-tuple-element.44, bf16[8,1024,512]{2,1,0:T(8,128)(2,1)} %get-tuple-element.45, bf16[8,1024,512]{2,1,0:T(8,128)(2,1)S(1)} %get-tuple-element.43, s32[8,1024]{1,0:T(8,128)S(1)} %eq.45), kind=kOutput, calls=%fused_computation.3 | convolution fusion | flops 25853689856 | bytes 75530240 | tf_op jit(solution)/shard_map/gkb,gbc->gkc/dot_general | solution.py:152
  928.7 23.9 %slice_add_fusion = f32[8,1024,512]{2,1,0:T(8,128)} fusion(f32[8,1024,1536]{2,1,0:T(8,128)} %fusion), kind=kLoop, calls=%fused_computation.14 | loop fusion | flops 8388608 | bytes 67108864 | tf_op jit(solution)/shard_map/add | solution.py:153
  998.6 21.5 %multiply_subtract_fusion = (f32[64,128,256]{2,0,1:T(8,128)}, f32[64,128,256]{2,0,1:T(8,128)}) fusion(f32[64,128,256]{2,0,1:T(8,128)} %fusion.17, f32[64,128]{0,1:T(8,128)S(1)} %fusion.137, f32[64,128]{0,1:T(8,128)S(1)} %copy-done.9, f32[64,128,256]{2,0,1:T(8,128)} %fusion.23, f32[64,128,256]{2,0,1:T(8,128)} %fusion.19, f32[64,128,256]{2,1,0:T(8,128)S(1)} %bitcast.131), kind=kOutput, calls=%fused_computation.40 | convolution fusion | flops 1631641600 | bytes 50397184 | tf_op jit(solution)/shard_map/abm,ca->cbm/dot_general | solution.py:46
  1020.2 16.3 %fusion.13 = f32[128,64,256]{2,0,1:T(8,128)S(1)} fusion(f32[64,128,256]{2,0,1:T(8,128)} %get-tuple-element.34), kind=kOutput, calls=%fused_computation.34 | convolution fusion | flops 3221454848 | bytes 16777216 | tf_op jit(solution)/shard_map/cbm,db->dcm/dot_general | solution.py:48
  1088.9 66.7 %all-to-all-done.1 = f32[8,1024,256]{2,1,0:T(8,128)} async-done(((f32[8,1024,256]{2,1,0:T(8,128)}), f32[8,1024,256]{2,1,0:T(8,128)}, u32[]{:S(2)}, u32[]{:S(2)}) %all-to-all-start.1) | async-done | bytes 8388640 | tf_op jit(solution)/shard_map/all_to_all | solution.py:249
  1172.3 13.6 %fusion.12 = f32[1024,2048]{0,1:T(8,128)} fusion(f32[1024,2048]{0,1:T(8,128)} %copy.154, f32[1024,2048]{0,1:T(8,128)} %reshape.121, f32[1024,8,256]{0,2,1:T(8,128)} %copy.153), kind=kLoop, calls=%fused_computation.33 | loop fusion | flops 8388608 | bytes 33554432 | tf_op jit(solution)/shard_map/max | solution.py:251
  (140 shorter events, 396.3 us)
Async XLA Ops:
  7.2 671.8 %copy-start = (f32[128,128]{1,0:T(8,128)S(1)}, f32[128,128]{1,0:T(8,128)}, u32[]{:S(2)}) copy-start(f32[128,128]{1,0:T(8,128)} %param.15) | copy-start | bytes 196612
  16.5 5.4 copy-start.16
  16.5 119.9 %all-to-all-start = ((f32[1024,8,256]{0,2,1:T(8,128)}), f32[1024,8,256]{0,2,1:T(8,128)}, u32[]{:S(2)}, u32[]{:S(2)}) async-start(f32[1024,8,256]{0,2,1:T(8,128)} %bitcast.123), calls=%async_computation | async-start | bytes 16777216 | tf_op jit(solution)/shard_map/all_to_all | solution.py:170
  21.8 610.3 %reduce-scatter.3.cloned.1.call-start = ((), (), s32[]{:S(2)}) async-start(), calls=%async_computation.4 | async-start | bytes 9437184 | tf_op jit(solution)/shard_map/reduce_scatter | solution.py:204
  92.8 0.8 copy-start.14
  93.1 69.9 %copy-start.8 = (f32[64,128]{0,1:T(8,128)}, f32[64,128]{0,1:T(8,128)S(1)}, u32[]{:S(2)}) copy-start(f32[64,128]{0,1:T(8,128)S(1)} %get-tuple-element.62) | copy-start | bytes 98308
  181.6 17.5 %slice-start.2 = ((s8[8388608]{0:T(1024)(128)(4,1)}), s8[4194304]{0:T(1024)(128)(4,1)S(1)}, s32[]{:S(2)}) async-start(s8[8388608]{0:T(1024)(128)(4,1)} %bitcast.126), calls=%async_computation.10 | async-start | bytes 8388608
  181.6 17.5 %slice-start.3 = ((s8[8388608]{0:T(1024)(128)(4,1)}), s8[4194304]{0:T(1024)(128)(4,1)S(1)}, s32[]{:S(2)}) async-start(s8[8388608]{0:T(1024)(128)(4,1)} %bitcast.126), calls=%async_computation.11 | async-start | bytes 8388608
  351.7 19.3 %copy-start.15 = (s32[256]{0:T(256)S(1)}, s32[256]{0:T(256)}, u32[]{:S(2)}) copy-start(s32[256]{0:T(256)} %copy-done.14) | copy-start | bytes 3076
  371.0 17.2 %copy-start.2 = (f32[8192,256]{0,1:T(8,128)S(1)}, f32[8192,256]{0,1:T(8,128)}, u32[]{:S(2)}) copy-start(f32[8192,256]{0,1:T(8,128)} %get-tuple-element.36) | copy-start | bytes 25165828
  388.2 29.4 %slice-start = ((s8[8388608]{0:T(1024)(128)(4,1)}), s8[4194304]{0:T(1024)(128)(4,1)S(1)}, s32[]{:S(2)}) async-start(s8[8388608]{0:T(1024)(128)(4,1)} %bitcast.121), calls=%async_computation.8 | async-start | bytes 8388608
  402.8 14.8 %slice-start.1 = ((s8[8388608]{0:T(1024)(128)(4,1)}), s8[4194304]{0:T(1024)(128)(4,1)S(1)}, s32[]{:S(2)}) async-start(s8[8388608]{0:T(1024)(128)(4,1)} %bitcast.121), calls=%async_computation.9 | async-start | bytes 8388608
  436.2 241.8 %reduce-scatter.5.cloned.1.call-start = ((), (), s32[]{:S(2)}) async-start(), calls=%async_computation.5 | async-start | bytes 1310720 | tf_op jit(solution)/shard_map/reduce_scatter | solution.py:205
  437.0 3.9 collective-permute-start
  502.4 10.9 copy-start.5
  502.4 22.5 %collective-permute-start.1 = (f32[1024,6]{0,1:T(8,128)S(1)}, f32[1024,6]{0,1:T(8,128)S(1)}, u32[]{:S(2)}, u32[]{:S(2)}) collective-permute-start(f32[1024,6]{0,1:T(8,128)S(1)} %slice.228), channel_id=1, source_target_pairs={{1,0},{2,1},{3,2},{0,3},{5,4},{6,5},{7,6},{4,7},{9,8},{10,9},{11,1... | collective-permute-start | bytes 73736 | tf_op jit(solution)/shard_map/ppermute | solution.py:27
  601.8 2.8 copy-start.4
  603.9 8.0 collective-permute-start.2
  626.3 5.8 collective-permute-start.3
  632.1 117.2 %all-gather.4.cloned.1.call-start = ((), (), s32[]{:S(2)}) async-start(), calls=%async_computation.6 | async-start | bytes 1310720 | tf_op jit(solution)/shard_map/all_gather | solution.py:234
  667.0 12.0 copy-start.12
  667.0 12.0 copy-start.13
  667.1 82.3 %copy-start.11 = (s32[8192]{0:T(1024)S(1)}, s32[8192]{0:T(1024)}, u32[]{:S(2)}) copy-start(s32[8192]{0:T(1024)} %copy-done.10) | copy-start | bytes 98308
  718.7 0.7 copy-start.6
  720.5 84.2 %all-gather.6.cloned.1.call-start = ((), (), s32[]{:S(2)}) async-start(), calls=%async_computation.7 | async-start | bytes 9437184 | tf_op jit(solution)/shard_map/all_gather | solution.py:235
  804.7 10.0 copy-start.3
  985.5 13.2 %copy-start.9 = (f32[64,128]{0,1:T(8,128)S(1)}, f32[64,128]{0,1:T(8,128)}, u32[]{:S(2)}) copy-start(f32[64,128]{0,1:T(8,128)} %copy-done.8) | copy-start | bytes 98308
  1020.2 16.3 %slice-start.4 = ((s8[8388608]{0:T(1024)(128)(4,1)}), s8[4194304]{0:T(1024)(128)(4,1)S(1)}, s32[]{:S(2)}) async-start(s8[8388608]{0:T(1024)(128)(4,1)} %bitcast.137), calls=%async_computation.12 | async-start | bytes 8388608
  1020.2 16.3 %slice-start.5 = ((s8[8388608]{0:T(1024)(128)(4,1)}), s8[4194304]{0:T(1024)(128)(4,1)S(1)}, s32[]{:S(2)}) async-start(s8[8388608]{0:T(1024)(128)(4,1)} %bitcast.137), calls=%async_computation.13 | async-start | bytes 8388608
  1056.6 99.0 %all-to-all-start.1 = ((f32[8,1024,256]{2,1,0:T(8,128)}), f32[8,1024,256]{2,1,0:T(8,128)}, u32[]{:S(2)}, u32[]{:S(2)}) async-start(f32[8,1024,256]{2,1,0:T(8,128)} %bitcast.136), calls=%async_computation.3 | async-start | bytes 16777216 | tf_op jit(solution)/shard_map/all_to_all | solution.py:249
  1061.6 9.3 copy-start.7
  1172.3 22.7 %copy-start.1 = (f32[128,128]{1,0:T(8,128)S(1)}, f32[128,128]{1,0:T(8,128)}, u32[]{:S(2)}) copy-start(f32[128,128]{1,0:T(8,128)} %param.15) | copy-start | bytes 196612
  (1 other events, 0.6 us)
Sparse Core Ops, SparseCore 0:
  436.3 67.4 reduce-scatter.2
  632.2 24.4 reduce-scatter.4
  720.7 28.5 all-gather.3
  751.0 53.6 all-gather.5

commit v4 on v2

--- a/solution.py
+++ b/solution.py
@@ -190,8 +190,9 @@
     cell_angles = cell_turns.astype(jnp.float32) * (TWO_PI / len_cols)
     cell_cos = jnp.cos(cell_angles)
     cell_sin = jnp.sin(cell_angles)
-    picked_real = jnp.take(spec_real, row_of, axis=0)
-    picked_imag = jnp.take(spec_imag, row_of, axis=0)
+    picked = jnp.take(jnp.concatenate([spec_real, spec_imag], axis=1), row_of, axis=0)
+    picked_real = picked[:, :chunk]
+    picked_imag = picked[:, chunk:]
     twisted_real = picked_real * band_cos + picked_imag * band_sin
     twisted_imag = picked_imag * band_cos - picked_real * band_sin
     part_real = jnp.dot(twisted_real, cell_cos, precision=precise) + jnp.dot(

time: 1190 us -> 1170 us (0.983)
  local copies, waits for them, and re-layouts: 342 us -> 310 us
  other arithmetic: 208 us -> 226 us
    gather x4 -> x2, local copies, waits for them, and re-layouts: 87.4 us -> 58.2 us  [on_device(): jnp.take(jnp.concatenate([spec_real, spec_imag], axis=1), row_of, axis=0)]
    unnamed x59 -> x63, local copies, waits for them, and re-layouts: 52 us -> 52 us
where the time goes in v4:
time: 1170 us; the launch traced here: 1160 us
  matrix products  356 us (30%)
  local copies, waits for them, and re-layouts  310 us (26%)
  other arithmetic  226 us (19%)
  waiting for transfers between devices  124 us (11%)
  blocking collectives  110 us (9%)
  between operations  16.5 us (1%)
  starting transfers between devices  15.6 us (1%)
    all_gather x1, blocking collectives, on_device(): lax.all_gather(block_index.astype(jnp.float32), ('vis', 'tile'), tiled=True)  70.9 us
    dot_general x4, matrix products, complex_einsum(): real_part = jnp.einsum(form, left_real, table_cos, precision=precise)  68.6 us
    reduce_scatter x1, waiting for transfers between devices, on_device(): partial = lax.psum_scatter(partial, 'vis', scatter_dimension=0, tiled=True)  67.5 us
    gather x2, local copies, waits for them, and re-layouts, on_device(): jnp.take(jnp.concatenate([spec_real, spec_imag], axis=1), row_of, axis=0)  58.2 us
    slice x4, local copies, waits for them, and re-layouts, analyse_local(): lax.slice_in_dim(extended, parity, extended.shape[1], 2, 1)  58.1 us
    unnamed x63, local copies, waits for them, and re-layouts  52 us
    dot_general x3, matrix products, complex_einsum(): imag_part = jnp.einsum(form, left_real, table_sin, precision=precise)  46 us
    dot_general x3, matrix products, complex_einsum(): jnp.einsum(form, left_imag, table_sin, precision=precise)  42.8 us
  transfers between devices with their start and end apart: 10, of which 3 were waited for; matrix products, arithmetic and copies ran while one was open for 26% of the time, Pallas kernels for 0%

profile of v4, /device:TPU:0, one launch (start us, length us, event | category | flops | bytes accessed | tf_op | source)
XLA Modules:
  0.0 1158.1 jit_solution(4737511129548298382)
XLA Ops:
  21.9 70.9 %all-gather = f32[32,1,256]{2,1,0:T(1,128)S(1)} all-gather(f32[1,1,256]{2,1,0:T(1,128)S(1)} %bitcast.142), channel_id=1, replica_groups=mesh['vis'=8,'tile'=4] {'vis','tile'}, dimensions={0}, use_global_device_ids=true | all-gather | bytes 33792 | tf_op jit(solution)/shard_map/all_gather | solution.py:172
  94.8 19.4 %fusion.63 = f32[8192,1536]{0,1:T(8,128)} fusion(s32[8192]{0:T(1024)S(1)} %fusion.125, bf16[64,512]{1,0:T(8,128)(2,1)S(1)} %get-tuple-element.45, bf16[64,512]{1,0:T(8,128)(2,1)S(1)} %get-tuple-element.44, bf16[64,512]{1,0:T(8,128)(2,1)S(1)} %get-tuple-element.43), kind=kOutput, calls=%fused_computation.121 | convolution fusion | flops 1611726848 | bytes 50561024 | tf_op jit(solution)/shard_map/dot_general | solution.py:142
  114.2 22.7 %slice_add_fusion.2 = f32[8192,512]{0,1:T(8,128)} fusion(f32[8192,1536]{0,1:T(8,128)} %fusion.63), kind=kLoop, calls=%fused_computation.15 | loop fusion | flops 8388608 | bytes 67108864 | tf_op jit(solution)/shard_map/add | solution.py:143
  146.1 17.6 %fusion.33 = f32[64,128,256]{2,0,1:T(8,128)} fusion(f32[64,128,256]{2,1,0:T(8,128)} %bitcast.123), kind=kOutput, calls=%fused_computation.67 | convolution fusion | flops 1610670080 | bytes 16777216 | tf_op jit(solution)/shard_map/abm,ca->cbm/dot_general | solution.py:46
  163.6 18.5 %multiply_subtract_fusion.3 = (f32[64,128,256]{2,0,1:T(8,128)S(1)}, f32[64,128,256]{2,0,1:T(8,128)}) fusion(f32[64,128,256]{2,0,1:T(8,128)} %fusion.33, f32[64,128]{0,1:T(8,128)S(1)} %get-tuple-element.54, f32[64,128]{0,1:T(8,128)S(1)} %get-tuple-element.55, f32[64,128,256]{2,1,0:T(8,128)} %bitcast.124), kind=kOutput, calls=%fused_computation.49 | convolution fusion | flops 1627451392 | bytes 33619968 | tf_op jit(solution)/shard_map/abm,ca->cbm/dot_general | solution.py:51
  182.2 17.5 %fusion.27 = f32[128,64,256]{2,0,1:T(8,128)} fusion(f32[64,128,256]{2,0,1:T(8,128)} %get-tuple-element.31), kind=kOutput, calls=%fused_computation.61 | convolution fusion | flops 3221454848 | bytes 16777216 | tf_op jit(solution)/shard_map/cbm,db->dcm/dot_general | solution.py:53
  199.7 13.6 %fusion.25 = f32[128,64,256]{2,0,1:T(8,128)} fusion(f32[64,128,256]{2,0,1:T(8,128)S(1)} %bitcast.126), kind=kOutput, calls=%fused_computation.59 | convolution fusion | flops 3221471232 | bytes 16777216 | tf_op jit(solution)/shard_map/cbm,db->dcm/dot_general | solution.py:48
  213.3 14.3 %fusion.45 = f32[128,64,256]{2,0,1:T(8,128)S(1)} fusion(f32[128,64,256]{2,0,1:T(8,128)} %fusion.27, f32[64,128,256]{2,0,1:T(8,128)S(1)} %get-tuple-element.30), kind=kOutput, calls=%fused_computation.95 | convolution fusion | flops 3223568384 | bytes 25165824 | tf_op jit(solution)/shard_map/cbm,db->dcm/dot_general | solution.py:51
  235.9 17.4 %subtract_add_fusion.1 = f32[128,64,256]{2,0,1:T(8,128)} fusion(f32[128,64,256]{2,0,1:T(8,128)} %fusion.25, f32[128,64,256]{2,0,1:T(8,128)S(1)} %fusion.45, f32[64,128,256]{2,0,1:T(8,128)S(1)} %get-tuple-element.30), kind=kOutput, calls=%fused_computation.47 | convolution fusion | flops 3227746304 | bytes 33554432 | tf_op jit(solution)/shard_map/cbm,db->dcm/dot_general | solution.py:46
  268.1 40.7 %gather_fusion = f32[8192,512]{1,0:T(8,128)} fusion(f32[8192,512]{1,0:T(8,128)} %pad_maximum_fusion, s32[8192]{0:T(1024)S(1)} %broadcast_clamp_fusion), kind=kCustom, calls=%fused_computation | custom fusion | bytes 33587200 | tf_op jit(solution)/shard_map/jit(_take)/gather | solution.py:193
  308.8 17.5 %copy.130 = f32[8192,512]{0,1:T(8,128)} copy(f32[8192,512]{1,0:T(8,128)} %gather_fusion) | data formatting | bytes 33554432 | tf_op jit(solution)/shard_map/jit(_take)/gather | solution.py:193
  338.0 18.8 %multiply_add_fusion.2 = (f32[8192,256]{0,1:T(8,128)}, f32[8192,256]{0,1:T(8,128)}) fusion(f32[8192,512]{0,1:T(8,128)} %broadcast_select_fusion, f32[8192,512]{0,1:T(8,128)} %slice_add_fusion.2), kind=kLoop, calls=%fused_computation.45 | loop fusion | flops 12582912 | bytes 50331648 | tf_op jit(solution)/shard_map/add | solution.py:196
  356.8 17.2 %fusion.105 = f32[8192,128]{1,0:T(8,128)S(1)} fusion(f32[8192,256]{0,1:T(8,128)} %get-tuple-element.28, s32[256]{0:T(256)S(1)} %copy-done.17), kind=kOutput, calls=%fused_computation.184 | convolution fusion | flops 3221684224 | bytes 12583936 | tf_op jit(solution)/shard_map/dot_general | solution.py:198
  374.0 14.6 %fusion.103 = f32[8192,128]{1,0:T(8,128)S(1)} fusion(f32[8192,256]{0,1:T(8,128)S(1)} %copy-done.2, s32[256]{0:T(256)S(1)} %copy-done.17), kind=kOutput, calls=%fused_computation.183 | convolution fusion | flops 3221684224 | bytes 12583936 | tf_op jit(solution)/shard_map/dot_general | solution.py:201
  388.6 14.8 %fusion.9 = f32[8192,1,128]{2,0,1:T(8,128)S(1)} fusion(f32[8192,128]{1,0:T(8,128)S(1)} %fusion.105, f32[8192,256]{0,1:T(8,128)S(1)} %copy-done.2, s32[256]{0:T(256)S(1)} %copy-done.17), kind=kOutput, calls=%fused_computation.25 | convolution fusion | flops 3222732800 | bytes 16778240 | tf_op jit(solution)/shard_map/dot_general | solution.py:198
  403.4 14.6 %fusion.8 = f32[8192,1,128]{2,0,1:T(8,128)S(1)} fusion(f32[8192,128]{1,0:T(8,128)S(1)} %fusion.103, f32[8192,256]{0,1:T(8,128)S(1)} %bitcast.119, s32[256]{0:T(256)S(1)} %copy-done.17), kind=kOutput, calls=%fused_computation.23 | convolution fusion | flops 3222732800 | bytes 16778240 | tf_op jit(solution)/shard_map/dot_general | solution.py:201
  422.0 67.5 %reduce-scatter.3.cloned.1.call-done = f32[1024,2,128]{2,0,1:T(8,128)} async-done(((f32[8192,2,128]{2,0,1:T(8,128)}), f32[1024,2,128]{2,0,1:T(8,128)}) %reduce-scatter.3.cloned.1.call-update) | async-done | bytes 1048592 | tf_op jit(solution)/shard_map/reduce_scatter | solution.py:205
  490.9 28.3 %reduce-scatter.5.cloned.1.call-done = f32[256,2,128]{2,0,1:T(8,128)} async-done(((f32[1024,2,128]{2,0,1:T(8,128)}), f32[256,2,128]{2,0,1:T(8,128)}) %reduce-scatter.5.cloned.1.call-update) | async-done | bytes 262160 | tf_op jit(solution)/shard_map/reduce_scatter | solution.py:206
  521.2 38.9 %all-reduce = (f32[]{:T(128)}, f32[]{:T(128)}) all-reduce(f32[]{:T(128)} %fusion.169, f32[]{:T(128)} %get-tuple-element.50), channel_id=1, replica_groups=mesh['vis'=8,'tile'=4] {'vis','tile'}, use_global_device_ids=true, to_apply=%region_3.4 | all-reduce | flops 2 | bytes 16 | tf_op jit(solution)/shard_map/psum | solution.py:212
  563.4 28.0 %all-gather.4.cloned.1.call-done = f32[1024,2,128]{2,0,1:T(8,128)} async-done(((f32[256,2,128]{2,0,1:T(8,128)}), f32[1024,2,128]{2,0,1:T(8,128)}) %all-gather.4.cloned.1.call-update) | async-done | bytes 1048592 | tf_op jit(solution)/shard_map/all_gather | solution.py:217
  606.9 19.1 %slice.180 = f32[1024,1027]{0,1:T(8,128)} slice(f32[1024,2054]{0,1:T(8,128)} %pad_maximum_fusion.2), slice={[0:1024:1], [0:2054:2]} | slice | bytes 8413184 | tf_op jit(solution)/shard_map/slice | solution.py:102
  626.0 18.9 %slice.182 = f32[1024,1027]{0,1:T(8,128)} slice(f32[1024,2054]{0,1:T(8,128)} %pad_maximum_fusion.2), slice={[0:1024:1], [1:2054:2]} | slice | bytes 8413184 | tf_op jit(solution)/shard_map/slice | solution.py:102
  644.8 13.6 %multiply_add_fusion.5 = f32[1024,1024]{0,1:T(8,128)S(1)} fusion(f32[1024,1027]{0,1:T(8,128)} %slice.182, f32[1024,1027]{0,1:T(8,128)} %slice.180), kind=kLoop, calls=%fused_computation.92 | loop fusion | flops 15728640 | bytes 37748736 | tf_op jit(solution)/shard_map/add | solution.py:108
  729.5 22.0 %multiply_subtract_fusion.1 = (f32[8192,256]{0,1:T(8,128)}, f32[8192,256]{0,1:T(8,128)}) fusion(f32[8192,256]{0,1:T(8,128)} %convolution_subtract_fusion, f32[8192,512]{0,1:T(8,128)} %slice_add_fusion.2, f32[8192,256]{0,1:T(8,128)} %fusion.43, s32[256]{0:T(256)S(1)} %copy-done.17, f32[8192,2,128]{2,0,1:T(8,128)} %all-gather.6.cloned.1.call-done), kind=kOutput, calls=%fused_computation.43 | convolution fusion | flops 3236364288 | bytes 54526976 | tf_op jit(solution)/shard_map/dot_general | solution.py:222
  763.2 17.4 %copy.152 = f32[8192,512]{1,0:T(8,128)} copy(f32[8192,512]{0,1:T(8,128)} %pad_maximum_fusion.1) | data formatting | bytes 33554432 | tf_op jit(solution)/shard_map/reshape | solution.py:228
  791.0 31.5 %fusion = f32[8,1024,1536]{2,1,0:T(8,128)} fusion(bf16[8,1024,512]{2,1,0:T(8,128)(2,1)S(1)} %get-tuple-element.35, bf16[8,1024,512]{2,1,0:T(8,128)(2,1)} %get-tuple-element.36, bf16[8,1024,512]{2,1,0:T(8,128)(2,1)S(1)} %get-tuple-element.34, s32[8,1024]{1,0:T(8,128)S(1)} %eq.45), kind=kOutput, calls=%fused_computation.2 | convolution fusion | flops 25853689856 | bytes 75530240 | tf_op jit(solution)/shard_map/gkb,gbc->gkc/dot_general | solution.py:152
  822.5 23.9 %slice_add_fusion = f32[8,1024,512]{2,1,0:T(8,128)} fusion(f32[8,1024,1536]{2,1,0:T(8,128)} %fusion), kind=kLoop, calls=%fused_computation.13 | loop fusion | flops 8388608 | bytes 67108864 | tf_op jit(solution)/shard_map/add | solution.py:153
  892.6 21.8 %multiply_subtract_fusion = (f32[64,128,256]{2,0,1:T(8,128)}, f32[64,128,256]{2,0,1:T(8,128)}) fusion(f32[64,128,256]{2,0,1:T(8,128)} %fusion.17, f32[64,128]{0,1:T(8,128)S(1)} %copy-done.13, f32[64,128]{0,1:T(8,128)S(1)} %copy-done.10, f32[64,128,256]{2,0,1:T(8,128)} %fusion.23, f32[64,128,256]{2,0,1:T(8,128)} %fusion.19, f32[64,128,256]{2,1,0:T(8,128)S(1)} %bitcast.130), kind=kOutput, calls=%fused_computation.40 | convolution fusion | flops 1631641600 | bytes 50397184 | tf_op jit(solution)/shard_map/abm,ca->cbm/dot_general | solution.py:46
  914.3 16.1 %fusion.13 = f32[128,64,256]{2,0,1:T(8,128)S(1)} fusion(f32[64,128,256]{2,0,1:T(8,128)} %get-tuple-element.25), kind=kOutput, calls=%fused_computation.34 | convolution fusion | flops 3221454848 | bytes 16777216 | tf_op jit(solution)/shard_map/cbm,db->dcm/dot_general | solution.py:48
  970.2 20.8 %fusion.42 = (f32[1024,1024]{0,1:T(8,128)}, f32[1024,1024]{0,1:T(8,128)}) fusion(f32[1024,1024]{0,1:T(8,128)} %mul.725, f32[1,1024,1024]{1,2,0:T(8,128)} %copy.154, f32[1024,1027]{0,1:T(8,128)} %slice.182, f32[1024,1027]{0,1:T(8,128)} %slice.180, f32[1,1024,1024]{1,2,0:T(8,128)} %copy.153), kind=kLoop, calls=%fused_computation.91 | loop fusion | flops 25165824 | bytes 54525952 | tf_op jit(solution)/shard_map/mul | solution.py:239
  1064.8 20.7 %add_bitcast_fusion.1 = (f32[1024,1024,1]{0,1,2:T(8,128)S(1)}, f32[1024,1024,1]{0,1,2:T(8,128)S(1)}) fusion(f32[1024,1024]{0,1:T(8,128)} %reshape.124, f32[1024,1024]{0,1:T(8,128)} %get-tuple-element.22, f32[1024,3]{0,1:T(4,128)S(1)} %get-tuple-element.47, f32[1024,3]{0,1:T(4,128)S(1)} %get-tuple-element.46), kind=kLoop, calls=%fused_computation.88 | loop fusion | flops 41943040 | bytes 16801792 | tf_op jit(solution)/shard_map/stack | solution.py:125
  1128.6 13.6 %fusion.12 = f32[1024,2048]{0,1:T(8,128)} fusion(f32[1024,2048]{0,1:T(8,128)} %copy.148, f32[1024,2048]{0,1:T(8,128)} %reshape.125, f32[1024,8,256]{0,2,1:T(8,128)} %copy.141), kind=kLoop, calls=%fused_computation.33 | loop fusion | flops 8388608 | bytes 33554432 | tf_op jit(solution)/shard_map/max | solution.py:249
  (150 shorter events, 389.3 us)
Async XLA Ops:
  7.2 512.0 %copy-start = (f32[128,128]{1,0:T(8,128)S(1)}, f32[128,128]{1,0:T(8,128)}, u32[]{:S(2)}) copy-start(f32[128,128]{1,0:T(8,128)} %param.13) | copy-start | bytes 196612
  16.5 120.5 %all-to-all-start = ((f32[1024,8,256]{0,2,1:T(8,128)}), f32[1024,8,256]{0,2,1:T(8,128)}, u32[]{:S(2)}, u32[]{:S(2)}) async-start(f32[1024,8,256]{0,2,1:T(8,128)} %bitcast.120), calls=%async_computation | async-start | bytes 16777216 | tf_op jit(solution)/shard_map/all_to_all | solution.py:170
  21.8 467.8 %reduce-scatter.3.cloned.1.call-start = ((), (), s32[]{:S(2)}) async-start(), calls=%async_computation.4 | async-start | bytes 9437184 | tf_op jit(solution)/shard_map/reduce_scatter | solution.py:205
  93.1 70.5 %copy-start.9 = (f32[64,128]{0,1:T(8,128)}, f32[64,128]{0,1:T(8,128)S(1)}, u32[]{:S(2)}) copy-start(f32[64,128]{0,1:T(8,128)S(1)} %get-tuple-element.55) | copy-start | bytes 98308
  182.2 17.6 %slice-start.4 = ((s8[8388608]{0:T(1024)(128)(4,1)}), s8[4194304]{0:T(1024)(128)(4,1)S(1)}, s32[]{:S(2)}) async-start(s8[8388608]{0:T(1024)(128)(4,1)} %bitcast.125), calls=%async_computation.12 | async-start | bytes 8388608
  182.2 17.6 %slice-start.5 = ((s8[8388608]{0:T(1024)(128)(4,1)}), s8[4194304]{0:T(1024)(128)(4,1)S(1)}, s32[]{:S(2)}) async-start(s8[8388608]{0:T(1024)(128)(4,1)} %bitcast.125), calls=%async_computation.13 | async-start | bytes 8388608
  253.3 8.4 copy-start.5
  308.8 17.5 %copy-start.18 = (pred[8192]{0:T(1024)(128)(4,1)S(1)}, pred[8192]{0:T(1024)(128)(4,1)}, u32[]{:S(2)}) copy-start(pred[8192]{0:T(1024)(128)(4,1)} %get-tuple-element.20) | copy-start | bytes 24580
  338.0 18.8 %copy-start.17 = (s32[256]{0:T(256)S(1)}, s32[256]{0:T(256)}, u32[]{:S(2)}) copy-start(s32[256]{0:T(256)} %copy-done.16) | copy-start | bytes 3076
  356.8 17.2 %copy-start.2 = (f32[8192,256]{0,1:T(8,128)S(1)}, f32[8192,256]{0,1:T(8,128)}, u32[]{:S(2)}) copy-start(f32[8192,256]{0,1:T(8,128)} %get-tuple-element.29) | copy-start | bytes 25165828
  374.0 29.4 %slice-start = ((s8[8388608]{0:T(1024)(128)(4,1)}), s8[4194304]{0:T(1024)(128)(4,1)S(1)}, s32[]{:S(2)}) async-start(s8[8388608]{0:T(1024)(128)(4,1)} %bitcast.118), calls=%async_computation.8 | async-start | bytes 8388608
  388.6 14.8 %slice-start.1 = ((s8[8388608]{0:T(1024)(128)(4,1)}), s8[4194304]{0:T(1024)(128)(4,1)S(1)}, s32[]{:S(2)}) async-start(s8[8388608]{0:T(1024)(128)(4,1)} %bitcast.118), calls=%async_computation.9 | async-start | bytes 8388608
  422.0 97.3 %copy-start.14 = (f32[256,2,128]{2,1,0:T(2,128)S(1)}, f32[256,2,128]{2,1,0:T(2,128)}, u32[]{:S(2)}) copy-start(f32[256,2,128]{2,1,0:T(2,128)} %param.12) | copy-start | bytes 786436
  422.0 97.3 %copy-start.15 = (f32[256,2,128]{2,1,0:T(2,128)S(1)}, f32[256,2,128]{2,1,0:T(2,128)}, u32[]{:S(2)}) copy-start(f32[256,2,128]{2,1,0:T(2,128)} %param.10) | copy-start | bytes 786436
  422.0 97.2 %reduce-scatter.5.cloned.1.call-start = ((), (), s32[]{:S(2)}) async-start(), calls=%async_computation.5 | async-start | bytes 1310720 | tf_op jit(solution)/shard_map/reduce_scatter | solution.py:206
  489.6 101.8 %all-gather.4.cloned.1.call-start = ((), (), s32[]{:S(2)}) async-start(), calls=%async_computation.6 | async-start | bytes 1310720 | tf_op jit(solution)/shard_map/all_gather | solution.py:217
  563.4 135.3 %all-gather.6.cloned.1.call-start = ((), (), s32[]{:S(2)}) async-start(), calls=%async_computation.7 | async-start | bytes 9437184 | tf_op jit(solution)/shard_map/all_gather | solution.py:218
  591.5 11.2 slice-start.2
  592.4 10.3 slice-start.3
  592.4 10.3 collective-permute-start
  644.8 18.1 %copy-start.12 = (s32[8192]{0:T(1024)S(1)}, s32[8192]{0:T(1024)}, u32[]{:S(2)}) copy-start(s32[8192]{0:T(1024)} %copy-done.11) | copy-start | bytes 98308
  660.5 13.2 %collective-permute-start.1 = (f32[1024,6]{0,1:T(8,128)S(1)}, f32[1024,6]{0,1:T(8,128)S(1)}, u32[]{:S(2)}, u32[]{:S(2)}) collective-permute-start(f32[1024,6]{0,1:T(8,128)S(1)} %slice.243), channel_id=1, source_target_pairs={{1,0},{2,1},{3,2},{0,3},{5,4},{6,5},{7,6},{4,7},{9,8},{10,9},{11,1... | collective-permute-start | bytes 73736 | tf_op jit(solution)/shard_map/ppermute | solution.py:27
  698.7 10.0 copy-start.3
  879.4 13.2 %copy-start.10 = (f32[64,128]{0,1:T(8,128)S(1)}, f32[64,128]{0,1:T(8,128)}, u32[]{:S(2)}) copy-start(f32[64,128]{0,1:T(8,128)} %copy-done.9) | copy-start | bytes 98308
  879.4 13.2 %copy-start.13 = (f32[64,128]{0,1:T(8,128)S(1)}, f32[64,128]{0,1:T(8,128)}, u32[]{:S(2)}) copy-start(f32[64,128]{0,1:T(8,128)} %fusion.139) | copy-start | bytes 98308
  914.3 16.1 %slice-start.6 = ((s8[8388608]{0:T(1024)(128)(4,1)}), s8[4194304]{0:T(1024)(128)(4,1)S(1)}, s32[]{:S(2)}) async-start(s8[8388608]{0:T(1024)(128)(4,1)} %bitcast.136), calls=%async_computation.14 | async-start | bytes 8388608
  914.3 16.1 %slice-start.7 = ((s8[8388608]{0:T(1024)(128)(4,1)}), s8[4194304]{0:T(1024)(128)(4,1)S(1)}, s32[]{:S(2)}) async-start(s8[8388608]{0:T(1024)(128)(4,1)} %bitcast.136), calls=%async_computation.15 | async-start | bytes 8388608
  950.6 161.3 %all-to-all-start.1 = ((f32[8,1024,256]{2,1,0:T(8,128)}), f32[8,1024,256]{2,1,0:T(8,128)}, u32[]{:S(2)}, u32[]{:S(2)}) async-start(f32[8,1024,256]{2,1,0:T(8,128)} %bitcast.135), calls=%async_computation.3 | async-start | bytes 16777216 | tf_op jit(solution)/shard_map/all_to_all | solution.py:232
  1022.1 10.2 collective-permute-start.2
  1046.3 18.4 %collective-permute-start.3 = (f32[2,1024,3]{1,2,0:T(4,128)S(1)}, f32[2,1024,3]{1,2,0:T(4,128)S(1)}, u32[]{:S(2)}, u32[]{:S(2)}) collective-permute-start(f32[2,1024,3]{1,2,0:T(4,128)S(1)} %pad_maximum_fusion.12), channel_id=1, source_target_pairs={{3,0},{0,1},{1,2},{2,3},{7,4},{4,5},{5,6},{6,7},{11,8},{8,9},{9,10... | collective-permute-start | bytes 73736 | tf_op jit(solution)/shard_map/ppermute | solution.py:27
  1100.1 11.0 copy-start.8
  1128.6 22.8 %copy-start.1 = (f32[128,128]{1,0:T(8,128)S(1)}, f32[128,128]{1,0:T(8,128)}, u32[]{:S(2)}) copy-start(f32[128,128]{1,0:T(8,128)} %param.13) | copy-start | bytes 196612
  (6 other events, 14.5 us)
Sparse Core Ops, SparseCore 0:
  422.1 67.4 reduce-scatter.2
  491.9 27.3 reduce-scatter.4
  563.5 27.9 all-gather.3
  593.2 53.6 all-gather.5

commit v5 on v4

--- a/solution.py
+++ b/solution.py
@@ -125,32 +125,31 @@
     return jnp.stack([even_part, odd_part], axis=2).reshape(ext_detail.shape[0], 2 * out_rows)
 
 
-def split_three(values):
+def split_three(values, axis):
     first = lax.reduce_precision(values, exponent_bits=8, mantissa_bits=7)
     rest = values - first
     second = lax.reduce_precision(rest, exponent_bits=8, mantissa_bits=7)
     third = rest - second
     pieces = [first, second, third]
-    return jnp.concatenate([piece.astype(jnp.bfloat16) for piece in pieces], axis=-1)
+    return jnp.concatenate([piece.astype(jnp.bfloat16) for piece in pieces], axis=axis)
 
 
 def pick_rows(index, table):
-    width = table.shape[1]
     selector = (index[:, None] == jnp.arange(table.shape[0], dtype=jnp.int32)[None, :]).astype(
         jnp.bfloat16
     )
-    summed = jnp.dot(selector, split_three(table), preferred_element_type=jnp.float32)
-    return summed[:, :width] + summed[:, width : 2 * width] + summed[:, 2 * width :]
+    selector = jnp.concatenate([selector] * 3, axis=1)
+    return jnp.dot(selector, split_three(table, 0), preferred_element_type=jnp.float32)
 
 
 def rows_to_grid(local_rows, values, row_count):
     groups, members, width = values.shape
-    pieces = split_three(values)
+    pieces = split_three(values, 1)
     selector = (
         jnp.arange(row_count, dtype=jnp.int32)[None, :, None] == local_rows[:, None, :]
     ).astype(jnp.bfloat16)
+    selector = jnp.concatenate([selector] * 3, axis=2)
     summed = jnp.einsum("gkb,gbc->gkc", selector, pieces, preferred_element_type=jnp.float32)
-    summed = summed[..., :width] + summed[..., width : 2 * width] + summed[..., 2 * width :]
     return summed.reshape(groups * row_count, width)
 
 

time: 1170 us -> 1140 us (0.974)
  other arithmetic: 226 us -> 190 us
  waiting for transfers between devices: 124 us -> 143 us
    add x2 -> x0, other arithmetic: 46.6 us -> none  [the longest x1 23.9 us: rows_to_grid(): summed[..., :width] + summed[..., width:2 * width] + summed[..., 2 * width:]]
    all_to_all x1, waiting for transfers between devices: 0.01 us -> 15 us  [on_device(): lax.all_to_all(extrapolated, 'vis', split_axis=1, concat_axis=0, tiled=True)]
    dot_general x1, matrix products: 19.4 us -> 7.09 us  [pick_rows(): jnp.dot(selector, split_three(table, 0), preferred_element_type=jnp.float32)]
    unnamed x63 -> x57, local copies, waits for them, and re-layouts: 52 us -> 51.7 us
  transfers between devices with their start and end apart: 10 -> 10, of which waited for: 3 -> 4; matrix products, arithmetic and copies ran while one was open for 26% -> 24% of each run, Pallas kernels for 0% -> 0%
where the time goes in v5:
time: 1140 us; the launch traced here: 1130 us
  matrix products  345 us (30%)
  local copies, waits for them, and re-layouts  310 us (27%)
  other arithmetic  190 us (17%)
  waiting for transfers between devices  143 us (13%)
  blocking collectives  110 us (10%)
  between operations  16.7 us (1%)
  starting transfers between devices  15.6 us (1%)
    reduce_scatter x1, waiting for transfers between devices, on_device(): partial = lax.psum_scatter(partial, 'vis', scatter_dimension=0, tiled=True)  71.5 us
    all_gather x1, blocking collectives, on_device(): lax.all_gather(block_index.astype(jnp.float32), ('vis', 'tile'), tiled=True)  70.9 us
    dot_general x4, matrix products, complex_einsum(): real_part = jnp.einsum(form, left_real, table_cos, precision=precise)  68.4 us
    gather x2, local copies, waits for them, and re-layouts, on_device(): jnp.take(jnp.concatenate([spec_real, spec_imag], axis=1), row_of, axis=0)  58.2 us
    slice x4, local copies, waits for them, and re-layouts, analyse_local(): lax.slice_in_dim(extended, parity, extended.shape[1], 2, 1)  58 us
    unnamed x57, local copies, waits for them, and re-layouts  51.7 us
    dot_general x3, matrix products, complex_einsum(): imag_part = jnp.einsum(form, left_real, table_sin, precision=precise)  46 us
    dot_general x3, matrix products, complex_einsum(): jnp.einsum(form, left_imag, table_sin, precision=precise)  43 us
  transfers between devices with their start and end apart: 10, of which 4 were waited for; matrix products, arithmetic and copies ran while one was open for 24% of the time, Pallas kernels for 0%

profile of v5, /device:TPU:0, one launch (start us, length us, event | category | flops | bytes accessed | tf_op | source)
XLA Modules:
  0.0 1129.6 jit_solution(4018835292371466064)
XLA Ops:
  21.9 70.9 %all-gather = f32[32,1,256]{2,1,0:T(1,128)S(1)} all-gather(f32[1,1,256]{2,1,0:T(1,128)S(1)} %bitcast.142), channel_id=1, replica_groups=mesh['vis'=8,'tile'=4] {'vis','tile'}, dimensions={0}, use_global_device_ids=true | all-gather | bytes 33792 | tf_op jit(solution)/shard_map/all_gather | solution.py:171
  101.6 15.0 %all-to-all-done = f32[1024,8,256]{0,2,1:T(8,128)} async-done(((f32[1024,8,256]{0,2,1:T(8,128)}), f32[1024,8,256]{0,2,1:T(8,128)}, u32[]{:S(2)}, u32[]{:S(2)}) %all-to-all-start) | async-done | bytes 8388640 | tf_op jit(solution)/shard_map/all_to_all | solution.py:169
  125.7 17.6 %fusion.37 = f32[64,128,256]{2,0,1:T(8,128)} fusion(f32[64,128,256]{2,1,0:T(8,128)} %bitcast.123), kind=kOutput, calls=%fused_computation.67 | convolution fusion | flops 1610670080 | bytes 16777216 | tf_op jit(solution)/shard_map/abm,ca->cbm/dot_general | solution.py:46
  143.3 18.6 %multiply_subtract_fusion.3 = (f32[64,128,256]{2,0,1:T(8,128)S(1)}, f32[64,128,256]{2,0,1:T(8,128)}) fusion(f32[64,128,256]{2,0,1:T(8,128)} %fusion.37, f32[64,128]{0,1:T(8,128)S(1)} %get-tuple-element.54, f32[64,128]{0,1:T(8,128)S(1)} %get-tuple-element.55, f32[64,128,256]{2,1,0:T(8,128)} %bitcast.124), kind=kOutput, calls=%fused_computation.49 | convolution fusion | flops 1627451392 | bytes 33619968 | tf_op jit(solution)/shard_map/abm,ca->cbm/dot_general | solution.py:51
  161.8 17.5 %fusion.31 = f32[128,64,256]{2,0,1:T(8,128)} fusion(f32[64,128,256]{2,0,1:T(8,128)} %get-tuple-element.31), kind=kOutput, calls=%fused_computation.61 | convolution fusion | flops 3221454848 | bytes 16777216 | tf_op jit(solution)/shard_map/cbm,db->dcm/dot_general | solution.py:53
  179.4 13.6 %fusion.29 = f32[128,64,256]{2,0,1:T(8,128)} fusion(f32[64,128,256]{2,0,1:T(8,128)S(1)} %bitcast.126), kind=kOutput, calls=%fused_computation.59 | convolution fusion | flops 3221471232 | bytes 16777216 | tf_op jit(solution)/shard_map/cbm,db->dcm/dot_general | solution.py:48
  193.0 14.3 %fusion.55 = f32[128,64,256]{2,0,1:T(8,128)S(1)} fusion(f32[128,64,256]{2,0,1:T(8,128)} %fusion.31, f32[64,128,256]{2,0,1:T(8,128)S(1)} %get-tuple-element.30), kind=kOutput, calls=%fused_computation.101 | convolution fusion | flops 3223568384 | bytes 25165824 | tf_op jit(solution)/shard_map/cbm,db->dcm/dot_general | solution.py:51
  215.5 17.4 %subtract_add_fusion.1 = f32[128,64,256]{2,0,1:T(8,128)} fusion(f32[128,64,256]{2,0,1:T(8,128)} %fusion.29, f32[128,64,256]{2,0,1:T(8,128)S(1)} %fusion.55, f32[64,128,256]{2,0,1:T(8,128)S(1)} %get-tuple-element.30), kind=kOutput, calls=%fused_computation.47 | convolution fusion | flops 3227746304 | bytes 33554432 | tf_op jit(solution)/shard_map/cbm,db->dcm/dot_general | solution.py:46
  247.7 40.8 %gather_fusion = f32[8192,512]{1,0:T(8,128)} fusion(f32[8192,512]{1,0:T(8,128)} %pad_maximum_fusion, s32[8192]{0:T(1024)S(1)} %broadcast_clamp_fusion), kind=kCustom, calls=%fused_computation | custom fusion | bytes 33587200 | tf_op jit(solution)/shard_map/jit(_take)/gather | solution.py:192
  288.5 17.5 %copy.130 = f32[8192,512]{0,1:T(8,128)} copy(f32[8192,512]{1,0:T(8,128)} %gather_fusion) | data formatting | bytes 33554432 | tf_op jit(solution)/shard_map/jit(_take)/gather | solution.py:192
  317.8 18.8 %multiply_add_fusion.2 = (f32[8192,256]{0,1:T(8,128)}, f32[8192,256]{0,1:T(8,128)}) fusion(f32[8192,512]{0,1:T(8,128)} %broadcast_select_fusion, f32[8192,512]{0,1:T(8,128)} %fusion.41), kind=kLoop, calls=%fused_computation.45 | loop fusion | flops 12582912 | bytes 50331648 | tf_op jit(solution)/shard_map/add | solution.py:195
  336.6 17.2 %fusion.113 = f32[8192,128]{1,0:T(8,128)S(1)} fusion(f32[8192,256]{0,1:T(8,128)} %get-tuple-element.28, s32[256]{0:T(256)S(1)} %iota_add_fusion), kind=kOutput, calls=%fused_computation.188 | convolution fusion | flops 3221684224 | bytes 12583936 | tf_op jit(solution)/shard_map/dot_general | solution.py:197
  353.8 14.6 %fusion.111 = f32[8192,128]{1,0:T(8,128)S(1)} fusion(f32[8192,256]{0,1:T(8,128)S(1)} %copy-done.2, s32[256]{0:T(256)S(1)} %iota_add_fusion), kind=kOutput, calls=%fused_computation.187 | convolution fusion | flops 3221684224 | bytes 12583936 | tf_op jit(solution)/shard_map/dot_general | solution.py:200
  368.4 14.8 %fusion.13 = f32[8192,1,128]{2,0,1:T(8,128)S(1)} fusion(f32[8192,128]{1,0:T(8,128)S(1)} %fusion.113, f32[8192,256]{0,1:T(8,128)S(1)} %copy-done.2, s32[256]{0:T(256)S(1)} %iota_add_fusion), kind=kOutput, calls=%fused_computation.25 | convolution fusion | flops 3222732800 | bytes 16778240 | tf_op jit(solution)/shard_map/dot_general | solution.py:197
  383.3 14.6 %fusion.12 = f32[8192,1,128]{2,0,1:T(8,128)S(1)} fusion(f32[8192,128]{1,0:T(8,128)S(1)} %fusion.111, f32[8192,256]{0,1:T(8,128)S(1)} %bitcast.119, s32[256]{0:T(256)S(1)} %iota_add_fusion), kind=kOutput, calls=%fused_computation.23 | convolution fusion | flops 3222732800 | bytes 16778240 | tf_op jit(solution)/shard_map/dot_general | solution.py:200
  401.9 71.5 %reduce-scatter.3.cloned.1.call-done = f32[1024,2,128]{2,0,1:T(8,128)} async-done(((f32[8192,2,128]{2,0,1:T(8,128)}), f32[1024,2,128]{2,0,1:T(8,128)}) %reduce-scatter.3.cloned.1.call-update) | async-done | bytes 1048592 | tf_op jit(solution)/shard_map/reduce_scatter | solution.py:204
  474.7 28.3 %reduce-scatter.5.cloned.1.call-done = f32[256,2,128]{2,0,1:T(8,128)} async-done(((f32[1024,2,128]{2,0,1:T(8,128)}), f32[256,2,128]{2,0,1:T(8,128)}) %reduce-scatter.5.cloned.1.call-update) | async-done | bytes 262160 | tf_op jit(solution)/shard_map/reduce_scatter | solution.py:205
  505.0 38.9 %all-reduce = (f32[]{:T(128)}, f32[]{:T(128)}) all-reduce(f32[]{:T(128)} %fusion.177, f32[]{:T(128)} %get-tuple-element.50), channel_id=1, replica_groups=mesh['vis'=8,'tile'=4] {'vis','tile'}, use_global_device_ids=true, to_apply=%region_3.4 | all-reduce | flops 2 | bytes 16 | tf_op jit(solution)/shard_map/psum | solution.py:211
  547.2 28.0 %all-gather.4.cloned.1.call-done = f32[1024,2,128]{2,0,1:T(8,128)} async-done(((f32[256,2,128]{2,0,1:T(8,128)}), f32[1024,2,128]{2,0,1:T(8,128)}) %all-gather.4.cloned.1.call-update) | async-done | bytes 1048592 | tf_op jit(solution)/shard_map/all_gather | solution.py:216
  599.5 19.0 %slice.156 = f32[1024,1027]{0,1:T(8,128)} slice(f32[1024,2054]{0,1:T(8,128)} %pad_maximum_fusion.2), slice={[0:1024:1], [0:2054:2]} | slice | bytes 8413184 | tf_op jit(solution)/shard_map/slice | solution.py:102
  618.5 18.9 %slice.158 = f32[1024,1027]{0,1:T(8,128)} slice(f32[1024,2054]{0,1:T(8,128)} %pad_maximum_fusion.2), slice={[0:1024:1], [1:2054:2]} | slice | bytes 8413184 | tf_op jit(solution)/shard_map/slice | solution.py:102
  637.4 13.9 %multiply_add_fusion.5 = f32[1024,1024]{0,1:T(8,128)S(1)} fusion(f32[1024,1027]{0,1:T(8,128)} %slice.158, f32[1024,1027]{0,1:T(8,128)} %slice.156), kind=kLoop, calls=%fused_computation.98 | loop fusion | flops 15728640 | bytes 37748736 | tf_op jit(solution)/shard_map/add | solution.py:108
  722.5 22.0 %multiply_subtract_fusion.1 = (f32[8192,256]{0,1:T(8,128)}, f32[8192,256]{0,1:T(8,128)}) fusion(f32[8192,256]{0,1:T(8,128)} %convolution_subtract_fusion, f32[8192,512]{0,1:T(8,128)} %fusion.41, f32[8192,256]{0,1:T(8,128)} %fusion.53, s32[256]{0:T(256)S(1)} %iota_add_fusion, f32[8192,2,128]{2,0,1:T(8,128)} %all-gather.6.cloned.1.call-done), kind=kOutput, calls=%fused_computation.43 | convolution fusion | flops 3236364288 | bytes 54526976 | tf_op jit(solution)/shard_map/dot_general | solution.py:221
  756.2 17.5 %copy.152 = f32[8192,512]{1,0:T(8,128)} copy(f32[8192,512]{0,1:T(8,128)} %pad_maximum_fusion.1) | data formatting | bytes 33554432 | tf_op jit(solution)/shard_map/reshape | solution.py:227
  786.3 32.1 %fusion = f32[8,1024,512]{2,1,0:T(8,128)} fusion(pred[8,1024,1024]{2,1,0:T(32,128)(4,1)} %iota_compare_fusion, bf16[8,1024,512]{2,1,0:T(8,128)(2,1)} %get-tuple-element.35, bf16[8,1024,512]{2,1,0:T(8,128)(2,1)} %get-tuple-element.36, bf16[8,1024,512]{2,1,0:T(8,128)(2,1)S(1)} %get-tuple-element.34), kind=kOutput, calls=%fused_computation.1 | convolution fusion | flops 25895632896 | bytes 50331648 | tf_op jit(solution)/shard_map/gkb,gbc->gkc/dot_general | solution.py:152
  824.9 13.2 %fusion.21 = f32[64,128,256]{2,0,1:T(8,128)} fusion(f32[64,128,256]{2,1,0:T(8,128)S(1)} %bitcast.127), kind=kOutput, calls=%fused_computation.51 | convolution fusion | flops 1610670080 | bytes 16777216 | tf_op jit(solution)/shard_map/abm,ca->cbm/dot_general | solution.py:48
  838.0 13.6 %fusion.23 = f32[64,128,256]{2,0,1:T(8,128)} fusion(f32[64,128,256]{2,1,0:T(8,128)S(1)} %bitcast.128), kind=kOutput, calls=%fused_computation.53 | convolution fusion | flops 1610670080 | bytes 16777216 | tf_op jit(solution)/shard_map/abm,ca->cbm/dot_general | solution.py:53
  864.8 21.5 %multiply_subtract_fusion = (f32[64,128,256]{2,0,1:T(8,128)}, f32[64,128,256]{2,0,1:T(8,128)}) fusion(f32[64,128,256]{2,0,1:T(8,128)} %fusion.21, f32[64,128]{0,1:T(8,128)S(1)} %copy-done.13, f32[64,128]{0,1:T(8,128)S(1)} %copy-done.10, f32[64,128,256]{2,0,1:T(8,128)} %fusion.27, f32[64,128,256]{2,0,1:T(8,128)} %fusion.23, f32[64,128,256]{2,1,0:T(8,128)S(1)} %bitcast.130), kind=kOutput, calls=%fused_computation.40 | convolution fusion | flops 1631641600 | bytes 50397184 | tf_op jit(solution)/shard_map/abm,ca->cbm/dot_general | solution.py:46
  886.4 16.3 %fusion.17 = f32[128,64,256]{2,0,1:T(8,128)S(1)} fusion(f32[64,128,256]{2,0,1:T(8,128)} %get-tuple-element.25), kind=kOutput, calls=%fused_computation.34 | convolution fusion | flops 3221454848 | bytes 16777216 | tf_op jit(solution)/shard_map/cbm,db->dcm/dot_general | solution.py:48
  942.3 20.8 %fusion.52 = (f32[1024,1024]{0,1:T(8,128)}, f32[1024,1024]{0,1:T(8,128)}) fusion(f32[1024,1024]{0,1:T(8,128)} %mul.725, f32[1,1024,1024]{1,2,0:T(8,128)} %copy.154, f32[1024,1027]{0,1:T(8,128)} %slice.158, f32[1024,1027]{0,1:T(8,128)} %slice.156, f32[1,1024,1024]{1,2,0:T(8,128)} %copy.153), kind=kLoop, calls=%fused_computation.97 | loop fusion | flops 25165824 | bytes 54525952 | tf_op jit(solution)/shard_map/mul | solution.py:238
  1036.0 20.7 %add_bitcast_fusion.1 = (f32[1024,1024,1]{0,1,2:T(8,128)S(1)}, f32[1024,1024,1]{0,1,2:T(8,128)S(1)}) fusion(f32[1024,1024]{0,1:T(8,128)} %reshape.124, f32[1024,1024]{0,1:T(8,128)} %get-tuple-element.22, f32[1024,3]{0,1:T(4,128)S(1)} %get-tuple-element.47, f32[1024,3]{0,1:T(4,128)S(1)} %get-tuple-element.46), kind=kLoop, calls=%fused_computation.94 | loop fusion | flops 41943040 | bytes 16801792 | tf_op jit(solution)/shard_map/stack | solution.py:125
  1099.9 13.7 %fusion.16 = f32[1024,2048]{0,1:T(8,128)} fusion(f32[1024,2048]{0,1:T(8,128)} %copy.148, f32[1024,2048]{0,1:T(8,128)} %reshape.125, f32[1024,8,256]{0,2,1:T(8,128)} %copy.141), kind=kLoop, calls=%fused_computation.33 | loop fusion | flops 8388608 | bytes 33554432 | tf_op jit(solution)/shard_map/max | solution.py:248
  (144 shorter events, 379.9 us)
Async XLA Ops:
  7.2 495.9 %copy-start = (f32[128,128]{1,0:T(8,128)S(1)}, f32[128,128]{1,0:T(8,128)}, u32[]{:S(2)}) copy-start(f32[128,128]{1,0:T(8,128)} %param.13) | copy-start | bytes 196612
  16.5 5.4 copy-start.16
  16.5 100.1 %all-to-all-start = ((f32[1024,8,256]{0,2,1:T(8,128)}), f32[1024,8,256]{0,2,1:T(8,128)}, u32[]{:S(2)}, u32[]{:S(2)}) async-start(f32[1024,8,256]{0,2,1:T(8,128)} %bitcast.120), calls=%async_computation | async-start | bytes 16777216 | tf_op jit(solution)/shard_map/all_to_all | solution.py:169
  21.8 451.6 %reduce-scatter.3.cloned.1.call-start = ((), (), s32[]{:S(2)}) async-start(), calls=%async_computation.4 | async-start | bytes 9437184 | tf_op jit(solution)/shard_map/reduce_scatter | solution.py:204
  93.1 50.1 %copy-start.9 = (f32[64,128]{0,1:T(8,128)}, f32[64,128]{0,1:T(8,128)S(1)}, u32[]{:S(2)}) copy-start(f32[64,128]{0,1:T(8,128)S(1)} %get-tuple-element.55) | copy-start | bytes 98308
  161.8 17.5 %slice-start.4 = ((s8[8388608]{0:T(1024)(128)(4,1)}), s8[4194304]{0:T(1024)(128)(4,1)S(1)}, s32[]{:S(2)}) async-start(s8[8388608]{0:T(1024)(128)(4,1)} %bitcast.125), calls=%async_computation.12 | async-start | bytes 8388608
  161.8 17.5 %slice-start.5 = ((s8[8388608]{0:T(1024)(128)(4,1)}), s8[4194304]{0:T(1024)(128)(4,1)S(1)}, s32[]{:S(2)}) async-start(s8[8388608]{0:T(1024)(128)(4,1)} %bitcast.125), calls=%async_computation.13 | async-start | bytes 8388608
  233.0 8.4 copy-start.5
  336.6 17.2 %copy-start.2 = (f32[8192,256]{0,1:T(8,128)S(1)}, f32[8192,256]{0,1:T(8,128)}, u32[]{:S(2)}) copy-start(f32[8192,256]{0,1:T(8,128)} %get-tuple-element.29) | copy-start | bytes 25165828
  353.8 29.4 %slice-start = ((s8[8388608]{0:T(1024)(128)(4,1)}), s8[4194304]{0:T(1024)(128)(4,1)S(1)}, s32[]{:S(2)}) async-start(s8[8388608]{0:T(1024)(128)(4,1)} %bitcast.118), calls=%async_computation.8 | async-start | bytes 8388608
  368.4 14.8 %slice-start.1 = ((s8[8388608]{0:T(1024)(128)(4,1)}), s8[4194304]{0:T(1024)(128)(4,1)S(1)}, s32[]{:S(2)}) async-start(s8[8388608]{0:T(1024)(128)(4,1)} %bitcast.118), calls=%async_computation.9 | async-start | bytes 8388608
  401.8 101.2 %copy-start.14 = (f32[256,2,128]{2,1,0:T(2,128)S(1)}, f32[256,2,128]{2,1,0:T(2,128)}, u32[]{:S(2)}) copy-start(f32[256,2,128]{2,1,0:T(2,128)} %param.12) | copy-start | bytes 786436
  401.8 101.2 %copy-start.15 = (f32[256,2,128]{2,1,0:T(2,128)S(1)}, f32[256,2,128]{2,1,0:T(2,128)}, u32[]{:S(2)}) copy-start(f32[256,2,128]{2,1,0:T(2,128)} %param.10) | copy-start | bytes 786436
  401.8 176.2 %copy-start.12 = (s32[8192]{0:T(1024)S(1)}, s32[8192]{0:T(1024)}, u32[]{:S(2)}) copy-start(s32[8192]{0:T(1024)} %copy-done.11) | copy-start | bytes 98308
  401.8 101.2 %reduce-scatter.5.cloned.1.call-start = ((), (), s32[]{:S(2)}) async-start(), calls=%async_computation.5 | async-start | bytes 1310720 | tf_op jit(solution)/shard_map/reduce_scatter | solution.py:205
  473.4 101.8 %all-gather.4.cloned.1.call-start = ((), (), s32[]{:S(2)}) async-start(), calls=%async_computation.6 | async-start | bytes 1310720 | tf_op jit(solution)/shard_map/all_gather | solution.py:216
  547.2 144.8 %all-gather.6.cloned.1.call-start = ((), (), s32[]{:S(2)}) async-start(), calls=%async_computation.7 | async-start | bytes 9437184 | tf_op jit(solution)/shard_map/all_gather | solution.py:217
  576.0 19.4 %collective-permute-start = (f32[1024,6]{0,1:T(8,128)S(1)}, f32[1024,6]{0,1:T(8,128)S(1)}, u32[]{:S(2)}, u32[]{:S(2)}) collective-permute-start(f32[1024,6]{0,1:T(8,128)S(1)} %slice.204), channel_id=1, source_target_pairs={{1,0},{2,1},{3,2},{0,3},{5,4},{6,5},{7,6},{4,7},{9,8},{10,9},{11,1... | collective-permute-start | bytes 73736 | tf_op jit(solution)/shard_map/ppermute | solution.py:27
  578.0 17.4 %slice-start.2 = ((s8[8388608]{0:T(1024)(128)(4,1)}), s8[4194304]{0:T(1024)(128)(4,1)S(1)}, s32[]{:S(2)}) async-start(s8[8388608]{0:T(1024)(128)(4,1)} %bitcast.121), calls=%async_computation.10 | async-start | bytes 8388608
  586.7 8.7 slice-start.3
  653.2 13.8 %collective-permute-start.1 = (f32[1024,6]{0,1:T(8,128)S(1)}, f32[1024,6]{0,1:T(8,128)S(1)}, u32[]{:S(2)}, u32[]{:S(2)}) collective-permute-start(f32[1024,6]{0,1:T(8,128)S(1)} %slice.213), channel_id=1, source_target_pairs={{1,0},{2,1},{3,2},{0,3},{5,4},{6,5},{7,6},{4,7},{9,8},{10,9},{11,1... | collective-permute-start | bytes 73736 | tf_op jit(solution)/shard_map/ppermute | solution.py:27
  691.9 10.0 copy-start.3
  851.7 13.2 %copy-start.10 = (f32[64,128]{0,1:T(8,128)S(1)}, f32[64,128]{0,1:T(8,128)}, u32[]{:S(2)}) copy-start(f32[64,128]{0,1:T(8,128)} %copy-done.9) | copy-start | bytes 98308
  851.7 13.2 %copy-start.13 = (f32[64,128]{0,1:T(8,128)S(1)}, f32[64,128]{0,1:T(8,128)}, u32[]{:S(2)}) copy-start(f32[64,128]{0,1:T(8,128)} %fusion.147) | copy-start | bytes 98308
  886.4 16.3 %slice-start.6 = ((s8[8388608]{0:T(1024)(128)(4,1)}), s8[4194304]{0:T(1024)(128)(4,1)S(1)}, s32[]{:S(2)}) async-start(s8[8388608]{0:T(1024)(128)(4,1)} %bitcast.135), calls=%async_computation.14 | async-start | bytes 8388608
  886.4 16.3 %slice-start.7 = ((s8[8388608]{0:T(1024)(128)(4,1)}), s8[4194304]{0:T(1024)(128)(4,1)S(1)}, s32[]{:S(2)}) async-start(s8[8388608]{0:T(1024)(128)(4,1)} %bitcast.135), calls=%async_computation.15 | async-start | bytes 8388608
  922.9 5.1 copy-start.4
  922.9 160.4 %all-to-all-start.1 = ((f32[8,1024,256]{2,1,0:T(8,128)}), f32[8,1024,256]{2,1,0:T(8,128)}, u32[]{:S(2)}, u32[]{:S(2)}) async-start(f32[8,1024,256]{2,1,0:T(8,128)} %bitcast.134), calls=%async_computation.3 | async-start | bytes 16777216 | tf_op jit(solution)/shard_map/all_to_all | solution.py:231
  994.1 9.7 collective-permute-start.2
  1018.1 17.9 %collective-permute-start.3 = (f32[2,1024,3]{1,2,0:T(4,128)S(1)}, f32[2,1024,3]{1,2,0:T(4,128)S(1)}, u32[]{:S(2)}, u32[]{:S(2)}) collective-permute-start(f32[2,1024,3]{1,2,0:T(4,128)S(1)} %pad_maximum_fusion.12), channel_id=1, source_target_pairs={{3,0},{0,1},{1,2},{2,3},{7,4},{4,5},{5,6},{6,7},{11,8},{8,9},{9,10... | collective-permute-start | bytes 73736 | tf_op jit(solution)/shard_map/ppermute | solution.py:27
  1071.3 11.0 copy-start.8
  1099.9 22.8 %copy-start.1 = (f32[128,128]{1,0:T(8,128)S(1)}, f32[128,128]{1,0:T(8,128)}, u32[]{:S(2)}) copy-start(f32[128,128]{1,0:T(8,128)} %param.13) | copy-start | bytes 196612
  (3 other events, 3.3 us)
Sparse Core Ops, SparseCore 0:
  401.9 71.4 reduce-scatter.2
  475.7 27.2 reduce-scatter.4
  547.3 27.9 all-gather.3
  577.0 53.6 all-gather.5

commit v6 on v5

--- a/solution.py
+++ b/solution.py
@@ -194,14 +194,22 @@
     picked_imag = picked[:, chunk:]
     twisted_real = picked_real * band_cos + picked_imag * band_sin
     twisted_imag = picked_imag * band_cos - picked_real * band_sin
-    part_real = jnp.dot(twisted_real, cell_cos, precision=precise) + jnp.dot(
-        twisted_imag, cell_sin, precision=precise
-    )
-    part_imag = jnp.dot(twisted_imag, cell_cos, precision=precise) - jnp.dot(
-        twisted_real, cell_sin, precision=precise
-    )
-    partial = jnp.stack([part_real, part_imag], axis=1)
-    partial = lax.psum_scatter(partial, "vis", scatter_dimension=0, tiled=True)
+    group_size = total_blocks // n_vis
+    halves = []
+    for half in range(2):
+        lo = half * (group_size // 2)
+        hi = lo + group_size // 2
+        half_real = twisted_real.reshape(n_vis, group_size, chunk)[:, lo:hi].reshape(-1, chunk)
+        half_imag = twisted_imag.reshape(n_vis, group_size, chunk)[:, lo:hi].reshape(-1, chunk)
+        part_real = jnp.dot(half_real, cell_cos, precision=precise) + jnp.dot(
+            half_imag, cell_sin, precision=precise
+        )
+        part_imag = jnp.dot(half_imag, cell_cos, precision=precise) - jnp.dot(
+            half_real, cell_sin, precision=precise
+        )
+        partial = jnp.stack([part_real, part_imag], axis=1)
+        halves.append(lax.psum_scatter(partial, "vis", scatter_dimension=0, tiled=True))
+    partial = jnp.concatenate(halves, axis=0)
     chosen = lax.psum_scatter(partial, "tile", scatter_dimension=0, tiled=True) * norm_scale
     model = jnp.einsum("ij,csj->csi", kernel, chosen, precision=precise)
     live_mask = (jnp.arange(slot_count, dtype=jnp.int32) < live_blocks[0]).astype(jnp.float32)[

time: 1140 us -> 1090 us (0.956)
  matrix products: 345 us -> 318 us
  local copies, waits for them, and re-layouts: 310 us -> 283 us
    dot_general x4 -> x8, matrix products: 61.1 us -> 35.5 us  [the longest x2 10.7 us: on_device(): jnp.dot(half_real, cell_cos, precision=precise)]
    gather x2 -> x1, local copies, waits for them, and re-layouts: 58.2 us -> 40.6 us  [on_device(): jnp.take(jnp.concatenate([spec_real, spec_imag], axis=1), row_of, axis=0)]
    reshape x1 -> x0, local copies, waits for them, and re-layouts: 17.5 us -> none  [on_device(): turned = turned.reshape(n_vis, total_blocks // n_vis, 2 * chunk)]
    reduce_scatter x1 -> x2, waiting for transfers between devices: 71.5 us -> 84.6 us  [on_device(): lax.psum_scatter(partial, 'vis', scatter_dimension=0, tiled=True)]
    unnamed x57 -> x55, local copies, waits for them, and re-layouts: 51.7 us -> 51.7 us
  transfers between devices with their start and end apart: 10 -> 11, of which waited for: 4 -> 5; matrix products, arithmetic and copies ran while one was open for 24% -> 27% of each run, Pallas kernels for 0% -> 0%
where the time goes in v6:
time: 1090 us; the launch traced here: 1080 us
  matrix products  318 us (29%)
  local copies, waits for them, and re-layouts  283 us (26%)
  other arithmetic  182 us (17%)
  waiting for transfers between devices  153 us (14%)
  blocking collectives  110 us (10%)
  between operations  16.6 us (2%)
  starting transfers between devices  15 us (1%)
    reduce_scatter x2, waiting for transfers between devices, on_device(): lax.psum_scatter(partial, 'vis', scatter_dimension=0, tiled=True)  84.6 us
    all_gather x1, blocking collectives, on_device(): lax.all_gather(block_index.astype(jnp.float32), ('vis', 'tile'), tiled=True)  70.9 us
    dot_general x4, matrix products, complex_einsum(): real_part = jnp.einsum(form, left_real, table_cos, precision=precise)  68.3 us
    slice x4, local copies, waits for them, and re-layouts, analyse_local(): lax.slice_in_dim(extended, parity, extended.shape[1], 2, 1)  58.1 us
    unnamed x55, local copies, waits for them, and re-layouts  51.7 us
    dot_general x3, matrix products, complex_einsum(): imag_part = jnp.einsum(form, left_real, table_sin, precision=precise)  45.8 us
    dot_general x3, matrix products, complex_einsum(): jnp.einsum(form, left_imag, table_sin, precision=precise)  43.1 us
    gather x1, local copies, waits for them, and re-layouts, on_device(): jnp.take(jnp.concatenate([spec_real, spec_imag], axis=1), row_of, axis=0)  40.6 us
  transfers between devices with their start and end apart: 11, of which 5 were waited for; matrix products, arithmetic and copies ran while one was open for 27% of the time, Pallas kernels for 0%

profile of v6, /device:TPU:0, one launch (start us, length us, event | category | flops | bytes accessed | tf_op | source)
XLA Modules:
  0.0 1078.2 jit_solution(15011735406753505240)
XLA Ops:
  21.9 70.9 %all-gather = f32[32,1,256]{2,1,0:T(1,128)S(1)} all-gather(f32[1,1,256]{2,1,0:T(1,128)S(1)} %bitcast.162), channel_id=1, replica_groups=mesh['vis'=8,'tile'=4] {'vis','tile'}, dimensions={0}, use_global_device_ids=true | all-gather | bytes 33792 | tf_op jit(solution)/shard_map/all_gather | solution.py:171
  102.7 13.8 %all-to-all-done = f32[1024,8,256]{0,2,1:T(8,128)} async-done(((f32[1024,8,256]{0,2,1:T(8,128)}), f32[1024,8,256]{0,2,1:T(8,128)}, u32[]{:S(2)}, u32[]{:S(2)}) %all-to-all-start) | async-done | bytes 8388640 | tf_op jit(solution)/shard_map/all_to_all | solution.py:169
  125.8 17.6 %fusion.35 = f32[64,128,256]{2,0,1:T(8,128)} fusion(f32[64,128,256]{2,1,0:T(8,128)} %bitcast.135), kind=kOutput, calls=%fused_computation.62 | convolution fusion | flops 1610670080 | bytes 16777216 | tf_op jit(solution)/shard_map/abm,ca->cbm/dot_general | solution.py:46
  143.4 18.3 %multiply_subtract_fusion.3 = (f32[64,128,256]{2,0,1:T(8,128)S(1)}, f32[64,128,256]{2,0,1:T(8,128)}) fusion(f32[64,128,256]{2,0,1:T(8,128)} %fusion.35, f32[64,128]{0,1:T(8,128)S(1)} %get-tuple-element.58, f32[64,128]{0,1:T(8,128)S(1)} %get-tuple-element.59, f32[64,128,256]{2,1,0:T(8,128)} %bitcast.136), kind=kOutput, calls=%fused_computation.44 | convolution fusion | flops 1627451392 | bytes 33619968 | tf_op jit(solution)/shard_map/abm,ca->cbm/dot_general | solution.py:51
  161.7 17.7 %fusion.29 = f32[128,64,256]{2,0,1:T(8,128)} fusion(f32[64,128,256]{2,0,1:T(8,128)} %get-tuple-element.31), kind=kOutput, calls=%fused_computation.56 | convolution fusion | flops 3221454848 | bytes 16777216 | tf_op jit(solution)/shard_map/cbm,db->dcm/dot_general | solution.py:53
  179.5 13.6 %fusion.27 = f32[128,64,256]{2,0,1:T(8,128)} fusion(f32[64,128,256]{2,0,1:T(8,128)S(1)} %copy-done.2), kind=kOutput, calls=%fused_computation.54 | convolution fusion | flops 3221471232 | bytes 16777216 | tf_op jit(solution)/shard_map/cbm,db->dcm/dot_general | solution.py:48
  193.0 14.3 %fusion.57 = f32[128,64,256]{2,0,1:T(8,128)S(1)} fusion(f32[128,64,256]{2,0,1:T(8,128)} %fusion.29, f32[64,128,256]{2,0,1:T(8,128)S(1)} %get-tuple-element.30), kind=kOutput, calls=%fused_computation.106 | convolution fusion | flops 3223568384 | bytes 25165824 | tf_op jit(solution)/shard_map/cbm,db->dcm/dot_general | solution.py:51
  215.6 17.3 %subtract_add_fusion.1 = f32[128,64,256]{2,0,1:T(8,128)} fusion(f32[128,64,256]{2,0,1:T(8,128)} %fusion.27, f32[128,64,256]{2,0,1:T(8,128)S(1)} %fusion.57, f32[64,128,256]{2,0,1:T(8,128)S(1)} %get-tuple-element.30), kind=kOutput, calls=%fused_computation.42 | convolution fusion | flops 3227746304 | bytes 33554432 | tf_op jit(solution)/shard_map/cbm,db->dcm/dot_general | solution.py:46
  247.6 40.6 %gather_fusion = f32[8192,512]{1,0:T(8,128)} fusion(f32[8192,512]{1,0:T(8,128)} %pad_maximum_fusion, s32[8192]{0:T(1024)S(1)} %broadcast_clamp_fusion), kind=kCustom, calls=%fused_computation | custom fusion | bytes 33587200 | tf_op jit(solution)/shard_map/jit(_take)/gather | solution.py:192
  288.2 11.5 %broadcast_select_fusion = f32[8192,512]{1,0:T(8,128)} fusion(f32[8192,512]{1,0:T(8,128)} %gather_fusion, pred[8192]{0:T(1024)(128)(4,1)S(1)} %get-tuple-element.20), kind=kLoop, calls=%fused_computation.41 | loop fusion | flops 4194304 | bytes 33562624 | tf_op jit(solution)/shard_map/jit(_take)/select_n | solution.py:192
  299.7 18.4 %multiply_add_fusion.2 = (f32[8192,256]{1,0:T(8,128)}, f32[8192,256]{1,0:T(8,128)}) fusion(f32[8192,512]{1,0:T(8,128)} %broadcast_select_fusion, f32[8192,512]{1,0:T(8,128)} %fusion.39), kind=kLoop, calls=%fused_computation.40 | loop fusion | flops 12582912 | bytes 50331648 | tf_op jit(solution)/shard_map/add | solution.py:195
  367.3 29.5 %reduce-scatter.4.cloned.1.call-done = f32[512,2,128]{2,0,1:T(8,128)} async-done(((f32[4096,2,128]{2,0,1:T(8,128)}), f32[512,2,128]{2,0,1:T(8,128)}) %reduce-scatter.4.cloned.1.call-update) | async-done | bytes 524304 | tf_op jit(solution)/shard_map/reduce_scatter | solution.py:211
  396.8 55.1 %reduce-scatter.6.cloned.1.call-done = f32[512,2,128]{2,0,1:T(8,128)} async-done(((f32[4096,2,128]{2,0,1:T(8,128)}), f32[512,2,128]{2,0,1:T(8,128)}) %reduce-scatter.6.cloned.1.call-update) | async-done | bytes 524304 | tf_op jit(solution)/shard_map/reduce_scatter | solution.py:211
  455.5 26.6 %reduce-scatter.8.cloned.1.call-done = f32[256,2,128]{2,0,1:T(8,128)} async-done(((f32[1024,2,128]{2,0,1:T(8,128)}), f32[256,2,128]{2,0,1:T(8,128)}) %reduce-scatter.8.cloned.1.call-update) | async-done | bytes 262160 | tf_op jit(solution)/shard_map/reduce_scatter | solution.py:213
  484.1 38.9 %all-reduce = (f32[]{:T(128)}, f32[]{:T(128)}) all-reduce(f32[]{:T(128)} %fusion.185, f32[]{:T(128)} %get-tuple-element.54), channel_id=1, replica_groups=mesh['vis'=8,'tile'=4] {'vis','tile'}, use_global_device_ids=true, to_apply=%region_4.5 | all-reduce | flops 2 | bytes 16 | tf_op jit(solution)/shard_map/psum | solution.py:219
  526.3 28.1 %all-gather.4.cloned.1.call-done = f32[1024,2,128]{2,0,1:T(8,128)} async-done(((f32[256,2,128]{2,0,1:T(8,128)}), f32[1024,2,128]{2,0,1:T(8,128)}) %all-gather.4.cloned.1.call-update) | async-done | bytes 1048592 | tf_op jit(solution)/shard_map/all_gather | solution.py:224
  578.4 19.1 %slice.172 = f32[1024,1027]{0,1:T(8,128)} slice(f32[1024,2054]{0,1:T(8,128)} %pad_maximum_fusion.2), slice={[0:1024:1], [0:2054:2]} | slice | bytes 8413184 | tf_op jit(solution)/shard_map/slice | solution.py:102
  597.5 18.8 %slice.174 = f32[1024,1027]{0,1:T(8,128)} slice(f32[1024,2054]{0,1:T(8,128)} %pad_maximum_fusion.2), slice={[0:1024:1], [1:2054:2]} | slice | bytes 8413184 | tf_op jit(solution)/shard_map/slice | solution.py:102
  616.3 13.5 %multiply_add_fusion.5 = f32[1024,1024]{0,1:T(8,128)S(1)} fusion(f32[1024,1027]{0,1:T(8,128)} %slice.174, f32[1024,1027]{0,1:T(8,128)} %slice.172), kind=kLoop, calls=%fused_computation.103 | loop fusion | flops 15728640 | bytes 37748736 | tf_op jit(solution)/shard_map/add | solution.py:108
  690.2 11.1 %convolution_subtract_fusion = f32[8192,256]{1,0:T(8,128)} fusion(f32[8192,256]{1,0:T(8,128)S(1)} %fusion.56, f32[8192,2,128]{2,0,1:T(8,128)S(1)} %copy-done.3, s32[256]{0:T(256)S(1)} %iota_add_fusion), kind=kOutput, calls=%fused_computation.21 | convolution fusion | flops 3223781376 | bytes 20972544 | tf_op jit(solution)/shard_map/dot_general | solution.py:226
  701.2 19.7 %multiply_subtract_fusion.1 = (f32[8192,256]{1,0:T(8,128)}, f32[8192,256]{1,0:T(8,128)}) fusion(f32[8192,256]{1,0:T(8,128)} %convolution_subtract_fusion, f32[8192,512]{1,0:T(8,128)} %fusion.39, f32[8192,256]{1,0:T(8,128)} %fusion.55, s32[256]{0:T(256)S(1)} %iota_add_fusion, f32[8192,2,128]{2,0,1:T(8,128)} %all-gather.6.cloned.1.call-done), kind=kOutput, calls=%fused_computation.38 | convolution fusion | flops 3236364288 | bytes 54526976 | tf_op jit(solution)/shard_map/dot_general | solution.py:229
  735.6 32.3 %fusion = f32[8,1024,512]{2,1,0:T(8,128)} fusion(pred[8,1024,1024]{2,1,0:T(32,128)(4,1)} %iota_compare_fusion, bf16[8,1024,512]{2,1,0:T(8,128)(2,1)} %get-tuple-element.35, bf16[8,1024,512]{2,1,0:T(8,128)(2,1)} %get-tuple-element.36, bf16[8,1024,512]{2,1,0:T(8,128)(2,1)S(1)} %get-tuple-element.34), kind=kOutput, calls=%fused_computation.1 | convolution fusion | flops 25895632896 | bytes 50331648 | tf_op jit(solution)/shard_map/gkb,gbc->gkc/dot_general | solution.py:152
  774.3 13.2 %fusion.19 = f32[64,128,256]{2,0,1:T(8,128)} fusion(f32[64,128,256]{2,1,0:T(8,128)S(1)} %bitcast.137), kind=kOutput, calls=%fused_computation.46 | convolution fusion | flops 1610670080 | bytes 16777216 | tf_op jit(solution)/shard_map/abm,ca->cbm/dot_general | solution.py:48
  787.4 13.3 %fusion.21 = f32[64,128,256]{2,0,1:T(8,128)} fusion(f32[64,128,256]{2,1,0:T(8,128)S(1)} %bitcast.138), kind=kOutput, calls=%fused_computation.48 | convolution fusion | flops 1610670080 | bytes 16777216 | tf_op jit(solution)/shard_map/abm,ca->cbm/dot_general | solution.py:53
  800.8 13.2 %fusion.25 = f32[64,128,256]{2,0,1:T(8,128)} fusion(f32[64,128,256]{2,1,0:T(8,128)S(1)} %bitcast.139), kind=kOutput, calls=%fused_computation.52 | convolution fusion | flops 1610670080 | bytes 16777216 | tf_op jit(solution)/shard_map/abm,ca->cbm/dot_general | solution.py:51
  813.9 21.6 %multiply_subtract_fusion = (f32[64,128,256]{2,0,1:T(8,128)}, f32[64,128,256]{2,0,1:T(8,128)}) fusion(f32[64,128,256]{2,0,1:T(8,128)} %fusion.19, f32[64,128]{0,1:T(8,128)S(1)} %copy-done.16, f32[64,128]{0,1:T(8,128)S(1)} %copy-done.13, f32[64,128,256]{2,0,1:T(8,128)} %fusion.25, f32[64,128,256]{2,0,1:T(8,128)} %fusion.21, f32[64,128,256]{2,1,0:T(8,128)S(1)} %bitcast.140), kind=kOutput, calls=%fused_computation.35 | convolution fusion | flops 1631641600 | bytes 50397184 | tf_op jit(solution)/shard_map/abm,ca->cbm/dot_general | solution.py:46
  835.5 16.3 %fusion.15 = f32[128,64,256]{2,0,1:T(8,128)S(1)} fusion(f32[64,128,256]{2,0,1:T(8,128)} %get-tuple-element.25), kind=kOutput, calls=%fused_computation.29 | convolution fusion | flops 3221454848 | bytes 16777216 | tf_op jit(solution)/shard_map/cbm,db->dcm/dot_general | solution.py:48
  851.9 11.8 %fusion.62 = f32[128,64,256]{2,0,1:T(8,128)S(1)} fusion(f32[128,64,256]{2,0,1:T(8,128)S(1)} %fusion.15, f32[64,128,256]{2,0,1:T(8,128)S(1)} %copy-done.7), kind=kOutput, calls=%fused_computation.107 | convolution fusion | flops 3223552000 | bytes 25165824 | tf_op jit(solution)/shard_map/cbm,db->dcm/dot_general | solution.py:46
  891.7 20.8 %fusion.54 = (f32[1024,1024]{0,1:T(8,128)}, f32[1024,1024]{0,1:T(8,128)}) fusion(f32[1024,1024]{0,1:T(8,128)} %mul.725, f32[1,1024,1024]{1,2,0:T(8,128)} %copy.162, f32[1024,1027]{0,1:T(8,128)} %slice.174, f32[1024,1027]{0,1:T(8,128)} %slice.172, f32[1,1024,1024]{1,2,0:T(8,128)} %copy.161), kind=kLoop, calls=%fused_computation.102 | loop fusion | flops 25165824 | bytes 54525952 | tf_op jit(solution)/shard_map/mul | solution.py:246
  985.3 20.2 %add_bitcast_fusion.1 = (f32[1024,1024,1]{0,1,2:T(8,128)S(1)}, f32[1024,1024,1]{0,1,2:T(8,128)S(1)}) fusion(f32[1024,1024]{0,1:T(8,128)} %reshape.150, f32[1024,1024]{0,1:T(8,128)} %get-tuple-element.22, f32[1024,3]{0,1:T(4,128)S(1)} %get-tuple-element.51, f32[1024,3]{0,1:T(4,128)S(1)} %get-tuple-element.50), kind=kLoop, calls=%fused_computation.99 | loop fusion | flops 41943040 | bytes 16801792 | tf_op jit(solution)/shard_map/stack | solution.py:125
  1007.2 13.0 %copy.152 = f32[1024,1024,2]{0,2,1:T(2,128)} copy(f32[1024,1024,2]{0,1,2:T(8,128)S(1)} %pad_maximum_fusion.3) | data formatting | bytes 16777216 | tf_op jit(solution)/shard_map/stack | solution.py:125
  1048.6 13.6 %fusion.14 = f32[1024,2048]{0,1:T(8,128)} fusion(f32[1024,2048]{0,1:T(8,128)} %copy.153, f32[1024,2048]{0,1:T(8,128)} %reshape.151, f32[1024,8,256]{0,2,1:T(8,128)} %copy.146), kind=kLoop, calls=%fused_computation.28 | loop fusion | flops 8388608 | bytes 33554432 | tf_op jit(solution)/shard_map/max | solution.py:256
  (149 shorter events, 357.9 us)
Async XLA Ops:
  7.2 474.9 %copy-start = (f32[128,128]{1,0:T(8,128)S(1)}, f32[128,128]{1,0:T(8,128)}, u32[]{:S(2)}) copy-start(f32[128,128]{1,0:T(8,128)} %param.13) | copy-start | bytes 196612
  16.5 5.4 copy-start.19
  16.5 100.1 %all-to-all-start = ((f32[1024,8,256]{0,2,1:T(8,128)}), f32[1024,8,256]{0,2,1:T(8,128)}, u32[]{:S(2)}, u32[]{:S(2)}) async-start(f32[1024,8,256]{0,2,1:T(8,128)} %bitcast.132), calls=%async_computation | async-start | bytes 16777216 | tf_op jit(solution)/shard_map/all_to_all | solution.py:169
  21.8 375.0 %reduce-scatter.4.cloned.1.call-start = ((), (), s32[]{:S(2)}) async-start(), calls=%async_computation.5 | async-start | bytes 4718592 | tf_op jit(solution)/shard_map/reduce_scatter | solution.py:211
  93.1 50.3 %copy-start.12 = (f32[64,128]{0,1:T(8,128)}, f32[64,128]{0,1:T(8,128)S(1)}, u32[]{:S(2)}) copy-start(f32[64,128]{0,1:T(8,128)S(1)} %get-tuple-element.59) | copy-start | bytes 98308
  161.7 17.7 %copy-start.2 = (f32[64,128,256]{2,0,1:T(8,128)S(1)}, f32[64,128,256]{2,0,1:T(8,128)}, u32[]{:S(2)}) copy-start(f32[64,128,256]{2,0,1:T(8,128)} %get-tuple-element.31) | copy-start | bytes 25165828
  232.9 8.4 copy-start.8
  318.2 10.3 slice-start.2
  318.2 10.3 slice-start.3
  345.5 106.4 %reduce-scatter.6.cloned.1.call-start = ((), (), s32[]{:S(2)}) async-start(), calls=%async_computation.6 | async-start | bytes 4718592 | tf_op jit(solution)/shard_map/reduce_scatter | solution.py:211
  345.5 6.7 copy-start.6
  356.3 4.1 copy-start.5
  367.2 114.9 %copy-start.17 = (f32[256,2,128]{2,1,0:T(2,128)S(1)}, f32[256,2,128]{2,1,0:T(2,128)}, u32[]{:S(2)}) copy-start(f32[256,2,128]{2,1,0:T(2,128)} %param.12) | copy-start | bytes 786436
  367.2 114.9 %copy-start.18 = (f32[256,2,128]{2,1,0:T(2,128)S(1)}, f32[256,2,128]{2,1,0:T(2,128)}, u32[]{:S(2)}) copy-start(f32[256,2,128]{2,1,0:T(2,128)} %param.10) | copy-start | bytes 786436
  367.3 189.7 %copy-start.15 = (s32[8192]{0:T(1024)S(1)}, s32[8192]{0:T(1024)}, u32[]{:S(2)}) copy-start(s32[8192]{0:T(1024)} %copy-done.14) | copy-start | bytes 98308
  367.3 114.8 %reduce-scatter.8.cloned.1.call-start = ((), (), s32[]{:S(2)}) async-start(), calls=%async_computation.7 | async-start | bytes 1310720 | tf_op jit(solution)/shard_map/reduce_scatter | solution.py:213
  454.2 100.2 %all-gather.4.cloned.1.call-start = ((), (), s32[]{:S(2)}) async-start(), calls=%async_computation.8 | async-start | bytes 1310720 | tf_op jit(solution)/shard_map/all_gather | solution.py:224
  526.2 143.9 %all-gather.6.cloned.1.call-start = ((), (), s32[]{:S(2)}) async-start(), calls=%async_computation.9 | async-start | bytes 9437184 | tf_op jit(solution)/shard_map/all_gather | solution.py:225
  555.1 19.0 %collective-permute-start = (f32[1024,6]{0,1:T(8,128)S(1)}, f32[1024,6]{0,1:T(8,128)S(1)}, u32[]{:S(2)}, u32[]{:S(2)}) collective-permute-start(f32[1024,6]{0,1:T(8,128)S(1)} %slice.224), channel_id=1, source_target_pairs={{1,0},{2,1},{3,2},{0,3},{5,4},{6,5},{7,6},{4,7},{9,8},{10,9},{11,1... | collective-permute-start | bytes 73736 | tf_op jit(solution)/shard_map/ppermute | solution.py:27
  556.9 17.2 %slice-start = ((s8[8388608]{0:T(1024)(128)(4,1)}), s8[4194304]{0:T(1024)(128)(4,1)S(1)}, s32[]{:S(2)}) async-start(s8[8388608]{0:T(1024)(128)(4,1)} %bitcast.133), calls=%async_computation.10 | async-start | bytes 8388608
  565.6 8.5 slice-start.1
  631.8 13.4 %collective-permute-start.1 = (f32[1024,6]{0,1:T(8,128)S(1)}, f32[1024,6]{0,1:T(8,128)S(1)}, u32[]{:S(2)}, u32[]{:S(2)}) collective-permute-start(f32[1024,6]{0,1:T(8,128)S(1)} %slice.233), channel_id=1, source_target_pairs={{1,0},{2,1},{3,2},{0,3},{5,4},{6,5},{7,6},{4,7},{9,8},{10,9},{11,1... | collective-permute-start | bytes 73736 | tf_op jit(solution)/shard_map/ppermute | solution.py:27
  670.1 10.0 copy-start.3
  800.8 13.2 %copy-start.13 = (f32[64,128]{0,1:T(8,128)S(1)}, f32[64,128]{0,1:T(8,128)}, u32[]{:S(2)}) copy-start(f32[64,128]{0,1:T(8,128)} %copy-done.12) | copy-start | bytes 98308
  800.8 13.2 %copy-start.16 = (f32[64,128]{0,1:T(8,128)S(1)}, f32[64,128]{0,1:T(8,128)}, u32[]{:S(2)}) copy-start(f32[64,128]{0,1:T(8,128)} %fusion.155) | copy-start | bytes 98308
  835.5 16.4 %copy-start.7 = (f32[64,128,256]{2,0,1:T(8,128)S(1)}, f32[64,128,256]{2,0,1:T(8,128)}, u32[]{:S(2)}) copy-start(f32[64,128,256]{2,0,1:T(8,128)} %get-tuple-element.24) | copy-start | bytes 25165828
  872.0 5.1 copy-start.4
  872.0 160.0 %all-to-all-start.1 = ((f32[8,1024,256]{2,1,0:T(8,128)}), f32[8,1024,256]{2,1,0:T(8,128)}, u32[]{:S(2)}, u32[]{:S(2)}) async-start(f32[8,1024,256]{2,1,0:T(8,128)} %bitcast.152), calls=%async_computation.4 | async-start | bytes 16777216 | tf_op jit(solution)/shard_map/all_to_all | solution.py:239
  943.5 9.7 collective-permute-start.2
  967.4 17.9 %collective-permute-start.3 = (f32[2,1024,3]{1,2,0:T(4,128)S(1)}, f32[2,1024,3]{1,2,0:T(4,128)S(1)}, u32[]{:S(2)}, u32[]{:S(2)}) collective-permute-start(f32[2,1024,3]{1,2,0:T(4,128)S(1)} %pad_maximum_fusion.14), channel_id=1, source_target_pairs={{3,0},{0,1},{1,2},{2,3},{7,4},{4,5},{5,6},{6,7},{11,8},{8,9},{9,10... | collective-permute-start | bytes 73736 | tf_op jit(solution)/shard_map/ppermute | solution.py:27
  1020.1 11.0 %copy-start.11 = (f32[256,2,128]{2,0,1:T(8,128)S(1)}, f32[256,2,128]{2,0,1:T(8,128)}, u32[]{:S(2)}) copy-start(f32[256,2,128]{2,0,1:T(8,128)} %copy-done.10) | copy-start | bytes 786436
  1062.2 9.2 copy-start.1
  (3 other events, 3.3 us)
Sparse Core Ops, SparseCore 0:
  345.6 51.1 reduce-scatter.3
  400.8 51.1 reduce-scatter.5
  454.8 27.2 reduce-scatter.7
  526.4 27.9 all-gather.3
  556.1 53.6 all-gather.5

commit v7 on v6

--- a/solution.py
+++ b/solution.py
@@ -196,9 +196,10 @@
     twisted_imag = picked_imag * band_cos - picked_real * band_sin
     group_size = total_blocks // n_vis
     halves = []
-    for half in range(2):
-        lo = half * (group_size // 2)
-        hi = lo + group_size // 2
+    pieces_count = 4
+    for half in range(pieces_count):
+        lo = half * (group_size // pieces_count)
+        hi = lo + group_size // pieces_count
         half_real = twisted_real.reshape(n_vis, group_size, chunk)[:, lo:hi].reshape(-1, chunk)
         half_imag = twisted_imag.reshape(n_vis, group_size, chunk)[:, lo:hi].reshape(-1, chunk)
         part_real = jnp.dot(half_real, cell_cos, precision=precise) + jnp.dot(

time: 1090 us -> 1150 us (1.055)
  waiting for transfers between devices: 153 us -> 206 us
    reduce_scatter x2 -> x4, waiting for transfers between devices: 84.6 us -> 138 us  [on_device(): lax.psum_scatter(partial, 'vis', scatter_dimension=0, tiled=True)]
    unnamed x55 -> x61, local copies, waits for them, and re-layouts: 51.7 us -> 51.3 us
  transfers between devices with their start and end apart: 11 -> 13, of which waited for: 5 -> 7; matrix products, arithmetic and copies ran while one was open for 27% -> 27% of each run, Pallas kernels for 0% -> 0%
where the time goes in v7:
time: 1150 us; the launch traced here: 1140 us
  matrix products  324 us (28%)
  local copies, waits for them, and re-layouts  284 us (25%)
  waiting for transfers between devices  206 us (18%)
  other arithmetic  183 us (16%)
  blocking collectives  110 us (10%)
  between operations  17 us (1%)
  starting transfers between devices  16.3 us (1%)
    reduce_scatter x4, waiting for transfers between devices, on_device(): lax.psum_scatter(partial, 'vis', scatter_dimension=0, tiled=True)  138 us
    all_gather x1, blocking collectives, on_device(): lax.all_gather(block_index.astype(jnp.float32), ('vis', 'tile'), tiled=True)  70.9 us
    dot_general x4, matrix products, complex_einsum(): real_part = jnp.einsum(form, left_real, table_cos, precision=precise)  68.4 us
    slice x4, local copies, waits for them, and re-layouts, analyse_local(): lax.slice_in_dim(extended, parity, extended.shape[1], 2, 1)  58.1 us
    unnamed x61, local copies, waits for them, and re-layouts  51.3 us
    dot_general x3, matrix products, complex_einsum(): imag_part = jnp.einsum(form, left_real, table_sin, precision=precise)  45.8 us
    dot_general x3, matrix products, complex_einsum(): jnp.einsum(form, left_imag, table_sin, precision=precise)  42.8 us
    gather x1, local copies, waits for them, and re-layouts, on_device(): jnp.take(jnp.concatenate([spec_real, spec_imag], axis=1), row_of, axis=0)  40.7 us
  transfers between devices with their start and end apart: 13, of which 7 were waited for; matrix products, arithmetic and copies ran while one was open for 27% of the time, Pallas kernels for 0%

profile of v7, /device:TPU:0, one launch (start us, length us, event | category | flops | bytes accessed | tf_op | source)
XLA Modules:
  0.0 1140.2 jit_solution(7321088688189134987)
XLA Ops:
  21.9 70.9 %all-gather = f32[32,1,256]{2,1,0:T(1,128)S(1)} all-gather(f32[1,1,256]{2,1,0:T(1,128)S(1)} %bitcast.190), channel_id=1, replica_groups=mesh['vis'=8,'tile'=4] {'vis','tile'}, dimensions={0}, use_global_device_ids=true | all-gather | bytes 33792 | tf_op jit(solution)/shard_map/all_gather | solution.py:171
  102.2 14.4 %all-to-all-done = f32[1024,8,256]{0,2,1:T(8,128)} async-done(((f32[1024,8,256]{0,2,1:T(8,128)}), f32[1024,8,256]{0,2,1:T(8,128)}, u32[]{:S(2)}, u32[]{:S(2)}) %all-to-all-start) | async-done | bytes 8388640 | tf_op jit(solution)/shard_map/all_to_all | solution.py:169
  125.8 17.6 %fusion.35 = f32[64,128,256]{2,0,1:T(8,128)} fusion(f32[64,128,256]{2,1,0:T(8,128)} %bitcast.155), kind=kOutput, calls=%fused_computation.62 | convolution fusion | flops 1610670080 | bytes 16777216 | tf_op jit(solution)/shard_map/abm,ca->cbm/dot_general | solution.py:46
  143.4 18.3 %multiply_subtract_fusion.3 = (f32[64,128,256]{2,0,1:T(8,128)S(1)}, f32[64,128,256]{2,0,1:T(8,128)}) fusion(f32[64,128,256]{2,0,1:T(8,128)} %fusion.35, f32[64,128]{0,1:T(8,128)S(1)} %get-tuple-element.62, f32[64,128]{0,1:T(8,128)S(1)} %get-tuple-element.63, f32[64,128,256]{2,1,0:T(8,128)} %bitcast.156), kind=kOutput, calls=%fused_computation.44 | convolution fusion | flops 1627451392 | bytes 33619968 | tf_op jit(solution)/shard_map/abm,ca->cbm/dot_general | solution.py:51
  161.7 17.7 %fusion.29 = f32[128,64,256]{2,0,1:T(8,128)} fusion(f32[64,128,256]{2,0,1:T(8,128)} %get-tuple-element.31), kind=kOutput, calls=%fused_computation.56 | convolution fusion | flops 3221454848 | bytes 16777216 | tf_op jit(solution)/shard_map/cbm,db->dcm/dot_general | solution.py:53
  179.5 13.6 %fusion.27 = f32[128,64,256]{2,0,1:T(8,128)} fusion(f32[64,128,256]{2,0,1:T(8,128)S(1)} %copy-done.2), kind=kOutput, calls=%fused_computation.54 | convolution fusion | flops 3221471232 | bytes 16777216 | tf_op jit(solution)/shard_map/cbm,db->dcm/dot_general | solution.py:48
  193.0 14.3 %fusion.53 = f32[128,64,256]{2,0,1:T(8,128)S(1)} fusion(f32[128,64,256]{2,0,1:T(8,128)} %fusion.29, f32[64,128,256]{2,0,1:T(8,128)S(1)} %get-tuple-element.30), kind=kOutput, calls=%fused_computation.96 | convolution fusion | flops 3223568384 | bytes 25165824 | tf_op jit(solution)/shard_map/cbm,db->dcm/dot_general | solution.py:51
  215.6 17.3 %subtract_add_fusion.1 = f32[128,64,256]{2,0,1:T(8,128)} fusion(f32[128,64,256]{2,0,1:T(8,128)} %fusion.27, f32[128,64,256]{2,0,1:T(8,128)S(1)} %fusion.53, f32[64,128,256]{2,0,1:T(8,128)S(1)} %get-tuple-element.30), kind=kOutput, calls=%fused_computation.42 | convolution fusion | flops 3227746304 | bytes 33554432 | tf_op jit(solution)/shard_map/cbm,db->dcm/dot_general | solution.py:46
  247.6 40.7 %gather_fusion = f32[8192,512]{1,0:T(8,128)} fusion(f32[8192,512]{1,0:T(8,128)} %pad_maximum_fusion, s32[8192]{0:T(1024)S(1)} %broadcast_clamp_fusion), kind=kCustom, calls=%fused_computation | custom fusion | bytes 33587200 | tf_op jit(solution)/shard_map/jit(_take)/gather | solution.py:192
  288.3 11.5 %broadcast_select_fusion = f32[8192,512]{1,0:T(8,128)} fusion(f32[8192,512]{1,0:T(8,128)} %gather_fusion, pred[8192]{0:T(1024)(128)(4,1)S(1)} %get-tuple-element.20), kind=kLoop, calls=%fused_computation.41 | loop fusion | flops 4194304 | bytes 33562624 | tf_op jit(solution)/shard_map/jit(_take)/select_n | solution.py:192
  299.9 18.4 %multiply_add_fusion.2 = (f32[8192,256]{1,0:T(8,128)}, f32[8192,256]{1,0:T(8,128)}) fusion(f32[8192,512]{1,0:T(8,128)} %broadcast_select_fusion, f32[8192,512]{1,0:T(8,128)} %fusion.39), kind=kLoop, calls=%fused_computation.40 | loop fusion | flops 12582912 | bytes 50331648 | tf_op jit(solution)/shard_map/add | solution.py:195
  379.9 44.4 %reduce-scatter.8.cloned.1.call-done = f32[256,2,128]{2,0,1:T(8,128)} async-done(((f32[2048,2,128]{2,0,1:T(8,128)}), f32[256,2,128]{2,0,1:T(8,128)}) %reduce-scatter.8.cloned.1.call-update) | async-done | bytes 262160 | tf_op jit(solution)/shard_map/reduce_scatter | solution.py:212
  424.3 44.4 %reduce-scatter.10.cloned.1.call-done = f32[256,2,128]{2,0,1:T(8,128)} async-done(((f32[2048,2,128]{2,0,1:T(8,128)}), f32[256,2,128]{2,0,1:T(8,128)}) %reduce-scatter.10.cloned.1.call-update) | async-done | bytes 262160 | tf_op jit(solution)/shard_map/reduce_scatter | solution.py:212
  468.8 44.8 %reduce-scatter.12.cloned.1.call-done = f32[256,2,128]{2,0,1:T(8,128)} async-done(((f32[2048,2,128]{2,0,1:T(8,128)}), f32[256,2,128]{2,0,1:T(8,128)}) %reduce-scatter.12.cloned.1.call-update) | async-done | bytes 262160 | tf_op jit(solution)/shard_map/reduce_scatter | solution.py:212
  517.2 26.4 %reduce-scatter.14.cloned.1.call-done = f32[256,2,128]{2,0,1:T(8,128)} async-done(((f32[1024,2,128]{2,0,1:T(8,128)}), f32[256,2,128]{2,0,1:T(8,128)}) %reduce-scatter.14.cloned.1.call-update) | async-done | bytes 262160 | tf_op jit(solution)/shard_map/reduce_scatter | solution.py:214
  545.6 38.9 %all-reduce = (f32[]{:T(128)}, f32[]{:T(128)}) all-reduce(f32[]{:T(128)} %fusion.201, f32[]{:T(128)} %get-tuple-element.58), channel_id=1, replica_groups=mesh['vis'=8,'tile'=4] {'vis','tile'}, use_global_device_ids=true, to_apply=%region_6.7 | all-reduce | flops 2 | bytes 16 | tf_op jit(solution)/shard_map/psum | solution.py:220
  587.8 28.0 %all-gather.4.cloned.1.call-done = f32[1024,2,128]{2,0,1:T(8,128)} async-done(((f32[256,2,128]{2,0,1:T(8,128)}), f32[1024,2,128]{2,0,1:T(8,128)}) %all-gather.4.cloned.1.call-update) | async-done | bytes 1048592 | tf_op jit(solution)/shard_map/all_gather | solution.py:225
  640.0 18.9 %slice.188 = f32[1024,1027]{0,1:T(8,128)} slice(f32[1024,2054]{0,1:T(8,128)} %pad_maximum_fusion.2), slice={[0:1024:1], [0:2054:2]} | slice | bytes 8413184 | tf_op jit(solution)/shard_map/slice | solution.py:102
  658.9 19.0 %slice.190 = f32[1024,1027]{0,1:T(8,128)} slice(f32[1024,2054]{0,1:T(8,128)} %pad_maximum_fusion.2), slice={[0:1024:1], [1:2054:2]} | slice | bytes 8413184 | tf_op jit(solution)/shard_map/slice | solution.py:102
  677.9 13.4 %multiply_add_fusion.5 = f32[1024,1024]{0,1:T(8,128)S(1)} fusion(f32[1024,1027]{0,1:T(8,128)} %slice.190, f32[1024,1027]{0,1:T(8,128)} %slice.188), kind=kLoop, calls=%fused_computation.93 | loop fusion | flops 15728640 | bytes 37748736 | tf_op jit(solution)/shard_map/add | solution.py:108
  763.1 19.7 %multiply_subtract_fusion.1 = (f32[8192,256]{1,0:T(8,128)}, f32[8192,256]{1,0:T(8,128)}) fusion(f32[8192,256]{1,0:T(8,128)} %convolution_subtract_fusion, f32[8192,512]{1,0:T(8,128)} %fusion.39, f32[8192,256]{1,0:T(8,128)} %fusion.51, s32[256]{0:T(256)S(1)} %iota_add_fusion, f32[8192,2,128]{2,0,1:T(8,128)} %all-gather.6.cloned.1.call-done), kind=kOutput, calls=%fused_computation.38 | convolution fusion | flops 3236364288 | bytes 54526976 | tf_op jit(solution)/shard_map/dot_general | solution.py:230
  797.4 32.1 %fusion = f32[8,1024,512]{2,1,0:T(8,128)} fusion(pred[8,1024,1024]{2,1,0:T(32,128)(4,1)} %iota_compare_fusion, bf16[8,1024,512]{2,1,0:T(8,128)(2,1)} %get-tuple-element.35, bf16[8,1024,512]{2,1,0:T(8,128)(2,1)} %get-tuple-element.36, bf16[8,1024,512]{2,1,0:T(8,128)(2,1)S(1)} %get-tuple-element.34), kind=kOutput, calls=%fused_computation.1 | convolution fusion | flops 25895632896 | bytes 50331648 | tf_op jit(solution)/shard_map/gkb,gbc->gkc/dot_general | solution.py:152
  835.9 13.2 %fusion.19 = f32[64,128,256]{2,0,1:T(8,128)} fusion(f32[64,128,256]{2,1,0:T(8,128)S(1)} %bitcast.157), kind=kOutput, calls=%fused_computation.46 | convolution fusion | flops 1610670080 | bytes 16777216 | tf_op jit(solution)/shard_map/abm,ca->cbm/dot_general | solution.py:48
  849.0 13.4 %fusion.21 = f32[64,128,256]{2,0,1:T(8,128)} fusion(f32[64,128,256]{2,1,0:T(8,128)S(1)} %bitcast.158), kind=kOutput, calls=%fused_computation.48 | convolution fusion | flops 1610670080 | bytes 16777216 | tf_op jit(solution)/shard_map/abm,ca->cbm/dot_general | solution.py:53
  862.5 13.2 %fusion.25 = f32[64,128,256]{2,0,1:T(8,128)} fusion(f32[64,128,256]{2,1,0:T(8,128)S(1)} %bitcast.159), kind=kOutput, calls=%fused_computation.52 | convolution fusion | flops 1610670080 | bytes 16777216 | tf_op jit(solution)/shard_map/abm,ca->cbm/dot_general | solution.py:51
  875.6 21.8 %multiply_subtract_fusion = (f32[64,128,256]{2,0,1:T(8,128)}, f32[64,128,256]{2,0,1:T(8,128)}) fusion(f32[64,128,256]{2,0,1:T(8,128)} %fusion.19, f32[64,128]{0,1:T(8,128)S(1)} %copy-done.19, f32[64,128]{0,1:T(8,128)S(1)} %copy-done.16, f32[64,128,256]{2,0,1:T(8,128)} %fusion.25, f32[64,128,256]{2,0,1:T(8,128)} %fusion.21, f32[64,128,256]{2,1,0:T(8,128)S(1)} %bitcast.160), kind=kOutput, calls=%fused_computation.35 | convolution fusion | flops 1631641600 | bytes 50397184 | tf_op jit(solution)/shard_map/abm,ca->cbm/dot_general | solution.py:46
  897.4 16.0 %fusion.15 = f32[128,64,256]{2,0,1:T(8,128)S(1)} fusion(f32[64,128,256]{2,0,1:T(8,128)} %get-tuple-element.25), kind=kOutput, calls=%fused_computation.29 | convolution fusion | flops 3221454848 | bytes 16777216 | tf_op jit(solution)/shard_map/cbm,db->dcm/dot_general | solution.py:48
  913.5 11.8 %fusion.58 = f32[128,64,256]{2,0,1:T(8,128)S(1)} fusion(f32[128,64,256]{2,0,1:T(8,128)S(1)} %fusion.15, f32[64,128,256]{2,0,1:T(8,128)S(1)} %copy-done.5), kind=kOutput, calls=%fused_computation.97 | convolution fusion | flops 3223552000 | bytes 25165824 | tf_op jit(solution)/shard_map/cbm,db->dcm/dot_general | solution.py:46
  953.4 20.9 %fusion.50 = (f32[1024,1024]{0,1:T(8,128)}, f32[1024,1024]{0,1:T(8,128)}) fusion(f32[1024,1024]{0,1:T(8,128)} %mul.725, f32[1,1024,1024]{1,2,0:T(8,128)} %copy.162, f32[1024,1027]{0,1:T(8,128)} %slice.190, f32[1024,1027]{0,1:T(8,128)} %slice.188, f32[1,1024,1024]{1,2,0:T(8,128)} %copy.161), kind=kLoop, calls=%fused_computation.92 | loop fusion | flops 25165824 | bytes 54525952 | tf_op jit(solution)/shard_map/mul | solution.py:247
  1047.3 20.0 %add_bitcast_fusion.1 = (f32[1024,1024,1]{0,1,2:T(8,128)S(1)}, f32[1024,1024,1]{0,1,2:T(8,128)S(1)}) fusion(f32[1024,1024]{0,1:T(8,128)} %reshape.170, f32[1024,1024]{0,1:T(8,128)} %get-tuple-element.22, f32[1024,3]{0,1:T(4,128)S(1)} %get-tuple-element.55, f32[1024,3]{0,1:T(4,128)S(1)} %get-tuple-element.54), kind=kLoop, calls=%fused_computation.89 | loop fusion | flops 41943040 | bytes 16801792 | tf_op jit(solution)/shard_map/stack | solution.py:125
  1069.0 12.9 %copy.152 = f32[1024,1024,2]{0,2,1:T(2,128)} copy(f32[1024,1024,2]{0,1,2:T(8,128)S(1)} %pad_maximum_fusion.3) | data formatting | bytes 16777216 | tf_op jit(solution)/shard_map/stack | solution.py:125
  1110.5 13.6 %fusion.14 = f32[1024,2048]{0,1:T(8,128)} fusion(f32[1024,2048]{0,1:T(8,128)} %copy.153, f32[1024,2048]{0,1:T(8,128)} %reshape.171, f32[1024,8,256]{0,2,1:T(8,128)} %copy.146), kind=kLoop, calls=%fused_computation.28 | loop fusion | flops 8388608 | bytes 33554432 | tf_op jit(solution)/shard_map/max | solution.py:257
  (171 shorter events, 381.6 us)
Async XLA Ops:
  7.2 536.4 %copy-start = (f32[128,128]{1,0:T(8,128)S(1)}, f32[128,128]{1,0:T(8,128)}, u32[]{:S(2)}) copy-start(f32[128,128]{1,0:T(8,128)} %param.13) | copy-start | bytes 196612
  16.5 5.4 copy-start.22
  16.5 100.1 %all-to-all-start = ((f32[1024,8,256]{0,2,1:T(8,128)}), f32[1024,8,256]{0,2,1:T(8,128)}, u32[]{:S(2)}, u32[]{:S(2)}) async-start(f32[1024,8,256]{0,2,1:T(8,128)} %bitcast.152), calls=%async_computation | async-start | bytes 16777216 | tf_op jit(solution)/shard_map/all_to_all | solution.py:169
  21.8 358.1 %reduce-scatter.6.cloned.1.call-start = ((), (), s32[]{:S(2)}) async-start(), calls=%async_computation.7 | async-start | bytes 2359296 | tf_op jit(solution)/shard_map/reduce_scatter | solution.py:212
  93.1 50.3 %copy-start.15 = (f32[64,128]{0,1:T(8,128)}, f32[64,128]{0,1:T(8,128)S(1)}, u32[]{:S(2)}) copy-start(f32[64,128]{0,1:T(8,128)S(1)} %get-tuple-element.63) | copy-start | bytes 98308
  93.6 8.6 copy-start.17
  161.7 17.7 %copy-start.2 = (f32[64,128,256]{2,0,1:T(8,128)S(1)}, f32[64,128,256]{2,0,1:T(8,128)}, u32[]{:S(2)}) copy-start(f32[64,128,256]{2,0,1:T(8,128)} %get-tuple-element.31) | copy-start | bytes 25165828
  232.8 8.4 copy-start.6
  318.3 8.8 slice-start.2
  318.3 8.8 slice-start.3
  338.6 85.8 %reduce-scatter.8.cloned.1.call-start = ((), (), s32[]{:S(2)}) async-start(), calls=%async_computation.8 | async-start | bytes 2359296 | tf_op jit(solution)/shard_map/reduce_scatter | solution.py:212
  351.5 117.2 %reduce-scatter.10.cloned.1.call-start = ((), (), s32[]{:S(2)}) async-start(), calls=%async_computation.9 | async-start | bytes 2359296 | tf_op jit(solution)/shard_map/reduce_scatter | solution.py:212
  364.5 149.0 %reduce-scatter.12.cloned.1.call-start = ((), (), s32[]{:S(2)}) async-start(), calls=%async_computation.10 | async-start | bytes 2359296 | tf_op jit(solution)/shard_map/reduce_scatter | solution.py:212
  374.5 169.1 %copy-start.20 = (f32[256,2,128]{2,1,0:T(2,128)S(1)}, f32[256,2,128]{2,1,0:T(2,128)}, u32[]{:S(2)}) copy-start(f32[256,2,128]{2,1,0:T(2,128)} %param.12) | copy-start | bytes 786436
  374.5 169.1 %copy-start.21 = (f32[256,2,128]{2,1,0:T(2,128)S(1)}, f32[256,2,128]{2,1,0:T(2,128)}, u32[]{:S(2)}) copy-start(f32[256,2,128]{2,1,0:T(2,128)} %param.10) | copy-start | bytes 786436
  376.0 242.6 %copy-start.18 = (s32[8192]{0:T(1024)S(1)}, s32[8192]{0:T(1024)}, u32[]{:S(2)}) copy-start(s32[8192]{0:T(1024)} %copy-done.17) | copy-start | bytes 98308
  376.0 167.6 %reduce-scatter.14.cloned.1.call-start = ((), (), s32[]{:S(2)}) async-start(), calls=%async_computation.11 | async-start | bytes 1310720 | tf_op jit(solution)/shard_map/reduce_scatter | solution.py:214
  515.8 100.0 %all-gather.4.cloned.1.call-start = ((), (), s32[]{:S(2)}) async-start(), calls=%async_computation.12 | async-start | bytes 1310720 | tf_op jit(solution)/shard_map/all_gather | solution.py:225
  587.7 144.1 %all-gather.6.cloned.1.call-start = ((), (), s32[]{:S(2)}) async-start(), calls=%async_computation.13 | async-start | bytes 9437184 | tf_op jit(solution)/shard_map/all_gather | solution.py:226
  616.6 19.2 %collective-permute-start = (f32[1024,6]{0,1:T(8,128)S(1)}, f32[1024,6]{0,1:T(8,128)S(1)}, u32[]{:S(2)}, u32[]{:S(2)}) collective-permute-start(f32[1024,6]{0,1:T(8,128)S(1)} %slice.244), channel_id=1, source_target_pairs={{1,0},{2,1},{3,2},{0,3},{5,4},{6,5},{7,6},{4,7},{9,8},{10,9},{11,1... | collective-permute-start | bytes 73736 | tf_op jit(solution)/shard_map/ppermute | solution.py:27
  618.6 17.2 %slice-start = ((s8[8388608]{0:T(1024)(128)(4,1)}), s8[4194304]{0:T(1024)(128)(4,1)S(1)}, s32[]{:S(2)}) async-start(s8[8388608]{0:T(1024)(128)(4,1)} %bitcast.153), calls=%async_computation.14 | async-start | bytes 8388608
  627.3 8.5 slice-start.1
  693.3 13.5 %collective-permute-start.1 = (f32[1024,6]{0,1:T(8,128)S(1)}, f32[1024,6]{0,1:T(8,128)S(1)}, u32[]{:S(2)}, u32[]{:S(2)}) collective-permute-start(f32[1024,6]{0,1:T(8,128)S(1)} %slice.253), channel_id=1, source_target_pairs={{1,0},{2,1},{3,2},{0,3},{5,4},{6,5},{7,6},{4,7},{9,8},{10,9},{11,1... | collective-permute-start | bytes 73736 | tf_op jit(solution)/shard_map/ppermute | solution.py:27
  731.8 10.0 copy-start.3
  862.4 13.2 %copy-start.16 = (f32[64,128]{0,1:T(8,128)S(1)}, f32[64,128]{0,1:T(8,128)}, u32[]{:S(2)}) copy-start(f32[64,128]{0,1:T(8,128)} %copy-done.15) | copy-start | bytes 98308
  862.5 13.2 %copy-start.19 = (f32[64,128]{0,1:T(8,128)S(1)}, f32[64,128]{0,1:T(8,128)}, u32[]{:S(2)}) copy-start(f32[64,128]{0,1:T(8,128)} %fusion.171) | copy-start | bytes 98308
  897.4 16.1 %copy-start.5 = (f32[64,128,256]{2,0,1:T(8,128)S(1)}, f32[64,128,256]{2,0,1:T(8,128)}, u32[]{:S(2)}) copy-start(f32[64,128,256]{2,0,1:T(8,128)} %get-tuple-element.24) | copy-start | bytes 25165828
  933.7 160.1 %all-to-all-start.1 = ((f32[8,1024,256]{2,1,0:T(8,128)}), f32[8,1024,256]{2,1,0:T(8,128)}, u32[]{:S(2)}, u32[]{:S(2)}) async-start(f32[8,1024,256]{2,1,0:T(8,128)} %bitcast.164), calls=%async_computation.6 | async-start | bytes 16777216 | tf_op jit(solution)/shard_map/all_to_all | solution.py:240
  1005.3 10.0 collective-permute-start.2
  1029.4 17.8 %collective-permute-start.3 = (f32[2,1024,3]{1,2,0:T(4,128)S(1)}, f32[2,1024,3]{1,2,0:T(4,128)S(1)}, u32[]{:S(2)}, u32[]{:S(2)}) collective-permute-start(f32[2,1024,3]{1,2,0:T(4,128)S(1)} %pad_maximum_fusion.16), channel_id=1, source_target_pairs={{3,0},{0,1},{1,2},{2,3},{7,4},{4,5},{5,6},{6,7},{11,8},{8,9},{9,10... | collective-permute-start | bytes 73736 | tf_op jit(solution)/shard_map/ppermute | solution.py:27
  1081.9 11.0 copy-start.14
  1124.0 9.2 copy-start.1
  (8 other events, 27.9 us)
Sparse Core Ops, SparseCore 0:
  338.7 41.1 reduce-scatter.5
  383.2 41.0 reduce-scatter.7
  427.6 41.0 reduce-scatter.9
  472.5 41.0 reduce-scatter.11
  516.3 27.2 reduce-scatter.13
  587.9 27.9 all-gather.3
  617.7 53.6 all-gather.5
